TPU v7x, 512 devices: a whole 4x8x8 slice. The times are simulated.
512 devices in a mesh: group: 8 (over x, y_hi), sub: 64 (over y_lo, z, core).
Axes of the slice: x: 4, y: 8 (y_hi: 2, y_lo: 4; y = y_hi * 4 + y_lo), z: 8, core: 2. Of those that a mesh axis runs over, the one named last changes fastest.
Arguments:
- modes: bfloat16 [524288, 512], P(('group', 'sub')), may hold values from -6 to 6
- block_vals: bfloat16 [24576, 128, 128], P(('group', 'sub')), may hold values from -0.21875 to 0.21875
- block_cols: int32 [24576], P(('group', 'sub')), may hold values from 0 to 7, as said below
- level_maps: bfloat16 [2, 128, 128], replicated, may hold values from -0.5 to 0.5
- psi: bfloat16 [524288, 512], P(('group', 'sub')), may hold values from -0.09375 to 0.09375
- parent_vals: bfloat16 [4096, 128, 128], P(('group', 'sub')), may hold values from -0.09375 to 0.09375
- parent_rows: int32 [4096], P(('group', 'sub')), may hold values from 0 to 63
Outputs:
- parent_coupling: bfloat16 [8192, 1024], P('sub', 'group')
- projected: float32 [4096, 512], P(('group', 'sub'))
Inputs may be any that keep to these rules, and one draw needn't show every extreme that they name: `block_cols`: within one interface row block of one device the 6 vertex blocks are distinct.
All inputs are finite; a program needn't handle non-finite values.
Results may differ from a plain program's by a relative error of at most 0.0078.
Values may be sent and summed in bfloat16 or wider, within the bound.
No kernel may reach another device: no remote copies, remote signals or barrier semaphores. Data moves between devices by JAX's collectives and lax.ppermute only.
A program may use at most 64 MiB of HBM per device.

v0:
```python
import jax
import jax.numpy as jnp
from jax import lax
from jax.sharding import PartitionSpec as P

IFB = 8
BPR = 6


def from_partner(value, axis, distance):
    mask = 2**distance
    pairs = [(source, source ^ mask) for source in range(lax.axis_size(axis))]
    return lax.ppermute(value, axis, pairs)


def on_device(modes, block_vals, block_cols, level_maps, psi, parent_vals, parent_rows):
    block_size = block_vals.shape[1]
    width = modes.shape[1]
    vertex_blocks = modes.shape[0] // block_size
    row_blocks = IFB
    levels = min(2, lax.axis_size("group").bit_length() - 1)
    group_index = lax.axis_index("group")
    onehot = (
        block_cols.reshape(row_blocks, BPR)[:, :, None] == jnp.arange(vertex_blocks)[None, None, :]
    ).astype(jnp.float32)
    blocks = block_vals.astype(jnp.float32).reshape(row_blocks, BPR, block_size, block_size)
    dense = (
        jnp.einsum("rbc,rbij->ricj", onehot, blocks)
        .reshape(row_blocks * block_size, vertex_blocks * block_size)
        .astype(jnp.bfloat16)
    )
    panel = jnp.dot(dense, modes, preferred_element_type=jnp.float32).astype(jnp.bfloat16)
    for level in range(levels):
        sibling = from_partner(panel, "group", level)
        total = (panel.astype(jnp.float32) + sibling.astype(jnp.float32)).astype(jnp.bfloat16)
        mapped = jnp.einsum(
            "ab,rbm->ram",
            level_maps[level],
            total.reshape(row_blocks, block_size, width),
            preferred_element_type=jnp.float32,
        )
        panel = mapped.reshape(row_blocks * block_size, width).astype(jnp.bfloat16)
    head = panel[:block_size]
    piece = lax.all_gather(head, "sub", axis=0, tiled=True)
    owners_here = piece.shape[0] // block_size
    owners = jnp.arange(owners_here)
    select = (parent_rows[:, None] == owners[None, :]).astype(jnp.bfloat16)
    picked = jnp.einsum(
        "kj,jbm->kbm",
        select,
        piece.reshape(owners_here, block_size, width),
        preferred_element_type=jnp.float32,
    ).astype(jnp.bfloat16)
    partial_sum = jnp.einsum("kab,kbm->am", parent_vals, picked, preferred_element_type=jnp.float32)
    for level in reversed(range(levels)):
        half = partial_sum.shape[1] // 2
        upper = group_index >> level & 1
        keeper = lax.dynamic_slice_in_dim(partial_sum, upper * half, half, 1)
        sender = lax.dynamic_slice_in_dim(partial_sum, (1 - upper) * half, half, 1)
        partial_sum = keeper + from_partner(sender, "group", level)
    parent_out = partial_sum.astype(jnp.bfloat16)
    projected = lax.psum_scatter(
        lax.dot_general(psi, panel, (((0,), (0,)), ((), ())), preferred_element_type=jnp.float32),
        "sub",
        scatter_dimension=0,
        tiled=True,
    )
    return (parent_out, projected)


def solution(mesh):
    return jax.shard_map(
        on_device,
        mesh=mesh,
        in_specs=(
            P(("group", "sub"), None),
            P(("group", "sub"), None, None),
            P(("group", "sub")),
            P(),
            P(("group", "sub"), None),
            P(("group", "sub"), None, None),
            P(("group", "sub")),
        ),
        out_specs=(P("sub", "group"), P(("group", "sub"), None)),
        check_vma=False,
    )
```

profile of v0, /device:TPU:1, one launch (start us, length us, event | category | flops | bytes accessed | tf_op | source)
XLA Modules:
  0.0 511.0 jit_solution(13691395936488366939)
XLA Ops:
  7.2 0.0 copy-start
  7.2 0.0 all-gather.3.cloned.1.call-start
  7.2 0.8 eq.31
  8.1 0.5 copy-done
  8.6 1.0 fusion.7
  9.6 0.2 copy-done.4
  9.8 1.2 fusion.10
  11.1 0.0 copy-start.2
  11.1 8.4 %collective-permute-start = (bf16[1024,512]{1,0:T(8,128)(2,1)S(1)}, bf16[1024,512]{1,0:T(8,128)(2,1)S(1)}, u32[]{:S(2)}, u32[]{:S(2)}) collective-permute-start(bf16[1024,512]{1,0:T(8,128)(2,1)S(1)} %fusion.10), channel_id=1, source_target_pairs={{0,64},{64,0},{128,192},{192,128},{256,320},{320,256},{384,448},{4... | collective-permute-start | bytes 3145736 | tf_op jit(solution)/shard_map/ppermute | solution.py:13
  19.5 33.9 %collective-permute-done = bf16[1024,512]{1,0:T(8,128)(2,1)S(1)} collective-permute-done((bf16[1024,512]{1,0:T(8,128)(2,1)S(1)}, bf16[1024,512]{1,0:T(8,128)(2,1)S(1)}, u32[]{:S(2)}, u32[]{:S(2)}) %collective-permute-start) | collective-permute-done | bytes 1048608 | tf_op jit(solution)/shard_map/ppermute | solution.py:13
  53.4 0.3 add_convert_fusion.1
  53.7 0.4 convolution_convert_fusion.1
  54.2 3.6 collective-permute-start.1
  57.8 12.2 %collective-permute-done.1 = bf16[1024,512]{1,0:T(8,128)(2,1)S(1)} collective-permute-done((bf16[1024,512]{1,0:T(8,128)(2,1)S(1)}, bf16[1024,512]{1,0:T(8,128)(2,1)S(1)}, u32[]{:S(2)}, u32[]{:S(2)}) %collective-permute-start.1) | collective-permute-done | bytes 1048608 | tf_op jit(solution)/shard_map/ppermute | solution.py:13
  70.0 0.4 add_convert_fusion
  70.4 0.4 convolution_convert_fusion
  70.8 0.7 slice.16
  71.4 0.0 all-gather.3.cloned.1.call-update
  71.5 0.2 reduce-scatter.4.cloned.1.call-start
  71.7 2.9 convolution_bitcast_fusion
  74.6 2.6 copy.18
  77.3 0.0 reduce-scatter.4.cloned.1.call-update
  77.3 143.5 %all-gather.3.cloned.1.call-done = bf16[1,8192,512]{2,1,0:T(8,128)(2,1)} async-done(((bf16[1,128,512]{2,1,0:T(8,128)(2,1)}), bf16[1,8192,512]{2,1,0:T(8,128)(2,1)}) %all-gather.3.cloned.1.call-update) | async-done | bytes 8388624 | tf_op jit(solution)/shard_map/all_gather | solution.py:44
  220.8 12.2 %fusion = bf16[8,128,512]{2,0,1:T(8,128)(2,1)S(1)} fusion(bf16[64,128,512]{2,1,0:T(8,128)(2,1)} %bitcast.52, s32[8]{0:T(128)S(1)} %copy-done.3), kind=kOutput, calls=%fused_computation | convolution fusion | flops 67109376 | bytes 9437216 | tf_op jit(solution)/shard_map/kj,jbm->kbm/dot_general | solution.py:48
  233.0 1.7 copy.17
  234.7 1.7 convolution_bitcast_fusion.1
  236.4 3.1 collective-permute-start.2
  239.5 3.7 collective-permute-done.2
  243.2 7.8 %collective-permute-start.3 = (f32[128,128]{0,1:T(8,128)S(1)}, f32[128,128]{0,1:T(8,128)S(1)}, u32[]{:S(2)}, u32[]{:S(2)}) collective-permute-start(f32[128,128]{0,1:T(8,128)S(1)} %constant_dynamic-slice_fusion), channel_id=1, source_target_pairs={{0,64},{64,0},{128,192},{192,128},{256,320},{320,256},{384,448},{4... | collective-permute-start | bytes 196616 | tf_op jit(solution)/shard_map/ppermute | solution.py:13
  251.0 1.7 collective-permute-done.3
  252.8 0.7 copy.13
  253.5 250.7 %reduce-scatter.4.cloned.1.call-done = f32[8,512]{1,0:T(8,128)} async-done(((f32[512,512]{1,0:T(8,128)}), f32[8,512]{1,0:T(8,128)}) %reduce-scatter.4.cloned.1.call-update) | async-done | bytes 16400
  (10 shorter events, 0.1 us)
Async XLA Ops:
  7.2 1.4 copy-start
  7.2 213.6 %all-gather.3.cloned.1.call-start = ((), (), s32[]{:S(2)}) async-start(), calls=%async_computation.1 | async-start | bytes 8519680 | tf_op jit(solution)/shard_map/all_gather | solution.py:44
  8.6 1.2 copy-start.4
  11.1 42.7 %copy-start.2 = (bf16[2,128,128]{2,1,0:T(8,128)(2,1)S(1)}, bf16[2,128,128]{2,1,0:T(8,128)(2,1)}, u32[]{:S(2)}) copy-start(bf16[2,128,128]{2,1,0:T(8,128)(2,1)} %param.10) | copy-start | bytes 196612
  11.1 42.3 %collective-permute-start = (bf16[1024,512]{1,0:T(8,128)(2,1)S(1)}, bf16[1024,512]{1,0:T(8,128)(2,1)S(1)}, u32[]{:S(2)}, u32[]{:S(2)}) collective-permute-start(bf16[1024,512]{1,0:T(8,128)(2,1)S(1)} %fusion.10), channel_id=1, source_target_pairs={{0,64},{64,0},{128,192},{192,128},{256,320},{320,256},{384,448},{4... | collective-permute-start | bytes 3145736 | tf_op jit(solution)/shard_map/ppermute | solution.py:13
  54.2 15.8 %collective-permute-start.1 = (bf16[1024,512]{1,0:T(8,128)(2,1)S(1)}, bf16[1024,512]{1,0:T(8,128)(2,1)S(1)}, u32[]{:S(2)}, u32[]{:S(2)}) collective-permute-start(bf16[1024,512]{1,0:T(8,128)(2,1)S(1)} %bitcast.53), channel_id=1, source_target_pairs={{0,128},{64,192},{128,0},{192,64},{256,384},{320,448},{384,256},{4... | collective-permute-start | bytes 3145736 | tf_op jit(solution)/shard_map/ppermute | solution.py:13
  71.5 432.7 %reduce-scatter.4.cloned.1.call-start = ((), (), s32[]{:S(2)}) async-start(), calls=%async_computation.2 | async-start | bytes 1064960
  74.6 146.2 %copy-start.3 = (s32[8]{0:T(128)S(1)}, s32[8]{0:T(128)}, u32[]{:S(2)}) copy-start(s32[8]{0:T(128)} %param.13) | copy-start | bytes 100
  233.0 1.7 copy-start.1
  236.4 6.8 %collective-permute-start.2 = (f32[128,256]{0,1:T(8,128)S(1)}, f32[128,256]{0,1:T(8,128)S(1)}, u32[]{:S(2)}, u32[]{:S(2)}) collective-permute-start(f32[128,256]{0,1:T(8,128)S(1)} %dynamic-slice_bitcast_fusion), channel_id=1, source_target_pairs={{0,128},{64,192},{128,0},{192,64},{256,384},{320,448},{384,256},{4... | collective-permute-start | bytes 393224 | tf_op jit(solution)/shard_map/ppermute | solution.py:13
  243.2 9.5 %collective-permute-start.3 = (f32[128,128]{0,1:T(8,128)S(1)}, f32[128,128]{0,1:T(8,128)S(1)}, u32[]{:S(2)}, u32[]{:S(2)}) collective-permute-start(f32[128,128]{0,1:T(8,128)S(1)} %constant_dynamic-slice_fusion), channel_id=1, source_target_pairs={{0,64},{64,0},{128,192},{192,128},{256,320},{320,256},{384,448},{4... | collective-permute-start | bytes 196616 | tf_op jit(solution)/shard_map/ppermute | solution.py:13
Sparse Core Ops, SparseCore 0:
  71.6 149.1 all-gather.2
  224.1 279.9 reduce-scatter.3
where the time goes:
time: 515 us; the launch traced here: 511 us
  waiting for transfers between devices  446 us (87%)
  starting transfers between devices  23.2 us (5%)
  matrix products  19.9 us (4%)
  between operations  14.2 us (3%)
  local copies, waits for them, and re-layouts  7.35 us (1%)
    unnamed x3, waiting for transfers between devices  251 us
    all_gather x1, waiting for transfers between devices, on_device(): piece = lax.all_gather(head, 'sub', axis=0, tiled=True)  143 us
    ppermute x4, waiting for transfers between devices, from_partner(): return lax.ppermute(value, axis, pairs)  51.5 us
    ppermute x4, starting transfers between devices, from_partner(): return lax.ppermute(value, axis, pairs)  22.9 us
    dot_general x1, matrix products, on_device(): jnp.einsum('kj,jbm->kbm', select, piece.reshape(owners_here, block_size,...  12.2 us
  transfers between devices with their start and end apart: 6, of which 6 were waited for; matrix products, arithmetic and copies ran while one was open for 4% of the time, Pallas kernels for 0%

commit v1 on v0

v1 whole, which is shorter than its diff:
```python
import jax
import jax.numpy as jnp
from jax import lax
from jax.sharding import PartitionSpec as P

IFB = 8
BPR = 6


def from_partner(value, axis, mask):
    pairs = [(source, source ^ mask) for source in range(lax.axis_size(axis))]
    return lax.ppermute(value, axis, pairs)


def on_device(modes, block_vals, block_cols, level_maps, psi, parent_vals, parent_rows):
    block_size = block_vals.shape[1]
    width = modes.shape[1]
    vertex_blocks = modes.shape[0] // block_size
    row_blocks = IFB
    levels = min(2, lax.axis_size("group").bit_length() - 1)
    merged = 2**levels
    n_sub = lax.axis_size("sub")
    group_index = lax.axis_index("group")

    vals_all = [parent_vals]
    rows_all = [parent_rows]
    for mask in range(1, merged):
        vals_all.append(from_partner(parent_vals, "group", mask))
        rows_all.append(from_partner(parent_rows, "group", mask))
    vals_all = jnp.concatenate(vals_all, axis=0)
    rows_all = jnp.concatenate(rows_all, axis=0)

    onehot = (
        block_cols.reshape(row_blocks, BPR)[:, :, None] == jnp.arange(vertex_blocks)[None, None, :]
    ).astype(jnp.float32)
    blocks = block_vals.astype(jnp.float32).reshape(row_blocks, BPR, block_size, block_size)
    dense = (
        jnp.einsum("rbc,rbij->ricj", onehot, blocks)
        .reshape(row_blocks * block_size, vertex_blocks * block_size)
        .astype(jnp.bfloat16)
    )
    panel = jnp.dot(dense, modes, preferred_element_type=jnp.float32).astype(jnp.bfloat16)
    for level in range(levels):
        sibling = from_partner(panel, "group", 2**level)
        total = (panel.astype(jnp.float32) + sibling.astype(jnp.float32)).astype(jnp.bfloat16)
        mapped = jnp.einsum(
            "ab,rbm->ram",
            level_maps[level],
            total.reshape(row_blocks, block_size, width),
            preferred_element_type=jnp.float32,
        )
        panel = mapped.reshape(row_blocks * block_size, width).astype(jnp.bfloat16)

    quarter = width // merged
    column = (group_index % merged) * quarter
    head = lax.dynamic_slice_in_dim(panel[:block_size], column, quarter, 1)
    piece = lax.all_gather(head, "sub", axis=0, tiled=True).reshape(n_sub, block_size, quarter)
    picked = jnp.take(piece, rows_all, axis=0)
    parent_out = jnp.einsum(
        "kab,kbm->am", vals_all, picked, preferred_element_type=jnp.float32
    ).astype(jnp.bfloat16)

    partial = lax.dot_general(psi, panel, (((0,), (0,)), ((), ())), preferred_element_type=jnp.float32)
    spread = lax.all_to_all(partial.reshape(n_sub, width // n_sub, width), "sub", 0, 0, tiled=True)
    projected = spread.sum(axis=0)
    return (parent_out, projected)


def solution(mesh):
    return jax.shard_map(
        on_device,
        mesh=mesh,
        in_specs=(
            P(("group", "sub"), None),
            P(("group", "sub"), None, None),
            P(("group", "sub")),
            P(),
            P(("group", "sub"), None),
            P(("group", "sub"), None, None),
            P(("group", "sub")),
        ),
        out_specs=(P("sub", "group"), P(("group", "sub"), None)),
        check_vma=False,
    )
```

time: 515 us -> 254 us (0.49)
  waiting for transfers between devices: 446 us -> 149 us
  starting transfers between devices: 23.2 us -> 74.7 us
  matrix products: 19.9 us -> 8.17 us
    unnamed x3 -> x1, waiting for transfers between devices: 251 us -> 0.02 us
    all_gather x1, waiting for transfers between devices: 143 us -> 76.8 us  [on_device(): lax.all_gather(head, 'sub', axis=0, tiled=True)]
    all_to_all x0 -> x1, starting transfers between devices: none -> 36.6 us  [on_device(): lax.all_to_all(partial.reshape(n_sub, width // n_sub, width), 'sub', 0, 0...]
    all_to_all x0 -> x1, waiting for transfers between devices: none -> 25.7 us  [on_device(): lax.all_to_all(partial.reshape(n_sub, width // n_sub, width), 'sub', 0, 0...]
    ppermute x4 -> x8, starting transfers between devices: 22.9 us -> 38.1 us  [from_partner(): return lax.ppermute(value, axis, pairs)]
    dot_general x2 -> x1, matrix products: 13.9 us -> 2.1 us  [on_device(): jnp.einsum('kab,kbm->am', vals_all, picked, preferred_element_type=jnp.fl...]
    ppermute x4 -> x8, waiting for transfers between devices: 51.5 us -> 46.7 us  [from_partner(): return lax.ppermute(value, axis, pairs)]
  transfers between devices with their start and end apart: 6 -> 10, of which waited for: 6 -> 5; matrix products, arithmetic and copies ran while one was open for 4% -> 2% of each run, Pallas kernels for 0% -> 0%
where the time goes in v1:
time: 254 us
  waiting for transfers between devices  149 us (59%)
  starting transfers between devices  74.7 us (29%)
  between operations  14.3 us (6%)
  matrix products  8.17 us (3%)
  local copies, waits for them, and re-layouts  4.54 us (2%)
  other arithmetic  2.7 us (1%)
    all_gather x1, waiting for transfers between devices, on_device(): lax.all_gather(head, 'sub', axis=0, tiled=True)  76.8 us
    ppermute x8, waiting for transfers between devices, from_partner(): return lax.ppermute(value, axis, pairs)  46.7 us
    ppermute x8, starting transfers between devices, from_partner(): return lax.ppermute(value, axis, pairs)  38.1 us
    all_to_all x1, starting transfers between devices, on_device(): lax.all_to_all(partial.reshape(n_sub, width // n_sub, width), 'sub', 0, 0...  36.6 us
    all_to_all x1, waiting for transfers between devices, on_device(): lax.all_to_all(partial.reshape(n_sub, width // n_sub, width), 'sub', 0, 0...  25.7 us
  transfers between devices with their start and end apart: 10, of which 5 were waited for; matrix products, arithmetic and copies ran while one was open for 2% of the time, Pallas kernels for 0%

profile of v1, /device:TPU:1, one launch (start us, length us, event | category | flops | bytes accessed | tf_op | source)
XLA Modules:
  0.0 253.6 jit_solution(811477235119022073)
XLA Ops:
  7.2 0.0 all-gather.3.cloned.1.call-start
  7.2 0.8 eq.17
  8.1 0.5 copy-done
  8.6 1.0 fusion.5
  9.6 0.2 copy-done.3
  9.8 1.2 fusion.8
  11.1 8.4 %collective-permute-start.6 = (bf16[1024,512]{1,0:T(8,128)(2,1)S(1)}, bf16[1024,512]{1,0:T(8,128)(2,1)S(1)}, u32[]{:S(2)}, u32[]{:S(2)}) collective-permute-start(bf16[1024,512]{1,0:T(8,128)(2,1)S(1)} %fusion.8), channel_id=1, source_target_pairs={{0,64},{64,0},{128,192},{192,128},{256,320},{320,256},{384,448},{4... | collective-permute-start | bytes 3145736 | tf_op jit(solution)/shard_map/ppermute | solution.py:12
  19.5 33.9 %collective-permute-done.6 = bf16[1024,512]{1,0:T(8,128)(2,1)S(1)} collective-permute-done((bf16[1024,512]{1,0:T(8,128)(2,1)S(1)}, bf16[1024,512]{1,0:T(8,128)(2,1)S(1)}, u32[]{:S(2)}, u32[]{:S(2)}) %collective-permute-start.6) | collective-permute-done | bytes 1048608 | tf_op jit(solution)/shard_map/ppermute | solution.py:12
  53.4 0.3 add_convert_fusion.1
  53.7 0.4 convolution_convert_fusion.1
  54.2 3.7 %collective-permute-start.7 = (bf16[1024,512]{1,0:T(8,128)(2,1)S(1)}, bf16[1024,512]{1,0:T(8,128)(2,1)}, u32[]{:S(2)}, u32[]{:S(2)}) collective-permute-start(bf16[1024,512]{1,0:T(8,128)(2,1)S(1)} %bitcast.52), channel_id=1, source_target_pairs={{0,128},{64,192},{128,0},{192,64},{256,384},{320,448},{384,256},{4... | collective-permute-start | bytes 3145736 | tf_op jit(solution)/shard_map/ppermute | solution.py:12
  57.9 12.3 %collective-permute-done.7 = bf16[1024,512]{1,0:T(8,128)(2,1)} collective-permute-done((bf16[1024,512]{1,0:T(8,128)(2,1)S(1)}, bf16[1024,512]{1,0:T(8,128)(2,1)}, u32[]{:S(2)}, u32[]{:S(2)}) %collective-permute-start.7) | collective-permute-done | bytes 1048608 | tf_op jit(solution)/shard_map/ppermute | solution.py:12
  70.1 1.5 add_convert_fusion
  71.6 0.4 convolution_convert_fusion
  72.1 0.6 constant_dynamic-slice_fusion
  72.7 0.0 all-gather.3.cloned.1.call-update
  72.7 3.0 %convolution_bitcast_fusion = f32[64,8,512]{2,1,0:T(8,128)} fusion(bf16[1024,512]{1,0:T(8,128)(2,1)S(1)} %bitcast.57, bf16[1024,512]{1,0:T(8,128)(2,1)} %param.11), kind=kOutput, calls=%fused_computation.12 | convolution fusion | flops 536870912 | bytes 3145728 | tf_op jit(solution)/shard_map/dot_general | solution.py:63
  75.7 36.6 %all-to-all-start = ((f32[64,8,512]{2,1,0:T(8,128)}), f32[64,8,512]{2,1,0:T(8,128)S(1)}, u32[]{:S(2)}, u32[]{:S(2)}) async-start(f32[64,8,512]{2,1,0:T(8,128)} %convolution_bitcast_fusion), calls=%async_computation | async-start | bytes 2097152 | tf_op jit(solution)/shard_map/all_to_all | solution.py:64
  112.3 4.8 %collective-permute-start.3 = (s32[8]{0:T(128)S(1)}, s32[8]{0:T(128)S(1)}, u32[]{:S(2)}, u32[]{:S(2)}) collective-permute-start(s32[8]{0:T(128)S(1)} %copy-done.2), channel_id=1, source_target_pairs={{0,64},{64,0},{128,192},{192,128},{256,320},{320,256},{384,448},{4... | collective-permute-start | bytes 104 | tf_op jit(solution)/shard_map/ppermute | solution.py:12
  117.2 3.1 %collective-permute-start.4 = (s32[8]{0:T(128)S(1)}, s32[8]{0:T(128)S(1)}, u32[]{:S(2)}, u32[]{:S(2)}) collective-permute-start(s32[8]{0:T(128)S(1)} %copy-done.2), channel_id=1, source_target_pairs={{0,128},{64,192},{128,0},{192,64},{256,384},{320,448},{384,256},{4... | collective-permute-start | bytes 104 | tf_op jit(solution)/shard_map/ppermute | solution.py:12
  120.3 4.3 %collective-permute-start.5 = (s32[8]{0:T(128)S(1)}, s32[8]{0:T(128)S(1)}, u32[]{:S(2)}, u32[]{:S(2)}) collective-permute-start(s32[8]{0:T(128)S(1)} %copy-done.2), channel_id=1, source_target_pairs={{0,192},{64,128},{128,64},{192,0},{256,448},{320,384},{384,320},{4... | collective-permute-start | bytes 104 | tf_op jit(solution)/shard_map/ppermute | solution.py:12
  124.6 4.8 %collective-permute-start = (bf16[8,128,128]{2,1,0:T(8,128)(2,1)S(1)}, bf16[8,128,128]{2,1,0:T(8,128)(2,1)S(1)}, u32[]{:S(2)}, u32[]{:S(2)}) collective-permute-start(bf16[8,128,128]{2,1,0:T(8,128)(2,1)S(1)} %copy-done.4), channel_id=1, source_target_pairs={{0,64},{64,0},{128,192},{192,128},{256,320},{320,256},{384,448},{4... | collective-permute-start | bytes 786440 | tf_op jit(solution)/shard_map/ppermute | solution.py:12
  129.5 3.1 %collective-permute-start.1 = (bf16[8,128,128]{2,1,0:T(8,128)(2,1)S(1)}, bf16[8,128,128]{2,1,0:T(8,128)(2,1)S(1)}, u32[]{:S(2)}, u32[]{:S(2)}) collective-permute-start(bf16[8,128,128]{2,1,0:T(8,128)(2,1)S(1)} %copy-done.4), channel_id=1, source_target_pairs={{0,128},{64,192},{128,0},{192,64},{256,384},{320,448},{384,256},{4... | collective-permute-start | bytes 786440 | tf_op jit(solution)/shard_map/ppermute | solution.py:12
  132.6 0.5 collective-permute-done.3
  133.1 5.8 %collective-permute-start.2 = (bf16[8,128,128]{2,1,0:T(8,128)(2,1)S(1)}, bf16[8,128,128]{2,1,0:T(8,128)(2,1)}, u32[]{:S(2)}, u32[]{:S(2)}) collective-permute-start(bf16[8,128,128]{2,1,0:T(8,128)(2,1)S(1)} %copy-done.4), channel_id=1, source_target_pairs={{0,192},{64,128},{128,64},{192,0},{256,448},{320,384},{384,320},{4... | collective-permute-start | bytes 786440 | tf_op jit(solution)/shard_map/ppermute | solution.py:12
  138.9 0.1 fusion.29
  138.9 0.1 compare_and_fusion
  139.0 25.7 %all-to-all-done = f32[64,8,512]{2,1,0:T(8,128)S(1)} async-done(((f32[64,8,512]{2,1,0:T(8,128)}), f32[64,8,512]{2,1,0:T(8,128)S(1)}, u32[]{:S(2)}, u32[]{:S(2)}) %all-to-all-start) | async-done | bytes 1048608 | tf_op jit(solution)/shard_map/all_to_all | solution.py:64
  164.7 0.7 reduce_sum.9
  165.4 76.8 %all-gather.3.cloned.1.call-done = bf16[1,8192,128]{2,1,0:T(8,128)(2,1)} async-done(((bf16[1,128,128]{2,1,0:T(8,128)(2,1)}), bf16[1,8192,128]{2,1,0:T(8,128)(2,1)}) %all-gather.3.cloned.1.call-update) | async-done | bytes 2097168 | tf_op jit(solution)/shard_map/all_gather | solution.py:57
  242.3 2.3 gather_fusion
  244.7 2.1 fusion.11
  (15 shorter events, 0.1 us)
Async XLA Ops:
  7.2 1.4 copy-start
  7.2 235.1 %all-gather.3.cloned.1.call-start = ((), (), s32[]{:S(2)}) async-start(), calls=%async_computation.1 | async-start | bytes 2129920 | tf_op jit(solution)/shard_map/all_gather | solution.py:57
  8.6 1.2 copy-start.3
  11.1 42.7 %copy-start.1 = (bf16[2,128,128]{2,1,0:T(8,128)(2,1)S(1)}, bf16[2,128,128]{2,1,0:T(8,128)(2,1)}, u32[]{:S(2)}) copy-start(bf16[2,128,128]{2,1,0:T(8,128)(2,1)} %param.10) | copy-start | bytes 196612
  11.1 42.3 %collective-permute-start.6 = (bf16[1024,512]{1,0:T(8,128)(2,1)S(1)}, bf16[1024,512]{1,0:T(8,128)(2,1)S(1)}, u32[]{:S(2)}, u32[]{:S(2)}) collective-permute-start(bf16[1024,512]{1,0:T(8,128)(2,1)S(1)} %fusion.8), channel_id=1, source_target_pairs={{0,64},{64,0},{128,192},{192,128},{256,320},{320,256},{384,448},{4... | collective-permute-start | bytes 3145736 | tf_op jit(solution)/shard_map/ppermute | solution.py:12
  54.2 16.0 %collective-permute-start.7 = (bf16[1024,512]{1,0:T(8,128)(2,1)S(1)}, bf16[1024,512]{1,0:T(8,128)(2,1)}, u32[]{:S(2)}, u32[]{:S(2)}) collective-permute-start(bf16[1024,512]{1,0:T(8,128)(2,1)S(1)} %bitcast.52), channel_id=1, source_target_pairs={{0,128},{64,192},{128,0},{192,64},{256,384},{320,448},{384,256},{4... | collective-permute-start | bytes 3145736 | tf_op jit(solution)/shard_map/ppermute | solution.py:12
  75.7 36.6 %copy-start.2 = (s32[8]{0:T(128)S(1)}, s32[8]{0:T(128)}, u32[]{:S(2)}) copy-start(s32[8]{0:T(128)} %param.13) | copy-start | bytes 100
  75.7 48.9 %copy-start.4 = (bf16[8,128,128]{2,1,0:T(8,128)(2,1)S(1)}, bf16[8,128,128]{2,1,0:T(8,128)(2,1)}, u32[]{:S(2)}) copy-start(bf16[8,128,128]{2,1,0:T(8,128)(2,1)} %param.12) | copy-start | bytes 786436
  75.7 89.0 %all-to-all-start = ((f32[64,8,512]{2,1,0:T(8,128)}), f32[64,8,512]{2,1,0:T(8,128)S(1)}, u32[]{:S(2)}, u32[]{:S(2)}) async-start(f32[64,8,512]{2,1,0:T(8,128)} %convolution_bitcast_fusion), calls=%async_computation | async-start | bytes 2097152 | tf_op jit(solution)/shard_map/all_to_all | solution.py:64
  112.3 20.8 %collective-permute-start.3 = (s32[8]{0:T(128)S(1)}, s32[8]{0:T(128)S(1)}, u32[]{:S(2)}, u32[]{:S(2)}) collective-permute-start(s32[8]{0:T(128)S(1)} %copy-done.2), channel_id=1, source_target_pairs={{0,64},{64,0},{128,192},{192,128},{256,320},{320,256},{384,448},{4... | collective-permute-start | bytes 104 | tf_op jit(solution)/shard_map/ppermute | solution.py:12
  117.2 21.7 %collective-permute-start.4 = (s32[8]{0:T(128)S(1)}, s32[8]{0:T(128)S(1)}, u32[]{:S(2)}, u32[]{:S(2)}) collective-permute-start(s32[8]{0:T(128)S(1)} %copy-done.2), channel_id=1, source_target_pairs={{0,128},{64,192},{128,0},{192,64},{256,384},{320,448},{384,256},{4... | collective-permute-start | bytes 104 | tf_op jit(solution)/shard_map/ppermute | solution.py:12
  120.3 18.6 %collective-permute-start.5 = (s32[8]{0:T(128)S(1)}, s32[8]{0:T(128)S(1)}, u32[]{:S(2)}, u32[]{:S(2)}) collective-permute-start(s32[8]{0:T(128)S(1)} %copy-done.2), channel_id=1, source_target_pairs={{0,192},{64,128},{128,64},{192,0},{256,448},{320,384},{384,320},{4... | collective-permute-start | bytes 104 | tf_op jit(solution)/shard_map/ppermute | solution.py:12
  124.6 120.0 %collective-permute-start = (bf16[8,128,128]{2,1,0:T(8,128)(2,1)S(1)}, bf16[8,128,128]{2,1,0:T(8,128)(2,1)S(1)}, u32[]{:S(2)}, u32[]{:S(2)}) collective-permute-start(bf16[8,128,128]{2,1,0:T(8,128)(2,1)S(1)} %copy-done.4), channel_id=1, source_target_pairs={{0,64},{64,0},{128,192},{192,128},{256,320},{320,256},{384,448},{4... | collective-permute-start | bytes 786440 | tf_op jit(solution)/shard_map/ppermute | solution.py:12
  129.5 115.2 %collective-permute-start.1 = (bf16[8,128,128]{2,1,0:T(8,128)(2,1)S(1)}, bf16[8,128,128]{2,1,0:T(8,128)(2,1)S(1)}, u32[]{:S(2)}, u32[]{:S(2)}) collective-permute-start(bf16[8,128,128]{2,1,0:T(8,128)(2,1)S(1)} %copy-done.4), channel_id=1, source_target_pairs={{0,128},{64,192},{128,0},{192,64},{256,384},{320,448},{384,256},{4... | collective-permute-start | bytes 786440 | tf_op jit(solution)/shard_map/ppermute | solution.py:12
  133.1 111.6 %collective-permute-start.2 = (bf16[8,128,128]{2,1,0:T(8,128)(2,1)S(1)}, bf16[8,128,128]{2,1,0:T(8,128)(2,1)}, u32[]{:S(2)}, u32[]{:S(2)}) collective-permute-start(bf16[8,128,128]{2,1,0:T(8,128)(2,1)S(1)} %copy-done.4), channel_id=1, source_target_pairs={{0,192},{64,128},{128,64},{192,0},{256,448},{320,384},{384,320},{4... | collective-permute-start | bytes 786440 | tf_op jit(solution)/shard_map/ppermute | solution.py:12
Sparse Core Ops, SparseCore 0:
  72.9 169.3 all-gather.2

commit v2 on v1

--- a/solution.py
+++ b/solution.py
@@ -20,15 +20,15 @@
     levels = min(2, lax.axis_size("group").bit_length() - 1)
     merged = 2**levels
     n_sub = lax.axis_size("sub")
+    n_parent = parent_vals.shape[0]
     group_index = lax.axis_index("group")
+    core = lax.axis_index("sub") % 2
 
-    vals_all = [parent_vals]
-    rows_all = [parent_rows]
-    for mask in range(1, merged):
-        vals_all.append(from_partner(parent_vals, "group", mask))
-        rows_all.append(from_partner(parent_rows, "group", mask))
-    vals_all = jnp.concatenate(vals_all, axis=0)
-    rows_all = jnp.concatenate(rows_all, axis=0)
+    rows_as_block = jnp.zeros((16, block_size), jnp.bfloat16).at[0, :n_parent].set(parent_rows.astype(jnp.bfloat16))
+    packed = jnp.concatenate([parent_vals.reshape(n_parent * block_size, block_size), rows_as_block], axis=0)
+    packs = [packed] + [from_partner(packed, "group", mask) for mask in range(1, merged)]
+    vals_all = jnp.concatenate([p[: n_parent * block_size] for p in packs], axis=0).reshape(-1, block_size, block_size)
+    rows_all = jnp.concatenate([p[n_parent * block_size, :n_parent] for p in packs]).astype(jnp.int32)
 
     onehot = (
         block_cols.reshape(row_blocks, BPR)[:, :, None] == jnp.arange(vertex_blocks)[None, None, :]
@@ -52,17 +52,31 @@
         panel = mapped.reshape(row_blocks * block_size, width).astype(jnp.bfloat16)
 
     quarter = width // merged
+    half_rows = block_size // 2
     column = (group_index % merged) * quarter
     head = lax.dynamic_slice_in_dim(panel[:block_size], column, quarter, 1)
-    piece = lax.all_gather(head, "sub", axis=0, tiled=True).reshape(n_sub, block_size, quarter)
-    picked = jnp.take(piece, rows_all, axis=0)
-    parent_out = jnp.einsum(
-        "kab,kbm->am", vals_all, picked, preferred_element_type=jnp.float32
-    ).astype(jnp.bfloat16)
+    outgoing = jnp.tile(head.reshape(2, half_rows, quarter), (n_sub // 2, 1, 1))
+    mine = lax.all_to_all(outgoing, "sub", 0, 0, tiled=True)
+    theirs = from_partner(mine, "sub", 1)
+    picked_mine = jnp.take(mine, rows_all, axis=0)
+    picked_theirs = jnp.take(theirs, rows_all, axis=0)
+    picked_low = jnp.where(core == 0, picked_mine, picked_theirs)
+    picked_high = jnp.where(core == 0, picked_theirs, picked_mine)
+    parent_sum = jnp.einsum(
+        "kab,kbm->am", vals_all[:, :, :half_rows], picked_low, preferred_element_type=jnp.float32
+    ) + jnp.einsum("kab,kbm->am", vals_all[:, :, half_rows:], picked_high, preferred_element_type=jnp.float32)
+    parent_out = parent_sum.astype(jnp.bfloat16)
 
-    partial = lax.dot_general(psi, panel, (((0,), (0,)), ((), ())), preferred_element_type=jnp.float32)
-    spread = lax.all_to_all(partial.reshape(n_sub, width // n_sub, width), "sub", 0, 0, tiled=True)
-    projected = spread.sum(axis=0)
+    half = width // 2
+    keep_cols = lax.dynamic_slice_in_dim(panel, core * half, half, 1)
+    send_cols = lax.dynamic_slice_in_dim(panel, (1 - core) * half, half, 1)
+    contract = (((0,), (0,)), ((), ()))
+    keep = lax.dot_general(psi, keep_cols, contract, preferred_element_type=jnp.float32)
+    send = lax.dot_general(psi, send_cols, contract, preferred_element_type=jnp.float32)
+    chip_sum = keep + from_partner(send, "sub", 1)
+    spread = lax.all_to_all(chip_sum.reshape(n_sub, width // n_sub, half), "sub", 0, 0, tiled=True)
+    by_half = spread.reshape(n_sub // 2, 2, width // n_sub, half).sum(axis=0)
+    projected = by_half.transpose(1, 0, 2).reshape(width // n_sub, width)
     return (parent_out, projected)
 
 

time: 254 us -> 187 us (0.74)
  waiting for transfers between devices: 149 us -> 86.3 us
  between operations: 14.3 us -> 0.94 us
  local copies, waits for them, and re-layouts: 4.54 us -> 13.3 us
    all_gather x1 -> x0, waiting for transfers between devices: 76.8 us -> none  [on_device(): lax.all_gather(head, 'sub', axis=0, tiled=True)]
    ppermute x8 -> x7, waiting for transfers between devices: 46.7 us -> 67.3 us  [from_partner(): return lax.ppermute(value, axis, pairs)]
    ppermute x8 -> x7, starting transfers between devices: 38.1 us -> 29.1 us  [from_partner(): return lax.ppermute(value, axis, pairs)]
    all_to_all x1 -> x2, waiting for transfers between devices: 25.7 us -> 19.1 us  [the longest x1 10.2 us: on_device(): lax.all_to_all(chip_sum.reshape(n_sub, width // n_sub, half), 'sub', 0, 0...]
    all_to_all x1 -> x2, starting transfers between devices: 36.6 us -> 43.2 us  [the longest x1 36.8 us: on_device(): mine = lax.all_to_all(outgoing, 'sub', 0, 0, tiled=True)]
    slice x0 -> x3, local copies, waits for them, and re-layouts: none -> 2.9 us  [on_device(): p[:n_parent * block_size]]
    dot_general x2 -> x4, matrix products: 5.05 us -> 6.33 us  [the longest x1 1.82 us: on_device(): lax.dot_general(psi, keep_cols, contract, preferred_element_type=jnp.floa...]
  transfers between devices with their start and end apart: 10 -> 9, of which waited for: 5 -> 5; matrix products, arithmetic and copies ran while one was open for 2% -> 7% of each run, Pallas kernels for 0% -> 0%
where the time goes in v2:
time: 187 us; the launch traced here: 186 us
  waiting for transfers between devices  86.3 us (46%)
  starting transfers between devices  72.3 us (39%)
  local copies, waits for them, and re-layouts  13.3 us (7%)
  matrix products  9.46 us (5%)
  other arithmetic  3.4 us (2%)
    ppermute x7, waiting for transfers between devices, from_partner(): return lax.ppermute(value, axis, pairs)  67.3 us
    all_to_all x1, starting transfers between devices, on_device(): mine = lax.all_to_all(outgoing, 'sub', 0, 0, tiled=True)  36.8 us
    ppermute x7, starting transfers between devices, from_partner(): return lax.ppermute(value, axis, pairs)  29.1 us
    all_to_all x1, waiting for transfers between devices, on_device(): lax.all_to_all(chip_sum.reshape(n_sub, width // n_sub, half), 'sub', 0, 0...  10.2 us
    all_to_all x1, waiting for transfers between devices, on_device(): mine = lax.all_to_all(outgoing, 'sub', 0, 0, tiled=True)  8.81 us
    all_to_all x1, starting transfers between devices, on_device(): lax.all_to_all(chip_sum.reshape(n_sub, width // n_sub, half), 'sub', 0, 0...  6.41 us
  transfers between devices with their start and end apart: 9, of which 5 were waited for; matrix products, arithmetic and copies ran while one was open for 7% of the time, Pallas kernels for 0%

profile of v2, /device:TPU:1, one launch (start us, length us, event | category | flops | bytes accessed | tf_op | source)
XLA Modules:
  0.0 185.8 jit_solution(17680202327041828079)
XLA Ops:
  0.6 0.8 eq.23
  2.1 1.0 fusion.5
  3.3 1.2 fusion.8
  4.5 8.4 %collective-permute-start.3 = (bf16[1024,512]{1,0:T(8,128)(2,1)S(1)}, bf16[1024,512]{1,0:T(8,128)(2,1)S(1)}, u32[]{:S(2)}, u32[]{:S(2)}) collective-permute-start(bf16[1024,512]{1,0:T(8,128)(2,1)S(1)} %fusion.8), channel_id=1, source_target_pairs={{0,64},{64,0},{128,192},{192,128},{256,320},{320,256},{384,448},{4... | collective-permute-start | bytes 3145736 | tf_op jit(solution)/shard_map/ppermute | solution.py:12
  13.0 33.9 %collective-permute-done.3 = bf16[1024,512]{1,0:T(8,128)(2,1)S(1)} collective-permute-done((bf16[1024,512]{1,0:T(8,128)(2,1)S(1)}, bf16[1024,512]{1,0:T(8,128)(2,1)S(1)}, u32[]{:S(2)}, u32[]{:S(2)}) %collective-permute-start.3) | collective-permute-done | bytes 1048608 | tf_op jit(solution)/shard_map/ppermute | solution.py:12
  47.6 3.6 %collective-permute-start.4 = (bf16[1024,512]{1,0:T(8,128)(2,1)S(1)}, bf16[1024,512]{1,0:T(8,128)(2,1)}, u32[]{:S(2)}, u32[]{:S(2)}) collective-permute-start(bf16[1024,512]{1,0:T(8,128)(2,1)S(1)} %bitcast.71), channel_id=1, source_target_pairs={{0,128},{64,192},{128,0},{192,64},{256,384},{320,448},{384,256},{4... | collective-permute-start | bytes 3145736 | tf_op jit(solution)/shard_map/ppermute | solution.py:12
  51.3 12.3 %collective-permute-done.4 = bf16[1024,512]{1,0:T(8,128)(2,1)} collective-permute-done((bf16[1024,512]{1,0:T(8,128)(2,1)S(1)}, bf16[1024,512]{1,0:T(8,128)(2,1)}, u32[]{:S(2)}, u32[]{:S(2)}) %collective-permute-start.4) | collective-permute-done | bytes 1048608 | tf_op jit(solution)/shard_map/ppermute | solution.py:12
  63.6 1.5 add_convert_fusion
  65.6 1.2 tile.11
  66.8 36.8 %all-to-all-start = ((bf16[64,64,128]{2,1,0:T(8,128)(2,1)}), bf16[64,64,128]{2,1,0:T(8,128)(2,1)}, u32[]{:S(2)}, u32[]{:S(2)}) async-start(bf16[64,64,128]{2,1,0:T(8,128)(2,1)} %bitcast.74), calls=%async_computation | async-start | bytes 2097152 | tf_op jit(solution)/shard_map/all_to_all | solution.py:59
  103.7 1.7 convolution_bitcast_fusion
  105.3 2.4 %collective-permute-start.6 = (f32[512,256]{0,1:T(8,128)S(1)}, f32[512,256]{0,1:T(8,128)}, u32[]{:S(2)}, u32[]{:S(2)}) collective-permute-start(f32[512,256]{0,1:T(8,128)S(1)} %convolution_bitcast_fusion), channel_id=1, source_target_pairs={{0,1},{1,0},{2,3},{3,2},{4,5},{5,4},{6,7},{7,6},{8,9},{9,8},{10,11... | collective-permute-start | bytes 1572872 | tf_op jit(solution)/shard_map/ppermute | solution.py:12
  107.8 0.7 fusion.23
  108.6 5.8 %collective-permute-start.2 = (bf16[1040,128]{1,0:T(8,128)(2,1)}, bf16[1040,128]{1,0:T(8,128)(2,1)}, u32[]{:S(2)}, u32[]{:S(2)}) collective-permute-start(bf16[1040,128]{1,0:T(8,128)(2,1)} %fusion.23), channel_id=1, source_target_pairs={{0,192},{64,128},{128,64},{192,0},{256,448},{320,384},{384,320},{4... | collective-permute-start | bytes 798728 | tf_op jit(solution)/shard_map/ppermute | solution.py:12
  114.3 2.2 %collective-permute-start.1 = (bf16[1040,128]{1,0:T(8,128)(2,1)}, bf16[1040,128]{1,0:T(8,128)(2,1)}, u32[]{:S(2)}, u32[]{:S(2)}) collective-permute-start(bf16[1040,128]{1,0:T(8,128)(2,1)} %fusion.23), channel_id=1, source_target_pairs={{0,128},{64,192},{128,0},{192,64},{256,384},{320,448},{384,256},{4... | collective-permute-start | bytes 798728 | tf_op jit(solution)/shard_map/ppermute | solution.py:12
  116.5 4.3 %collective-permute-start = (bf16[1040,128]{1,0:T(8,128)(2,1)}, bf16[1040,128]{1,0:T(8,128)(2,1)}, u32[]{:S(2)}, u32[]{:S(2)}) collective-permute-start(bf16[1040,128]{1,0:T(8,128)(2,1)} %fusion.23), channel_id=1, source_target_pairs={{0,64},{64,0},{128,192},{192,128},{256,320},{320,256},{384,448},{4... | collective-permute-start | bytes 798728 | tf_op jit(solution)/shard_map/ppermute | solution.py:12
  120.9 21.1 %collective-permute-done.2 = bf16[1040,128]{1,0:T(8,128)(2,1)} collective-permute-done((bf16[1040,128]{1,0:T(8,128)(2,1)}, bf16[1040,128]{1,0:T(8,128)(2,1)}, u32[]{:S(2)}, u32[]{:S(2)}) %collective-permute-start.2) | collective-permute-done | bytes 266272 | tf_op jit(solution)/shard_map/ppermute | solution.py:12
  141.9 0.7 slice_bitcast_fusion
  142.6 1.8 fusion.11
  144.5 1.0 copy.13
  145.5 8.8 %all-to-all-done = bf16[64,64,128]{2,1,0:T(8,128)(2,1)} async-done(((bf16[64,64,128]{2,1,0:T(8,128)(2,1)}), bf16[64,64,128]{2,1,0:T(8,128)(2,1)}, u32[]{:S(2)}, u32[]{:S(2)}) %all-to-all-start) | async-done | bytes 1048608 | tf_op jit(solution)/shard_map/all_to_all | solution.py:59
  154.3 6.4 %all-to-all-start.1 = ((f32[64,8,256]{2,1,0:T(8,128)}), f32[64,8,256]{2,1,0:T(8,128)S(1)}, u32[]{:S(2)}, u32[]{:S(2)}) async-start(f32[64,8,256]{2,1,0:T(8,128)} %bitcast.28), calls=%async_computation.1 | async-start | bytes 1048576 | tf_op jit(solution)/shard_map/all_to_all | solution.py:77
  160.7 2.4 %collective-permute-start.5 = (bf16[64,64,128]{2,1,0:T(8,128)(2,1)}, bf16[64,64,128]{2,1,0:T(8,128)(2,1)}, u32[]{:S(2)}, u32[]{:S(2)}) collective-permute-start(bf16[64,64,128]{2,1,0:T(8,128)(2,1)} %all-to-all-done), channel_id=1, source_target_pairs={{0,1},{1,0},{2,3},{3,2},{4,5},{5,4},{6,7},{7,6},{8,9},{9,8},{10,11... | collective-permute-start | bytes 3145736 | tf_op jit(solution)/shard_map/ppermute | solution.py:12
  163.1 0.7 slice_bitcast_fusion.1
  163.8 1.0 slice.70
  164.7 1.0 slice.71
  165.7 1.0 slice.69
  167.5 10.2 %all-to-all-done.1 = f32[64,8,256]{2,1,0:T(8,128)S(1)} async-done(((f32[64,8,256]{2,1,0:T(8,128)}), f32[64,8,256]{2,1,0:T(8,128)S(1)}, u32[]{:S(2)}, u32[]{:S(2)}) %all-to-all-start.1) | async-done | bytes 524320 | tf_op jit(solution)/shard_map/all_to_all | solution.py:77
  178.4 1.9 %gather_fusion = bf16[32,64,128]{2,1,0:T(8,128)(2,1)S(1)} fusion(bf16[64,64,128]{2,1,0:T(8,128)(2,1)} %all-to-all-done, s32[1024]{0:T(1024)S(1)} %pad_clamp_fusion), kind=kCustom, calls=%fused_computation.clone | custom fusion | bytes 1048704 | tf_op jit(solution)/shard_map/jit(_take)/gather | solution.py:61
  180.3 2.6 %gather_fusion.1 = bf16[32,64,128]{2,1,0:T(8,128)(2,1)} fusion(bf16[64,64,128]{2,1,0:T(8,128)(2,1)} %collective-permute-done.5, s32[1024]{0:T(1024)S(1)} %pad_clamp_fusion), kind=kCustom, calls=%fused_computation.1.clone | custom fusion | bytes 1048704 | tf_op jit(solution)/shard_map/jit(_take)/gather | solution.py:62
  182.9 1.8 convolution_bitcast_fusion.2
  184.8 1.0 fusion.13
  (27 shorter events, 3.4 us)
Async XLA Ops:
  0.6 1.4 copy-start
  2.1 1.2 copy-start.4
  4.5 42.7 %copy-start.3 = (bf16[2,128,128]{2,1,0:T(8,128)(2,1)S(1)}, bf16[2,128,128]{2,1,0:T(8,128)(2,1)}, u32[]{:S(2)}) copy-start(bf16[2,128,128]{2,1,0:T(8,128)(2,1)} %param.14) | copy-start | bytes 196612
  4.5 42.3 %collective-permute-start.3 = (bf16[1024,512]{1,0:T(8,128)(2,1)S(1)}, bf16[1024,512]{1,0:T(8,128)(2,1)S(1)}, u32[]{:S(2)}, u32[]{:S(2)}) collective-permute-start(bf16[1024,512]{1,0:T(8,128)(2,1)S(1)} %fusion.8), channel_id=1, source_target_pairs={{0,64},{64,0},{128,192},{192,128},{256,320},{320,256},{384,448},{4... | collective-permute-start | bytes 3145736 | tf_op jit(solution)/shard_map/ppermute | solution.py:12
  47.6 15.9 %collective-permute-start.4 = (bf16[1024,512]{1,0:T(8,128)(2,1)S(1)}, bf16[1024,512]{1,0:T(8,128)(2,1)}, u32[]{:S(2)}, u32[]{:S(2)}) collective-permute-start(bf16[1024,512]{1,0:T(8,128)(2,1)S(1)} %bitcast.71), channel_id=1, source_target_pairs={{0,128},{64,192},{128,0},{192,64},{256,384},{320,448},{384,256},{4... | collective-permute-start | bytes 3145736 | tf_op jit(solution)/shard_map/ppermute | solution.py:12
  65.5 38.1 %copy-start.5 = (s32[8]{0:T(128)S(1)}, s32[8]{0:T(128)}, u32[]{:S(2)}) copy-start(s32[8]{0:T(128)} %param.17) | copy-start | bytes 100
  66.8 41.0 %copy-start.1 = (bf16[8,128,128]{2,1,0:T(8,128)(2,1)S(1)}, bf16[8,128,128]{2,1,0:T(8,128)(2,1)}, u32[]{:S(2)}) copy-start(bf16[8,128,128]{2,1,0:T(8,128)(2,1)} %param.16) | copy-start | bytes 786436
  66.8 87.5 %all-to-all-start = ((bf16[64,64,128]{2,1,0:T(8,128)(2,1)}), bf16[64,64,128]{2,1,0:T(8,128)(2,1)}, u32[]{:S(2)}, u32[]{:S(2)}) async-start(bf16[64,64,128]{2,1,0:T(8,128)(2,1)} %bitcast.74), calls=%async_computation | async-start | bytes 2097152 | tf_op jit(solution)/shard_map/all_to_all | solution.py:59
  105.3 37.3 %collective-permute-start.6 = (f32[512,256]{0,1:T(8,128)S(1)}, f32[512,256]{0,1:T(8,128)}, u32[]{:S(2)}, u32[]{:S(2)}) collective-permute-start(f32[512,256]{0,1:T(8,128)S(1)} %convolution_bitcast_fusion), channel_id=1, source_target_pairs={{0,1},{1,0},{2,3},{3,2},{4,5},{5,4},{6,7},{7,6},{8,9},{9,8},{10,11... | collective-permute-start | bytes 1572872 | tf_op jit(solution)/shard_map/ppermute | solution.py:12
  108.6 33.4 %collective-permute-start.2 = (bf16[1040,128]{1,0:T(8,128)(2,1)}, bf16[1040,128]{1,0:T(8,128)(2,1)}, u32[]{:S(2)}, u32[]{:S(2)}) collective-permute-start(bf16[1040,128]{1,0:T(8,128)(2,1)} %fusion.23), channel_id=1, source_target_pairs={{0,192},{64,128},{128,64},{192,0},{256,448},{320,384},{384,320},{4... | collective-permute-start | bytes 798728 | tf_op jit(solution)/shard_map/ppermute | solution.py:12
  114.3 48.7 %collective-permute-start.1 = (bf16[1040,128]{1,0:T(8,128)(2,1)}, bf16[1040,128]{1,0:T(8,128)(2,1)}, u32[]{:S(2)}, u32[]{:S(2)}) collective-permute-start(bf16[1040,128]{1,0:T(8,128)(2,1)} %fusion.23), channel_id=1, source_target_pairs={{0,128},{64,192},{128,0},{192,64},{256,384},{320,448},{384,256},{4... | collective-permute-start | bytes 798728 | tf_op jit(solution)/shard_map/ppermute | solution.py:12
  116.5 49.2 %collective-permute-start = (bf16[1040,128]{1,0:T(8,128)(2,1)}, bf16[1040,128]{1,0:T(8,128)(2,1)}, u32[]{:S(2)}, u32[]{:S(2)}) collective-permute-start(bf16[1040,128]{1,0:T(8,128)(2,1)} %fusion.23), channel_id=1, source_target_pairs={{0,64},{64,0},{128,192},{192,128},{256,320},{320,256},{384,448},{4... | collective-permute-start | bytes 798728 | tf_op jit(solution)/shard_map/ppermute | solution.py:12
  154.3 23.5 %all-to-all-start.1 = ((f32[64,8,256]{2,1,0:T(8,128)}), f32[64,8,256]{2,1,0:T(8,128)S(1)}, u32[]{:S(2)}, u32[]{:S(2)}) async-start(f32[64,8,256]{2,1,0:T(8,128)} %bitcast.28), calls=%async_computation.1 | async-start | bytes 1048576 | tf_op jit(solution)/shard_map/all_to_all | solution.py:77
  160.7 19.6 %collective-permute-start.5 = (bf16[64,64,128]{2,1,0:T(8,128)(2,1)}, bf16[64,64,128]{2,1,0:T(8,128)(2,1)}, u32[]{:S(2)}, u32[]{:S(2)}) collective-permute-start(bf16[64,64,128]{2,1,0:T(8,128)(2,1)} %all-to-all-done), channel_id=1, source_target_pairs={{0,1},{1,0},{2,3},{3,2},{4,5},{5,4},{6,7},{7,6},{8,9},{9,8},{10,11... | collective-permute-start | bytes 3145736 | tf_op jit(solution)/shard_map/ppermute | solution.py:12
  182.9 1.8 copy-start.2

commit v3 on v2

--- a/solution.py
+++ b/solution.py
@@ -40,16 +40,27 @@
         .astype(jnp.bfloat16)
     )
     panel = jnp.dot(dense, modes, preferred_element_type=jnp.float32).astype(jnp.bfloat16)
+
+    held = panel
+    for level in reversed(range(levels)):
+        half_len = held.shape[0] // 2
+        upper = (group_index >> level) & 1
+        keep = lax.dynamic_slice_in_dim(held, upper * half_len, half_len, 0)
+        away = lax.dynamic_slice_in_dim(held, (1 - upper) * half_len, half_len, 0)
+        total = keep.astype(jnp.float32) + from_partner(away, "group", 2**level).astype(jnp.float32)
+        held = total if level == 0 else total.astype(jnp.bfloat16)
+    mapped = held.reshape(-1, block_size, width)
     for level in range(levels):
-        sibling = from_partner(panel, "group", 2**level)
-        total = (panel.astype(jnp.float32) + sibling.astype(jnp.float32)).astype(jnp.bfloat16)
         mapped = jnp.einsum(
-            "ab,rbm->ram",
-            level_maps[level],
-            total.reshape(row_blocks, block_size, width),
-            preferred_element_type=jnp.float32,
+            "ab,rbm->ram", level_maps[level].astype(jnp.float32), mapped, preferred_element_type=jnp.float32
         )
-        panel = mapped.reshape(row_blocks * block_size, width).astype(jnp.bfloat16)
+    piece = mapped.reshape(-1, width).astype(jnp.bfloat16)
+    vals_all, rows_all, piece = lax.optimization_barrier((vals_all, rows_all, piece))
+    for level in range(levels):
+        upper = (group_index >> level) & 1
+        other = from_partner(piece, "group", 2**level)
+        piece = jnp.where(upper == 0, jnp.concatenate([piece, other], 0), jnp.concatenate([other, piece], 0))
+    panel = piece
 
     quarter = width // merged
     half_rows = block_size // 2

time: 187 us -> 177 us (0.947)
  waiting for transfers between devices: 86.3 us -> 71.9 us
  other arithmetic: 3.4 us -> 6.26 us
  local copies, waits for them, and re-layouts: 13.3 us -> 16 us
    ppermute x7 -> x9, waiting for transfers between devices: 67.3 us -> 31.7 us  [from_partner(): return lax.ppermute(value, axis, pairs)]
    all_to_all x1, starting transfers between devices: 36.8 us -> 16.4 us  [on_device(): mine = lax.all_to_all(outgoing, 'sub', 0, 0, tiled=True)]
    ppermute x7 -> x9, starting transfers between devices: 29.1 us -> 48.6 us  [from_partner(): return lax.ppermute(value, axis, pairs)]
    all_to_all x1, waiting for transfers between devices: 8.81 us -> 24.5 us  [on_device(): mine = lax.all_to_all(outgoing, 'sub', 0, 0, tiled=True)]
    all_to_all x1, waiting for transfers between devices: 10.2 us -> 15.7 us  [on_device(): lax.all_to_all(chip_sum.reshape(n_sub, width // n_sub, half), 'sub', 0, 0...]
  transfers between devices with their start and end apart: 9 -> 11, of which waited for: 5 -> 6; matrix products, arithmetic and copies ran while one was open for 7% -> 12% of each run, Pallas kernels for 0% -> 0%
where the time goes in v3:
time: 177 us; the launch traced here: 176 us
  waiting for transfers between devices  71.9 us (41%)
  starting transfers between devices  70.9 us (40%)
  local copies, waits for them, and re-layouts  16 us (9%)
  matrix products  9.58 us (5%)
  other arithmetic  6.26 us (4%)
    ppermute x9, starting transfers between devices, from_partner(): return lax.ppermute(value, axis, pairs)  48.6 us
    ppermute x9, waiting for transfers between devices, from_partner(): return lax.ppermute(value, axis, pairs)  31.7 us
    all_to_all x1, waiting for transfers between devices, on_device(): mine = lax.all_to_all(outgoing, 'sub', 0, 0, tiled=True)  24.5 us
    all_to_all x1, starting transfers between devices, on_device(): mine = lax.all_to_all(outgoing, 'sub', 0, 0, tiled=True)  16.4 us
    all_to_all x1, waiting for transfers between devices, on_device(): lax.all_to_all(chip_sum.reshape(n_sub, width // n_sub, half), 'sub', 0, 0...  15.7 us
    all_to_all x1, starting transfers between devices, on_device(): lax.all_to_all(chip_sum.reshape(n_sub, width // n_sub, half), 'sub', 0, 0...  5.86 us
  transfers between devices with their start and end apart: 11, of which 6 were waited for; matrix products, arithmetic and copies ran while one was open for 12% of the time, Pallas kernels for 0%

profile of v3, /device:TPU:1, one launch (start us, length us, event | category | flops | bytes accessed | tf_op | source)
XLA Modules:
  0.0 175.5 jit_solution(631244145317250767)
XLA Ops:
  1.4 1.7 fusion.25
  3.1 8.3 %collective-permute-start = (bf16[1040,128]{1,0:T(8,128)(2,1)}, bf16[1040,128]{1,0:T(8,128)(2,1)}, u32[]{:S(2)}, u32[]{:S(2)}) collective-permute-start(bf16[1040,128]{1,0:T(8,128)(2,1)} %fusion.25), channel_id=1, source_target_pairs={{0,64},{64,0},{128,192},{192,128},{256,320},{320,256},{384,448},{4... | collective-permute-start | bytes 798728 | tf_op jit(solution)/shard_map/ppermute | solution.py:12
  11.4 3.1 %collective-permute-start.1 = (bf16[1040,128]{1,0:T(8,128)(2,1)}, bf16[1040,128]{1,0:T(8,128)(2,1)}, u32[]{:S(2)}, u32[]{:S(2)}) collective-permute-start(bf16[1040,128]{1,0:T(8,128)(2,1)} %fusion.25), channel_id=1, source_target_pairs={{0,128},{64,192},{128,0},{192,64},{256,384},{320,448},{384,256},{4... | collective-permute-start | bytes 798728 | tf_op jit(solution)/shard_map/ppermute | solution.py:12
  14.5 1.9 %collective-permute-start.2 = (bf16[1040,128]{1,0:T(8,128)(2,1)}, bf16[1040,128]{1,0:T(8,128)(2,1)}, u32[]{:S(2)}, u32[]{:S(2)}) collective-permute-start(bf16[1040,128]{1,0:T(8,128)(2,1)} %fusion.25), channel_id=1, source_target_pairs={{0,192},{64,128},{128,64},{192,0},{256,448},{320,384},{384,320},{4... | collective-permute-start | bytes 798728 | tf_op jit(solution)/shard_map/ppermute | solution.py:12
  17.2 1.0 fusion.5
  18.4 1.2 fusion.8
  20.5 3.1 %collective-permute-start.3 = (bf16[512,512]{1,0:T(8,128)(2,1)}, bf16[512,512]{1,0:T(8,128)(2,1)S(1)}, u32[]{:S(2)}, u32[]{:S(2)}) collective-permute-start(bf16[512,512]{1,0:T(8,128)(2,1)} %constant_dynamic-slice_fusion.2), channel_id=1, source_target_pairs={{0,128},{64,192},{128,0},{192,64},{256,384},{320,448},{384,256},{4... | collective-permute-start | bytes 1572872 | tf_op jit(solution)/shard_map/ppermute | solution.py:12
  23.6 10.4 %collective-permute-done.2 = bf16[1040,128]{1,0:T(8,128)(2,1)} collective-permute-done((bf16[1040,128]{1,0:T(8,128)(2,1)}, bf16[1040,128]{1,0:T(8,128)(2,1)}, u32[]{:S(2)}, u32[]{:S(2)}) %collective-permute-start.2) | collective-permute-done | bytes 266272 | tf_op jit(solution)/shard_map/ppermute | solution.py:12
  36.3 1.0 slice.70
  38.3 1.1 pad_maximum_fusion
  39.5 8.8 %collective-permute-start.4 = (bf16[256,512]{1,0:T(8,128)(2,1)S(1)}, bf16[256,512]{1,0:T(8,128)(2,1)S(1)}, u32[]{:S(2)}, u32[]{:S(2)}) collective-permute-start(bf16[256,512]{1,0:T(8,128)(2,1)S(1)} %constant_dynamic-slice_fusion.1), channel_id=1, source_target_pairs={{0,64},{64,0},{128,192},{192,128},{256,320},{320,256},{384,448},{4... | collective-permute-start | bytes 786440 | tf_op jit(solution)/shard_map/ppermute | solution.py:12
  49.1 6.8 %collective-permute-done.4 = bf16[256,512]{1,0:T(8,128)(2,1)S(1)} collective-permute-done((bf16[256,512]{1,0:T(8,128)(2,1)S(1)}, bf16[256,512]{1,0:T(8,128)(2,1)S(1)}, u32[]{:S(2)}, u32[]{:S(2)}) %collective-permute-start.4) | collective-permute-done | bytes 262176 | tf_op jit(solution)/shard_map/ppermute | solution.py:12
  56.4 7.2 %collective-permute-start.5 = (bf16[256,512]{1,0:T(8,128)(2,1)S(1)}, bf16[256,512]{1,0:T(8,128)(2,1)S(1)}, u32[]{:S(2)}, u32[]{:S(2)}) collective-permute-start(bf16[256,512]{1,0:T(8,128)(2,1)S(1)} %bitcast.74), channel_id=1, source_target_pairs={{0,64},{64,0},{128,192},{192,128},{256,320},{320,256},{384,448},{4... | collective-permute-start | bytes 786440 | tf_op jit(solution)/shard_map/ppermute | solution.py:12
  63.6 3.8 %collective-permute-done.5 = bf16[256,512]{1,0:T(8,128)(2,1)S(1)} collective-permute-done((bf16[256,512]{1,0:T(8,128)(2,1)S(1)}, bf16[256,512]{1,0:T(8,128)(2,1)S(1)}, u32[]{:S(2)}, u32[]{:S(2)}) %collective-permute-start.5) | collective-permute-done | bytes 262176 | tf_op jit(solution)/shard_map/ppermute | solution.py:12
  67.6 11.7 %collective-permute-start.6 = (bf16[512,512]{1,0:T(8,128)(2,1)S(1)}, bf16[512,512]{1,0:T(8,128)(2,1)}, u32[]{:S(2)}, u32[]{:S(2)}) collective-permute-start(bf16[512,512]{1,0:T(8,128)(2,1)S(1)} %maximum_select_fusion.1), channel_id=1, source_target_pairs={{0,128},{64,192},{128,0},{192,64},{256,384},{320,448},{384,256},{4... | collective-permute-start | bytes 1572872 | tf_op jit(solution)/shard_map/ppermute | solution.py:12
  79.4 10.7 %collective-permute-done.6 = bf16[512,512]{1,0:T(8,128)(2,1)} collective-permute-done((bf16[512,512]{1,0:T(8,128)(2,1)S(1)}, bf16[512,512]{1,0:T(8,128)(2,1)}, u32[]{:S(2)}, u32[]{:S(2)}) %collective-permute-start.6) | collective-permute-done | bytes 524320 | tf_op jit(solution)/shard_map/ppermute | solution.py:12
  90.1 1.6 maximum_select_fusion
  91.8 1.2 tile.11
  93.0 16.4 %all-to-all-start = ((bf16[64,64,128]{2,1,0:T(8,128)(2,1)}), bf16[64,64,128]{2,1,0:T(8,128)(2,1)}, u32[]{:S(2)}, u32[]{:S(2)}) async-start(bf16[64,64,128]{2,1,0:T(8,128)(2,1)} %bitcast.70), calls=%async_computation | async-start | bytes 2097152 | tf_op jit(solution)/shard_map/all_to_all | solution.py:70
  109.5 1.7 convolution_bitcast_fusion
  111.1 2.4 %collective-permute-start.8 = (f32[512,256]{0,1:T(8,128)S(1)}, f32[512,256]{0,1:T(8,128)}, u32[]{:S(2)}, u32[]{:S(2)}) collective-permute-start(f32[512,256]{0,1:T(8,128)S(1)} %convolution_bitcast_fusion), channel_id=1, source_target_pairs={{0,1},{1,0},{2,3},{3,2},{4,5},{5,4},{6,7},{7,6},{8,9},{9,8},{10,11... | collective-permute-start | bytes 1572872 | tf_op jit(solution)/shard_map/ppermute | solution.py:12
  113.6 24.5 %all-to-all-done = bf16[64,64,128]{2,1,0:T(8,128)(2,1)} async-done(((bf16[64,64,128]{2,1,0:T(8,128)(2,1)}), bf16[64,64,128]{2,1,0:T(8,128)(2,1)}, u32[]{:S(2)}, u32[]{:S(2)}) %all-to-all-start) | async-done | bytes 1048608 | tf_op jit(solution)/shard_map/all_to_all | solution.py:70
  138.1 1.9 %collective-permute-start.7 = (bf16[64,64,128]{2,1,0:T(8,128)(2,1)}, bf16[64,64,128]{2,1,0:T(8,128)(2,1)}, u32[]{:S(2)}, u32[]{:S(2)}) collective-permute-start(bf16[64,64,128]{2,1,0:T(8,128)(2,1)} %all-to-all-done), channel_id=1, source_target_pairs={{0,1},{1,0},{2,3},{3,2},{4,5},{5,4},{6,7},{7,6},{8,9},{9,8},{10,11... | collective-permute-start | bytes 3145736 | tf_op jit(solution)/shard_map/ppermute | solution.py:12
  140.0 2.6 %fusion.11 = f32[512,256]{0,1:T(8,128)} fusion(f32[512,256]{0,1:T(8,128)} %collective-permute-done.8, bf16[1024,512]{1,0:T(8,128)(2,1)} %param.15, bf16[1024,512]{1,0:T(8,128)(2,1)S(1)} %maximum_select_fusion, s32[]{:T(128)S(6)} %select_n.81), kind=kOutput, calls=%fused_computation.11 | convolution fusion | flops 268566528 | bytes 2621444 | tf_op jit(solution)/shard_map/dot_general | solution.py:85
  142.7 2.1 %copy.13 = f32[512,256]{1,0:T(8,128)} copy(f32[512,256]{0,1:T(8,128)} %fusion.11) | data formatting | bytes 1048576 | tf_op jit(solution)/shard_map/add | solution.py:87
  144.8 5.9 %all-to-all-start.1 = ((f32[64,8,256]{2,1,0:T(8,128)}), f32[64,8,256]{2,1,0:T(8,128)S(1)}, u32[]{:S(2)}, u32[]{:S(2)}) async-start(f32[64,8,256]{2,1,0:T(8,128)} %bitcast.73), calls=%async_computation.1 | async-start | bytes 1048576 | tf_op jit(solution)/shard_map/all_to_all | solution.py:88
  150.7 1.3 copy.11
  152.0 15.7 %all-to-all-done.1 = f32[64,8,256]{2,1,0:T(8,128)S(1)} async-done(((f32[64,8,256]{2,1,0:T(8,128)}), f32[64,8,256]{2,1,0:T(8,128)S(1)}, u32[]{:S(2)}, u32[]{:S(2)}) %all-to-all-start.1) | async-done | bytes 524320 | tf_op jit(solution)/shard_map/all_to_all | solution.py:88
  168.4 1.9 %gather_fusion = bf16[32,64,128]{2,1,0:T(8,128)(2,1)S(1)} fusion(bf16[64,64,128]{2,1,0:T(8,128)(2,1)} %all-to-all-done, s32[1024]{0:T(1024)S(1)} %pad_clamp_fusion), kind=kCustom, calls=%fused_computation.clone | custom fusion | bytes 1048704 | tf_op jit(solution)/shard_map/jit(_take)/gather | solution.py:72
  170.3 2.7 %gather_fusion.1 = bf16[32,64,128]{2,1,0:T(8,128)(2,1)} fusion(bf16[64,64,128]{2,1,0:T(8,128)(2,1)} %collective-permute-done.7, s32[1024]{0:T(1024)S(1)} %pad_clamp_fusion), kind=kCustom, calls=%fused_computation.1.clone | custom fusion | bytes 1048704 | tf_op jit(solution)/shard_map/jit(_take)/gather | solution.py:73
  172.9 1.6 convolution_bitcast_fusion.3
  174.5 1.1 fusion.15
  (39 shorter events, 8.2 us)
Async XLA Ops:
  0.6 16.5 %copy-start = (bf16[48,128,128]{2,1,0:T(8,128)(2,1)S(1)}, bf16[48,128,128]{2,1,0:T(8,128)(2,1)}, u32[]{:S(2)}) copy-start(bf16[48,128,128]{2,1,0:T(8,128)(2,1)} %param.12) | copy-start | bytes 4718596
  3.1 34.2 %collective-permute-start = (bf16[1040,128]{1,0:T(8,128)(2,1)}, bf16[1040,128]{1,0:T(8,128)(2,1)}, u32[]{:S(2)}, u32[]{:S(2)}) collective-permute-start(bf16[1040,128]{1,0:T(8,128)(2,1)} %fusion.25), channel_id=1, source_target_pairs={{0,64},{64,0},{128,192},{192,128},{256,320},{320,256},{384,448},{4... | collective-permute-start | bytes 798728 | tf_op jit(solution)/shard_map/ppermute | solution.py:12
  11.4 23.3 %collective-permute-start.1 = (bf16[1040,128]{1,0:T(8,128)(2,1)}, bf16[1040,128]{1,0:T(8,128)(2,1)}, u32[]{:S(2)}, u32[]{:S(2)}) collective-permute-start(bf16[1040,128]{1,0:T(8,128)(2,1)} %fusion.25), channel_id=1, source_target_pairs={{0,128},{64,192},{128,0},{192,64},{256,384},{320,448},{384,256},{4... | collective-permute-start | bytes 798728 | tf_op jit(solution)/shard_map/ppermute | solution.py:12
  14.5 19.5 %collective-permute-start.2 = (bf16[1040,128]{1,0:T(8,128)(2,1)}, bf16[1040,128]{1,0:T(8,128)(2,1)}, u32[]{:S(2)}, u32[]{:S(2)}) collective-permute-start(bf16[1040,128]{1,0:T(8,128)(2,1)} %fusion.25), channel_id=1, source_target_pairs={{0,192},{64,128},{128,64},{192,0},{256,448},{320,384},{384,320},{4... | collective-permute-start | bytes 798728 | tf_op jit(solution)/shard_map/ppermute | solution.py:12
  17.2 1.2 copy-start.6
  19.6 18.6 %copy-start.3 = (bf16[8,128,128]{2,1,0:T(8,128)(2,1)S(1)}, bf16[8,128,128]{2,1,0:T(8,128)(2,1)}, u32[]{:S(2)}) copy-start(bf16[8,128,128]{2,1,0:T(8,128)(2,1)} %param.16) | copy-start | bytes 786436
  20.5 18.8 %collective-permute-start.3 = (bf16[512,512]{1,0:T(8,128)(2,1)}, bf16[512,512]{1,0:T(8,128)(2,1)S(1)}, u32[]{:S(2)}, u32[]{:S(2)}) collective-permute-start(bf16[512,512]{1,0:T(8,128)(2,1)} %constant_dynamic-slice_fusion.2), channel_id=1, source_target_pairs={{0,128},{64,192},{128,0},{192,64},{256,384},{320,448},{384,256},{4... | collective-permute-start | bytes 1572872 | tf_op jit(solution)/shard_map/ppermute | solution.py:12
  38.3 17.7 %copy-start.5 = (bf16[2,128,128]{2,1,0:T(8,128)(2,1)S(1)}, bf16[2,128,128]{2,1,0:T(8,128)(2,1)}, u32[]{:S(2)}) copy-start(bf16[2,128,128]{2,1,0:T(8,128)(2,1)} %param.14) | copy-start | bytes 196612
  39.5 16.4 %collective-permute-start.4 = (bf16[256,512]{1,0:T(8,128)(2,1)S(1)}, bf16[256,512]{1,0:T(8,128)(2,1)S(1)}, u32[]{:S(2)}, u32[]{:S(2)}) collective-permute-start(bf16[256,512]{1,0:T(8,128)(2,1)S(1)} %constant_dynamic-slice_fusion.1), channel_id=1, source_target_pairs={{0,64},{64,0},{128,192},{192,128},{256,320},{320,256},{384,448},{4... | collective-permute-start | bytes 786440 | tf_op jit(solution)/shard_map/ppermute | solution.py:12
  56.4 11.0 %collective-permute-start.5 = (bf16[256,512]{1,0:T(8,128)(2,1)S(1)}, bf16[256,512]{1,0:T(8,128)(2,1)S(1)}, u32[]{:S(2)}, u32[]{:S(2)}) collective-permute-start(bf16[256,512]{1,0:T(8,128)(2,1)S(1)} %bitcast.74), channel_id=1, source_target_pairs={{0,64},{64,0},{128,192},{192,128},{256,320},{320,256},{384,448},{4... | collective-permute-start | bytes 786440 | tf_op jit(solution)/shard_map/ppermute | solution.py:12
  67.6 22.5 %collective-permute-start.6 = (bf16[512,512]{1,0:T(8,128)(2,1)S(1)}, bf16[512,512]{1,0:T(8,128)(2,1)}, u32[]{:S(2)}, u32[]{:S(2)}) collective-permute-start(bf16[512,512]{1,0:T(8,128)(2,1)S(1)} %maximum_select_fusion.1), channel_id=1, source_target_pairs={{0,128},{64,192},{128,0},{192,64},{256,384},{320,448},{384,256},{4... | collective-permute-start | bytes 1572872 | tf_op jit(solution)/shard_map/ppermute | solution.py:12
  93.0 45.1 %all-to-all-start = ((bf16[64,64,128]{2,1,0:T(8,128)(2,1)}), bf16[64,64,128]{2,1,0:T(8,128)(2,1)}, u32[]{:S(2)}, u32[]{:S(2)}) async-start(bf16[64,64,128]{2,1,0:T(8,128)(2,1)} %bitcast.70), calls=%async_computation | async-start | bytes 2097152 | tf_op jit(solution)/shard_map/all_to_all | solution.py:70
  111.1 28.9 %collective-permute-start.8 = (f32[512,256]{0,1:T(8,128)S(1)}, f32[512,256]{0,1:T(8,128)}, u32[]{:S(2)}, u32[]{:S(2)}) collective-permute-start(f32[512,256]{0,1:T(8,128)S(1)} %convolution_bitcast_fusion), channel_id=1, source_target_pairs={{0,1},{1,0},{2,3},{3,2},{4,5},{5,4},{6,7},{7,6},{8,9},{9,8},{10,11... | collective-permute-start | bytes 1572872 | tf_op jit(solution)/shard_map/ppermute | solution.py:12
  138.1 32.2 %collective-permute-start.7 = (bf16[64,64,128]{2,1,0:T(8,128)(2,1)}, bf16[64,64,128]{2,1,0:T(8,128)(2,1)}, u32[]{:S(2)}, u32[]{:S(2)}) collective-permute-start(bf16[64,64,128]{2,1,0:T(8,128)(2,1)} %all-to-all-done), channel_id=1, source_target_pairs={{0,1},{1,0},{2,3},{3,2},{4,5},{5,4},{6,7},{7,6},{8,9},{9,8},{10,11... | collective-permute-start | bytes 3145736 | tf_op jit(solution)/shard_map/ppermute | solution.py:12
  142.7 8.0 %copy-start.1 = (bf16[4096,128]{1,0:T(8,128)(2,1)S(1)}, bf16[4096,128]{1,0:T(8,128)(2,1)}, u32[]{:S(2)}) copy-start(bf16[4096,128]{1,0:T(8,128)(2,1)} %pad_maximum_fusion) | copy-start | bytes 3145732
  144.8 22.9 %all-to-all-start.1 = ((f32[64,8,256]{2,1,0:T(8,128)}), f32[64,8,256]{2,1,0:T(8,128)S(1)}, u32[]{:S(2)}, u32[]{:S(2)}) async-start(f32[64,8,256]{2,1,0:T(8,128)} %bitcast.73), calls=%async_computation.1 | async-start | bytes 1048576 | tf_op jit(solution)/shard_map/all_to_all | solution.py:88
  152.0 20.9 %copy-start.2 = (bf16[32,128,128]{1,2,0:T(8,128)(2,1)S(1)}, bf16[32,128,128]{1,2,0:T(8,128)(2,1)}, u32[]{:S(2)}) copy-start(bf16[32,128,128]{1,2,0:T(8,128)(2,1)} %copy.11) | copy-start | bytes 3145732
  172.9 1.6 copy-start.4

commit v4 on v2

--- a/solution.py
+++ b/solution.py
@@ -26,9 +26,6 @@
 
     rows_as_block = jnp.zeros((16, block_size), jnp.bfloat16).at[0, :n_parent].set(parent_rows.astype(jnp.bfloat16))
     packed = jnp.concatenate([parent_vals.reshape(n_parent * block_size, block_size), rows_as_block], axis=0)
-    packs = [packed] + [from_partner(packed, "group", mask) for mask in range(1, merged)]
-    vals_all = jnp.concatenate([p[: n_parent * block_size] for p in packs], axis=0).reshape(-1, block_size, block_size)
-    rows_all = jnp.concatenate([p[n_parent * block_size, :n_parent] for p in packs]).astype(jnp.int32)
 
     onehot = (
         block_cols.reshape(row_blocks, BPR)[:, :, None] == jnp.arange(vertex_blocks)[None, None, :]
@@ -40,9 +37,16 @@
         .astype(jnp.bfloat16)
     )
     panel = jnp.dot(dense, modes, preferred_element_type=jnp.float32).astype(jnp.bfloat16)
+    carried = packed[None]
     for level in range(levels):
         sibling = from_partner(panel, "group", 2**level)
+        partner = levels - 1 - level
+        carried, panel = lax.optimization_barrier((carried, panel))
+        arrived = from_partner(carried, "group", 2**partner)
         total = (panel.astype(jnp.float32) + sibling.astype(jnp.float32)).astype(jnp.bfloat16)
+        if level < levels - 1:
+            arrived, total = lax.optimization_barrier((arrived, total))
+        carried = jnp.concatenate([carried, arrived], axis=0)
         mapped = jnp.einsum(
             "ab,rbm->ram",
             level_maps[level],
@@ -50,6 +54,8 @@
             preferred_element_type=jnp.float32,
         )
         panel = mapped.reshape(row_blocks * block_size, width).astype(jnp.bfloat16)
+    vals_all = carried[:, : n_parent * block_size].reshape(-1, block_size, block_size)
+    rows_all = carried[:, n_parent * block_size, :n_parent].reshape(-1).astype(jnp.int32)
 
     quarter = width // merged
     half_rows = block_size // 2

time: 187 us -> 187 us (level)
  starting transfers between devices: 72.3 us -> 67.8 us
  waiting for transfers between devices: 86.3 us -> 90.5 us
    all_to_all x1, waiting for transfers between devices: 8.81 us -> 36.2 us  [on_device(): mine = lax.all_to_all(outgoing, 'sub', 0, 0, tiled=True)]
    ppermute x7 -> x6, waiting for transfers between devices: 67.3 us -> 42 us  [from_partner(): return lax.ppermute(value, axis, pairs)]
    ppermute x7 -> x6, starting transfers between devices: 29.1 us -> 24.8 us  [from_partner(): return lax.ppermute(value, axis, pairs)]
    all_to_all x1, waiting for transfers between devices: 10.2 us -> 12.3 us  [on_device(): lax.all_to_all(chip_sum.reshape(n_sub, width // n_sub, half), 'sub', 0, 0...]
    squeeze x3 -> x0, local copies, waits for them, and re-layouts: 2.02 us -> none  [on_device(): p[n_parent * block_size, :n_parent]]
  transfers between devices with their start and end apart: 9 -> 8, of which waited for: 5 -> 4; matrix products, arithmetic and copies ran while one was open for 7% -> 7% of each run, Pallas kernels for 0% -> 0%
where the time goes in v4:
time: 187 us; the launch traced here: 186 us
  waiting for transfers between devices  90.5 us (48%)
  starting transfers between devices  67.8 us (36%)
  local copies, waits for them, and re-layouts  12.1 us (6%)
  matrix products  11.1 us (6%)
  other arithmetic  3.57 us (2%)
    ppermute x6, waiting for transfers between devices, from_partner(): return lax.ppermute(value, axis, pairs)  42 us
    all_to_all x1, starting transfers between devices, on_device(): mine = lax.all_to_all(outgoing, 'sub', 0, 0, tiled=True)  36.6 us
    all_to_all x1, waiting for transfers between devices, on_device(): mine = lax.all_to_all(outgoing, 'sub', 0, 0, tiled=True)  36.2 us
    ppermute x6, starting transfers between devices, from_partner(): return lax.ppermute(value, axis, pairs)  24.8 us
    all_to_all x1, waiting for transfers between devices, on_device(): lax.all_to_all(chip_sum.reshape(n_sub, width // n_sub, half), 'sub', 0, 0...  12.3 us
    all_to_all x1, starting transfers between devices, on_device(): lax.all_to_all(chip_sum.reshape(n_sub, width // n_sub, half), 'sub', 0, 0...  6.41 us
  transfers between devices with their start and end apart: 8, of which 4 were waited for; matrix products, arithmetic and copies ran while one was open for 7% of the time, Pallas kernels for 0%

profile of v4, /device:TPU:1, one launch (start us, length us, event | category | flops | bytes accessed | tf_op | source)
XLA Modules:
  0.0 186.1 jit_solution(10961917856744109321)
XLA Ops:
  0.6 0.8 eq.22
  1.5 0.6 copy-done
  2.1 1.0 fusion.5
  3.3 1.2 fusion.8
  4.5 8.4 %collective-permute-start.1 = (bf16[1024,512]{1,0:T(8,128)(2,1)S(1)}, bf16[1024,512]{1,0:T(8,128)(2,1)S(1)}, u32[]{:S(2)}, u32[]{:S(2)}) collective-permute-start(bf16[1024,512]{1,0:T(8,128)(2,1)S(1)} %fusion.8), channel_id=1, source_target_pairs={{0,64},{64,0},{128,192},{192,128},{256,320},{320,256},{384,448},{4... | collective-permute-start | bytes 3145736 | tf_op jit(solution)/shard_map/ppermute | solution.py:12
  13.0 3.1 %collective-permute-start = (bf16[1,1040,128]{2,1,0:T(8,128)(2,1)S(1)}, bf16[1,1040,128]{2,1,0:T(8,128)(2,1)S(1)}, u32[]{:S(2)}, u32[]{:S(2)}) collective-permute-start(bf16[1,1040,128]{2,1,0:T(8,128)(2,1)S(1)} %fusion.24), channel_id=1, source_target_pairs={{0,128},{64,192},{128,0},{192,64},{256,384},{320,448},{384,256},{4... | collective-permute-start | bytes 798728 | tf_op jit(solution)/shard_map/ppermute | solution.py:12
  16.1 30.8 %collective-permute-done.1 = bf16[1024,512]{1,0:T(8,128)(2,1)S(1)} collective-permute-done((bf16[1024,512]{1,0:T(8,128)(2,1)S(1)}, bf16[1024,512]{1,0:T(8,128)(2,1)S(1)}, u32[]{:S(2)}, u32[]{:S(2)}) %collective-permute-start.1) | collective-permute-done | bytes 1048608 | tf_op jit(solution)/shard_map/ppermute | solution.py:12
  46.9 0.3 add_convert_fusion.1
  47.3 0.4 convolution_convert_fusion.1
  48.0 3.6 %collective-permute-start.3 = (bf16[1024,512]{1,0:T(8,128)(2,1)S(1)}, bf16[1024,512]{1,0:T(8,128)(2,1)}, u32[]{:S(2)}, u32[]{:S(2)}) collective-permute-start(bf16[1024,512]{1,0:T(8,128)(2,1)S(1)} %bitcast.66), channel_id=1, source_target_pairs={{0,128},{64,192},{128,0},{192,64},{256,384},{320,448},{384,256},{4... | collective-permute-start | bytes 3145736 | tf_op jit(solution)/shard_map/ppermute | solution.py:12
  51.6 1.0 pad_maximum_fusion
  52.6 11.3 %collective-permute-done.3 = bf16[1024,512]{1,0:T(8,128)(2,1)} collective-permute-done((bf16[1024,512]{1,0:T(8,128)(2,1)S(1)}, bf16[1024,512]{1,0:T(8,128)(2,1)}, u32[]{:S(2)}, u32[]{:S(2)}) %collective-permute-start.3) | collective-permute-done | bytes 1048608 | tf_op jit(solution)/shard_map/ppermute | solution.py:12
  63.9 1.5 add_convert_fusion
  65.4 0.4 convolution_convert_fusion
  65.9 1.3 tile.11
  67.1 36.6 %all-to-all-start = ((bf16[64,64,128]{2,1,0:T(8,128)(2,1)}), bf16[64,64,128]{2,1,0:T(8,128)(2,1)}, u32[]{:S(2)}, u32[]{:S(2)}) async-start(bf16[64,64,128]{2,1,0:T(8,128)(2,1)} %bitcast.70), calls=%async_computation | async-start | bytes 2097152 | tf_op jit(solution)/shard_map/all_to_all | solution.py:65
  103.8 2.5 %convolution_bitcast_fusion = f32[512,256]{0,1:T(8,128)} fusion(bf16[1024,512]{1,0:T(8,128)(2,1)} %param.15, bf16[1024,512]{1,0:T(8,128)(2,1)S(1)} %bitcast.64, s32[]{:T(128)S(6)} %select_n.46), kind=kOutput, calls=%fused_computation.13 | convolution fusion | flops 268435456 | bytes 2097156 | tf_op jit(solution)/shard_map/dot_general | solution.py:81
  106.3 2.4 %collective-permute-start.5 = (f32[512,256]{0,1:T(8,128)}, f32[512,256]{0,1:T(8,128)}, u32[]{:S(2)}, u32[]{:S(2)}) collective-permute-start(f32[512,256]{0,1:T(8,128)} %convolution_bitcast_fusion), channel_id=1, source_target_pairs={{0,1},{1,0},{2,3},{3,2},{4,5},{5,4},{6,7},{7,6},{8,9},{9,8},{10,11... | collective-permute-start | bytes 1572872 | tf_op jit(solution)/shard_map/ppermute | solution.py:12
  108.7 4.8 %collective-permute-start.2 = (bf16[2,1040,128]{2,1,0:T(8,128)(2,1)S(1)}, bf16[2,1040,128]{2,1,0:T(8,128)(2,1)}, u32[]{:S(2)}, u32[]{:S(2)}) collective-permute-start(bf16[2,1040,128]{2,1,0:T(8,128)(2,1)S(1)} %pad_maximum_fusion), channel_id=1, source_target_pairs={{0,64},{64,0},{128,192},{192,128},{256,320},{320,256},{384,448},{4... | collective-permute-start | bytes 1597448 | tf_op jit(solution)/shard_map/ppermute | solution.py:12
  113.6 2.6 %fusion.11 = f32[512,256]{0,1:T(8,128)} fusion(f32[512,256]{0,1:T(8,128)} %collective-permute-done.5, bf16[1024,512]{1,0:T(8,128)(2,1)} %param.15, bf16[1024,512]{1,0:T(8,128)(2,1)S(1)} %bitcast.65, s32[]{:T(128)S(6)} %select_n.45), kind=kOutput, calls=%fused_computation.15 | convolution fusion | flops 268566528 | bytes 2621444 | tf_op jit(solution)/shard_map/dot_general | solution.py:80
  116.2 2.1 %copy.13 = f32[512,256]{1,0:T(8,128)} copy(f32[512,256]{0,1:T(8,128)} %fusion.11) | data formatting | bytes 1048576 | tf_op jit(solution)/shard_map/add | solution.py:82
  118.3 36.2 %all-to-all-done = bf16[64,64,128]{2,1,0:T(8,128)(2,1)} async-done(((bf16[64,64,128]{2,1,0:T(8,128)(2,1)}), bf16[64,64,128]{2,1,0:T(8,128)(2,1)}, u32[]{:S(2)}, u32[]{:S(2)}) %all-to-all-start) | async-done | bytes 1048608 | tf_op jit(solution)/shard_map/all_to_all | solution.py:65
  154.5 6.4 %all-to-all-start.1 = ((f32[64,8,256]{2,1,0:T(8,128)}), f32[64,8,256]{2,1,0:T(8,128)S(1)}, u32[]{:S(2)}, u32[]{:S(2)}) async-start(f32[64,8,256]{2,1,0:T(8,128)} %bitcast.26), calls=%async_computation.1 | async-start | bytes 1048576 | tf_op jit(solution)/shard_map/all_to_all | solution.py:83
  160.9 2.4 %collective-permute-start.4 = (bf16[64,64,128]{2,1,0:T(8,128)(2,1)}, bf16[64,64,128]{2,1,0:T(8,128)(2,1)}, u32[]{:S(2)}, u32[]{:S(2)}) collective-permute-start(bf16[64,64,128]{2,1,0:T(8,128)(2,1)} %all-to-all-done), channel_id=1, source_target_pairs={{0,1},{1,0},{2,3},{3,2},{4,5},{5,4},{6,7},{7,6},{8,9},{9,8},{10,11... | collective-permute-start | bytes 3145736 | tf_op jit(solution)/shard_map/ppermute | solution.py:12
  163.3 1.1 constant_dynamic-update-slice_fusion
  164.4 1.0 slice.49
  165.6 12.3 %all-to-all-done.1 = f32[64,8,256]{2,1,0:T(8,128)S(1)} async-done(((f32[64,8,256]{2,1,0:T(8,128)}), f32[64,8,256]{2,1,0:T(8,128)S(1)}, u32[]{:S(2)}, u32[]{:S(2)}) %all-to-all-start.1) | async-done | bytes 524320 | tf_op jit(solution)/shard_map/all_to_all | solution.py:83
  177.9 0.6 reduce_sum.9
  178.6 2.0 %gather_fusion = bf16[32,64,128]{2,1,0:T(8,128)(2,1)S(1)} fusion(bf16[64,64,128]{2,1,0:T(8,128)(2,1)} %all-to-all-done, s32[1024]{0:T(1024)S(1)} %pad_clamp_fusion), kind=kCustom, calls=%fused_computation.clone | custom fusion | bytes 1048704 | tf_op jit(solution)/shard_map/jit(_take)/gather | solution.py:67
  180.6 2.6 %gather_fusion.1 = bf16[32,64,128]{2,1,0:T(8,128)(2,1)} fusion(bf16[64,64,128]{2,1,0:T(8,128)(2,1)} %collective-permute-done.4, s32[1024]{0:T(1024)S(1)} %pad_clamp_fusion), kind=kCustom, calls=%fused_computation.1.clone | custom fusion | bytes 1048704 | tf_op jit(solution)/shard_map/jit(_take)/gather | solution.py:68
  183.2 1.8 convolution_bitcast_fusion.2
  185.0 1.0 fusion.13
  (29 shorter events, 0.7 us)
Async XLA Ops:
  0.6 1.4 copy-start
  2.1 1.2 copy-start.6
  3.3 9.7 %copy-start.7 = (s32[8]{0:T(128)S(1)}, s32[8]{0:T(128)}, u32[]{:S(2)}) copy-start(s32[8]{0:T(128)} %param.17) | copy-start | bytes 100
  3.3 9.7 %copy-start.4 = (bf16[8,128,128]{2,1,0:T(8,128)(2,1)S(1)}, bf16[8,128,128]{2,1,0:T(8,128)(2,1)}, u32[]{:S(2)}) copy-start(bf16[8,128,128]{2,1,0:T(8,128)(2,1)} %param.16) | copy-start | bytes 786436
  4.5 42.7 %copy-start.5 = (bf16[2,128,128]{2,1,0:T(8,128)(2,1)S(1)}, bf16[2,128,128]{2,1,0:T(8,128)(2,1)}, u32[]{:S(2)}) copy-start(bf16[2,128,128]{2,1,0:T(8,128)(2,1)} %param.14) | copy-start | bytes 196612
  4.5 42.4 %collective-permute-start.1 = (bf16[1024,512]{1,0:T(8,128)(2,1)S(1)}, bf16[1024,512]{1,0:T(8,128)(2,1)S(1)}, u32[]{:S(2)}, u32[]{:S(2)}) collective-permute-start(bf16[1024,512]{1,0:T(8,128)(2,1)S(1)} %fusion.8), channel_id=1, source_target_pairs={{0,64},{64,0},{128,192},{192,128},{256,320},{320,256},{384,448},{4... | collective-permute-start | bytes 3145736 | tf_op jit(solution)/shard_map/ppermute | solution.py:12
  13.0 34.2 %collective-permute-start = (bf16[1,1040,128]{2,1,0:T(8,128)(2,1)S(1)}, bf16[1,1040,128]{2,1,0:T(8,128)(2,1)S(1)}, u32[]{:S(2)}, u32[]{:S(2)}) collective-permute-start(bf16[1,1040,128]{2,1,0:T(8,128)(2,1)S(1)} %fusion.24), channel_id=1, source_target_pairs={{0,128},{64,192},{128,0},{192,64},{256,384},{320,448},{384,256},{4... | collective-permute-start | bytes 798728 | tf_op jit(solution)/shard_map/ppermute | solution.py:12
  47.3 0.7 copy-start.3
  48.0 15.9 %collective-permute-start.3 = (bf16[1024,512]{1,0:T(8,128)(2,1)S(1)}, bf16[1024,512]{1,0:T(8,128)(2,1)}, u32[]{:S(2)}, u32[]{:S(2)}) collective-permute-start(bf16[1024,512]{1,0:T(8,128)(2,1)S(1)} %bitcast.66), channel_id=1, source_target_pairs={{0,128},{64,192},{128,0},{192,64},{256,384},{320,448},{384,256},{4... | collective-permute-start | bytes 3145736 | tf_op jit(solution)/shard_map/ppermute | solution.py:12
  67.1 87.3 %all-to-all-start = ((bf16[64,64,128]{2,1,0:T(8,128)(2,1)}), bf16[64,64,128]{2,1,0:T(8,128)(2,1)}, u32[]{:S(2)}, u32[]{:S(2)}) async-start(bf16[64,64,128]{2,1,0:T(8,128)(2,1)} %bitcast.70), calls=%async_computation | async-start | bytes 2097152 | tf_op jit(solution)/shard_map/all_to_all | solution.py:65
  106.3 7.3 %collective-permute-start.5 = (f32[512,256]{0,1:T(8,128)}, f32[512,256]{0,1:T(8,128)}, u32[]{:S(2)}, u32[]{:S(2)}) collective-permute-start(f32[512,256]{0,1:T(8,128)} %convolution_bitcast_fusion), channel_id=1, source_target_pairs={{0,1},{1,0},{2,3},{3,2},{4,5},{5,4},{6,7},{7,6},{8,9},{9,8},{10,11... | collective-permute-start | bytes 1572872 | tf_op jit(solution)/shard_map/ppermute | solution.py:12
  108.7 54.6 %collective-permute-start.2 = (bf16[2,1040,128]{2,1,0:T(8,128)(2,1)S(1)}, bf16[2,1040,128]{2,1,0:T(8,128)(2,1)}, u32[]{:S(2)}, u32[]{:S(2)}) collective-permute-start(bf16[2,1040,128]{2,1,0:T(8,128)(2,1)S(1)} %pad_maximum_fusion), channel_id=1, source_target_pairs={{0,64},{64,0},{128,192},{192,128},{256,320},{320,256},{384,448},{4... | collective-permute-start | bytes 1597448 | tf_op jit(solution)/shard_map/ppermute | solution.py:12
  154.5 23.5 %all-to-all-start.1 = ((f32[64,8,256]{2,1,0:T(8,128)}), f32[64,8,256]{2,1,0:T(8,128)S(1)}, u32[]{:S(2)}, u32[]{:S(2)}) async-start(f32[64,8,256]{2,1,0:T(8,128)} %bitcast.26), calls=%async_computation.1 | async-start | bytes 1048576 | tf_op jit(solution)/shard_map/all_to_all | solution.py:83
  160.9 19.7 %collective-permute-start.4 = (bf16[64,64,128]{2,1,0:T(8,128)(2,1)}, bf16[64,64,128]{2,1,0:T(8,128)(2,1)}, u32[]{:S(2)}, u32[]{:S(2)}) collective-permute-start(bf16[64,64,128]{2,1,0:T(8,128)(2,1)} %all-to-all-done), channel_id=1, source_target_pairs={{0,1},{1,0},{2,3},{3,2},{4,5},{5,4},{6,7},{7,6},{8,9},{9,8},{10,11... | collective-permute-start | bytes 3145736 | tf_op jit(solution)/shard_map/ppermute | solution.py:12
  178.6 4.6 %copy-start.1 = (bf16[4,1024,128]{2,1,0:T(8,128)(2,1)S(1)}, bf16[4,1024,128]{2,1,0:T(8,128)(2,1)}, u32[]{:S(2)}) copy-start(bf16[4,1024,128]{2,1,0:T(8,128)(2,1)} %slice.49) | copy-start | bytes 3145732
  183.2 1.8 copy-start.2

commit v5 on v4

--- a/solution.py
+++ b/solution.py
@@ -54,13 +54,13 @@
             preferred_element_type=jnp.float32,
         )
         panel = mapped.reshape(row_blocks * block_size, width).astype(jnp.bfloat16)
-    vals_all = carried[:, : n_parent * block_size].reshape(-1, block_size, block_size)
-    rows_all = carried[:, n_parent * block_size, :n_parent].reshape(-1).astype(jnp.int32)
-
     quarter = width // merged
     half_rows = block_size // 2
     column = (group_index % merged) * quarter
     head = lax.dynamic_slice_in_dim(panel[:block_size], column, quarter, 1)
+    carried, head = lax.optimization_barrier((carried, head))
+    vals_all = carried[:, : n_parent * block_size].reshape(-1, block_size, block_size)
+    rows_all = carried[:, n_parent * block_size, :n_parent].reshape(-1).astype(jnp.int32)
     outgoing = jnp.tile(head.reshape(2, half_rows, quarter), (n_sub // 2, 1, 1))
     mine = lax.all_to_all(outgoing, "sub", 0, 0, tiled=True)
     theirs = from_partner(mine, "sub", 1)

time: 187 us -> 179 us (0.957)
  waiting for transfers between devices: 90.5 us -> 80.1 us
    all_to_all x1, waiting for transfers between devices: 36.2 us -> 24.5 us  [on_device(): mine = lax.all_to_all(outgoing, 'sub', 0, 0, tiled=True)]
    all_to_all x1, waiting for transfers between devices: 12.3 us -> 15.9 us  [on_device(): lax.all_to_all(chip_sum.reshape(n_sub, width // n_sub, half), 'sub', 0, 0...]
    ppermute x6, waiting for transfers between devices: 42 us -> 39.8 us  [from_partner(): return lax.ppermute(value, axis, pairs)]
    ppermute x6, starting transfers between devices: 24.8 us -> 27 us  [from_partner(): return lax.ppermute(value, axis, pairs)]
where the time goes in v5:
time: 179 us; the launch traced here: 176 us
  waiting for transfers between devices  80.1 us (45%)
  starting transfers between devices  69.6 us (39%)
  local copies, waits for them, and re-layouts  10.7 us (6%)
  matrix products  10.3 us (6%)
  other arithmetic  4.68 us (3%)
    ppermute x6, waiting for transfers between devices, from_partner(): return lax.ppermute(value, axis, pairs)  39.8 us
    all_to_all x1, starting transfers between devices, on_device(): mine = lax.all_to_all(outgoing, 'sub', 0, 0, tiled=True)  36.7 us
    ppermute x6, starting transfers between devices, from_partner(): return lax.ppermute(value, axis, pairs)  27 us
    all_to_all x1, waiting for transfers between devices, on_device(): mine = lax.all_to_all(outgoing, 'sub', 0, 0, tiled=True)  24.5 us
    all_to_all x1, waiting for transfers between devices, on_device(): lax.all_to_all(chip_sum.reshape(n_sub, width // n_sub, half), 'sub', 0, 0...  15.9 us
    all_to_all x1, starting transfers between devices, on_device(): lax.all_to_all(chip_sum.reshape(n_sub, width // n_sub, half), 'sub', 0, 0...  5.86 us
  transfers between devices with their start and end apart: 8, of which 4 were waited for; matrix products, arithmetic and copies ran while one was open for 7% of the time, Pallas kernels for 0%

profile of v5, /device:TPU:1, one launch (start us, length us, event | category | flops | bytes accessed | tf_op | source)
XLA Modules:
  0.0 176.2 jit_solution(7160458029615902937)
XLA Ops:
  0.6 0.8 eq.22
  1.5 0.6 copy-done
  2.1 1.0 fusion.5
  3.1 0.2 copy-done.6
  3.3 1.2 fusion.8
  4.5 8.4 %collective-permute-start.1 = (bf16[1024,512]{1,0:T(8,128)(2,1)S(1)}, bf16[1024,512]{1,0:T(8,128)(2,1)S(1)}, u32[]{:S(2)}, u32[]{:S(2)}) collective-permute-start(bf16[1024,512]{1,0:T(8,128)(2,1)S(1)} %fusion.8), channel_id=1, source_target_pairs={{0,64},{64,0},{128,192},{192,128},{256,320},{320,256},{384,448},{4... | collective-permute-start | bytes 3145736 | tf_op jit(solution)/shard_map/ppermute | solution.py:12
  13.0 3.1 %collective-permute-start = (bf16[1,1040,128]{2,1,0:T(8,128)(2,1)S(1)}, bf16[1,1040,128]{2,1,0:T(8,128)(2,1)S(1)}, u32[]{:S(2)}, u32[]{:S(2)}) collective-permute-start(bf16[1,1040,128]{2,1,0:T(8,128)(2,1)S(1)} %fusion.24), channel_id=1, source_target_pairs={{0,128},{64,192},{128,0},{192,64},{256,384},{320,448},{384,256},{4... | collective-permute-start | bytes 798728 | tf_op jit(solution)/shard_map/ppermute | solution.py:12
  16.1 30.8 %collective-permute-done.1 = bf16[1024,512]{1,0:T(8,128)(2,1)S(1)} collective-permute-done((bf16[1024,512]{1,0:T(8,128)(2,1)S(1)}, bf16[1024,512]{1,0:T(8,128)(2,1)S(1)}, u32[]{:S(2)}, u32[]{:S(2)}) %collective-permute-start.1) | collective-permute-done | bytes 1048608 | tf_op jit(solution)/shard_map/ppermute | solution.py:12
  46.9 0.3 add_convert_fusion.1
  47.2 0.4 convolution_convert_fusion.1
  47.7 3.6 %collective-permute-start.3 = (bf16[1024,512]{1,0:T(8,128)(2,1)S(1)}, bf16[1024,512]{1,0:T(8,128)(2,1)}, u32[]{:S(2)}, u32[]{:S(2)}) collective-permute-start(bf16[1024,512]{1,0:T(8,128)(2,1)S(1)} %bitcast.68), channel_id=1, source_target_pairs={{0,128},{64,192},{128,0},{192,64},{256,384},{320,448},{384,256},{4... | collective-permute-start | bytes 3145736 | tf_op jit(solution)/shard_map/ppermute | solution.py:12
  51.4 7.5 %collective-permute-start.2 = (bf16[2,1040,128]{2,1,0:T(8,128)(2,1)S(1)}, bf16[2,1040,128]{2,1,0:T(8,128)(2,1)}, u32[]{:S(2)}, u32[]{:S(2)}) collective-permute-start(bf16[2,1040,128]{2,1,0:T(8,128)(2,1)S(1)} %pad_maximum_fusion.1), channel_id=1, source_target_pairs={{0,64},{64,0},{128,192},{192,128},{256,320},{320,256},{384,448},{4... | collective-permute-start | bytes 1597448 | tf_op jit(solution)/shard_map/ppermute | solution.py:12
  58.9 9.0 %collective-permute-done.2 = bf16[2,1040,128]{2,1,0:T(8,128)(2,1)} collective-permute-done((bf16[2,1040,128]{2,1,0:T(8,128)(2,1)S(1)}, bf16[2,1040,128]{2,1,0:T(8,128)(2,1)}, u32[]{:S(2)}, u32[]{:S(2)}) %collective-permute-start.2) | collective-permute-done | bytes 532512 | tf_op jit(solution)/shard_map/ppermute | solution.py:12
  67.8 2.1 %pad_maximum_fusion = bf16[4,1040,128]{2,1,0:T(8,128)(2,1)} fusion(bf16[2,1040,128]{2,1,0:T(8,128)(2,1)} %collective-permute-done.2, bf16[2,1040,128]{2,1,0:T(8,128)(2,1)S(1)} %pad_maximum_fusion.1), kind=kLoop, calls=%fused_computation.20 | loop fusion | flops 532480 | bytes 2129920 | tf_op jit(solution)/shard_map/concatenate | solution.py:49
  69.9 1.5 add_convert_fusion
  71.5 0.4 convolution_convert_fusion
  71.9 1.2 tile.11
  73.2 36.7 %all-to-all-start = ((bf16[64,64,128]{2,1,0:T(8,128)(2,1)}), bf16[64,64,128]{2,1,0:T(8,128)(2,1)}, u32[]{:S(2)}, u32[]{:S(2)}) async-start(bf16[64,64,128]{2,1,0:T(8,128)(2,1)} %bitcast.72), calls=%async_computation | async-start | bytes 2097152 | tf_op jit(solution)/shard_map/all_to_all | solution.py:65
  109.9 1.7 convolution_bitcast_fusion
  111.6 2.4 %collective-permute-start.5 = (f32[512,256]{0,1:T(8,128)S(1)}, f32[512,256]{0,1:T(8,128)}, u32[]{:S(2)}, u32[]{:S(2)}) collective-permute-start(f32[512,256]{0,1:T(8,128)S(1)} %convolution_bitcast_fusion), channel_id=1, source_target_pairs={{0,1},{1,0},{2,3},{3,2},{4,5},{5,4},{6,7},{7,6},{8,9},{9,8},{10,11... | collective-permute-start | bytes 1572872 | tf_op jit(solution)/shard_map/ppermute | solution.py:12
  114.1 24.5 %all-to-all-done = bf16[64,64,128]{2,1,0:T(8,128)(2,1)} async-done(((bf16[64,64,128]{2,1,0:T(8,128)(2,1)}), bf16[64,64,128]{2,1,0:T(8,128)(2,1)}, u32[]{:S(2)}, u32[]{:S(2)}) %all-to-all-start) | async-done | bytes 1048608 | tf_op jit(solution)/shard_map/all_to_all | solution.py:65
  138.5 1.9 %collective-permute-start.4 = (bf16[64,64,128]{2,1,0:T(8,128)(2,1)}, bf16[64,64,128]{2,1,0:T(8,128)(2,1)}, u32[]{:S(2)}, u32[]{:S(2)}) collective-permute-start(bf16[64,64,128]{2,1,0:T(8,128)(2,1)} %all-to-all-done), channel_id=1, source_target_pairs={{0,1},{1,0},{2,3},{3,2},{4,5},{5,4},{6,7},{7,6},{8,9},{9,8},{10,11... | collective-permute-start | bytes 3145736 | tf_op jit(solution)/shard_map/ppermute | solution.py:12
  140.5 2.6 %fusion.11 = f32[512,256]{0,1:T(8,128)} fusion(f32[512,256]{0,1:T(8,128)} %collective-permute-done.5, bf16[1024,512]{1,0:T(8,128)(2,1)} %param.15, bf16[1024,512]{1,0:T(8,128)(2,1)S(1)} %bitcast.67, s32[]{:T(128)S(6)} %select_n.45), kind=kOutput, calls=%fused_computation.15 | convolution fusion | flops 268566528 | bytes 2621444 | tf_op jit(solution)/shard_map/dot_general | solution.py:80
  143.1 2.1 %copy.13 = f32[512,256]{1,0:T(8,128)} copy(f32[512,256]{0,1:T(8,128)} %fusion.11) | data formatting | bytes 1048576 | tf_op jit(solution)/shard_map/add | solution.py:82
  145.3 5.9 %all-to-all-start.1 = ((f32[64,8,256]{2,1,0:T(8,128)}), f32[64,8,256]{2,1,0:T(8,128)S(1)}, u32[]{:S(2)}, u32[]{:S(2)}) async-start(f32[64,8,256]{2,1,0:T(8,128)} %bitcast.75), calls=%async_computation.1 | async-start | bytes 1048576 | tf_op jit(solution)/shard_map/all_to_all | solution.py:83
  151.1 1.0 slice.41
  152.3 15.9 %all-to-all-done.1 = f32[64,8,256]{2,1,0:T(8,128)S(1)} async-done(((f32[64,8,256]{2,1,0:T(8,128)}), f32[64,8,256]{2,1,0:T(8,128)S(1)}, u32[]{:S(2)}, u32[]{:S(2)}) %all-to-all-start.1) | async-done | bytes 524320 | tf_op jit(solution)/shard_map/all_to_all | solution.py:83
  168.2 0.6 reduce_sum.9
  168.8 1.9 %gather_fusion = bf16[32,64,128]{2,1,0:T(8,128)(2,1)S(1)} fusion(bf16[64,64,128]{2,1,0:T(8,128)(2,1)} %all-to-all-done, s32[1024]{0:T(1024)S(1)} %pad_clamp_fusion), kind=kCustom, calls=%fused_computation.clone | custom fusion | bytes 1048704 | tf_op jit(solution)/shard_map/jit(_take)/gather | solution.py:67
  170.7 2.7 %gather_fusion.1 = bf16[32,64,128]{2,1,0:T(8,128)(2,1)} fusion(bf16[64,64,128]{2,1,0:T(8,128)(2,1)} %collective-permute-done.4, s32[1024]{0:T(1024)S(1)} %pad_clamp_fusion), kind=kCustom, calls=%fused_computation.1.clone | custom fusion | bytes 1048704 | tf_op jit(solution)/shard_map/jit(_take)/gather | solution.py:68
  173.4 1.8 %convolution_bitcast_fusion.2 = f32[128,128]{1,0:T(8,128)S(1)} fusion(bf16[32,128,128]{2,1,0:T(8,128)(2,1)S(1)} %bitcast.76, pred[]{:T(512)S(6)} %eq.26, bf16[32,64,128]{2,1,0:T(8,128)(2,1)S(1)} %gather_fusion, pred[32]{0:T(512)(128)(4,1)S(1)} %compare_and_fusion, bf16[32,64,128]{2,1,0:T(8,128)(2,1)} %gather_fusion.1), kind=kOutput, calls=%fused_computation.16 | convolution fusion | flops 67895296 | bytes 2162721 | tf_op jit(solution)/shard_map/kab,kbm->am/dot_general | solution.py:73
  175.2 1.0 fusion.13
  (28 shorter events, 0.3 us)
Async XLA Ops:
  0.6 1.4 copy-start
  2.1 1.2 copy-start.6
  3.3 9.7 %copy-start.7 = (s32[8]{0:T(128)S(1)}, s32[8]{0:T(128)}, u32[]{:S(2)}) copy-start(s32[8]{0:T(128)} %param.17) | copy-start | bytes 100
  3.3 9.7 %copy-start.4 = (bf16[8,128,128]{2,1,0:T(8,128)(2,1)S(1)}, bf16[8,128,128]{2,1,0:T(8,128)(2,1)}, u32[]{:S(2)}) copy-start(bf16[8,128,128]{2,1,0:T(8,128)(2,1)} %param.16) | copy-start | bytes 786436
  4.5 42.7 %copy-start.5 = (bf16[2,128,128]{2,1,0:T(8,128)(2,1)S(1)}, bf16[2,128,128]{2,1,0:T(8,128)(2,1)}, u32[]{:S(2)}) copy-start(bf16[2,128,128]{2,1,0:T(8,128)(2,1)} %param.14) | copy-start | bytes 196612
  4.5 42.4 %collective-permute-start.1 = (bf16[1024,512]{1,0:T(8,128)(2,1)S(1)}, bf16[1024,512]{1,0:T(8,128)(2,1)S(1)}, u32[]{:S(2)}, u32[]{:S(2)}) collective-permute-start(bf16[1024,512]{1,0:T(8,128)(2,1)S(1)} %fusion.8), channel_id=1, source_target_pairs={{0,64},{64,0},{128,192},{192,128},{256,320},{320,256},{384,448},{4... | collective-permute-start | bytes 3145736 | tf_op jit(solution)/shard_map/ppermute | solution.py:12
  13.0 34.2 %collective-permute-start = (bf16[1,1040,128]{2,1,0:T(8,128)(2,1)S(1)}, bf16[1,1040,128]{2,1,0:T(8,128)(2,1)S(1)}, u32[]{:S(2)}, u32[]{:S(2)}) collective-permute-start(bf16[1,1040,128]{2,1,0:T(8,128)(2,1)S(1)} %fusion.24), channel_id=1, source_target_pairs={{0,128},{64,192},{128,0},{192,64},{256,384},{320,448},{384,256},{4... | collective-permute-start | bytes 798728 | tf_op jit(solution)/shard_map/ppermute | solution.py:12
  47.7 22.3 %collective-permute-start.3 = (bf16[1024,512]{1,0:T(8,128)(2,1)S(1)}, bf16[1024,512]{1,0:T(8,128)(2,1)}, u32[]{:S(2)}, u32[]{:S(2)}) collective-permute-start(bf16[1024,512]{1,0:T(8,128)(2,1)S(1)} %bitcast.68), channel_id=1, source_target_pairs={{0,128},{64,192},{128,0},{192,64},{256,384},{320,448},{384,256},{4... | collective-permute-start | bytes 3145736 | tf_op jit(solution)/shard_map/ppermute | solution.py:12
  51.4 16.5 %collective-permute-start.2 = (bf16[2,1040,128]{2,1,0:T(8,128)(2,1)S(1)}, bf16[2,1040,128]{2,1,0:T(8,128)(2,1)}, u32[]{:S(2)}, u32[]{:S(2)}) collective-permute-start(bf16[2,1040,128]{2,1,0:T(8,128)(2,1)S(1)} %pad_maximum_fusion.1), channel_id=1, source_target_pairs={{0,64},{64,0},{128,192},{192,128},{256,320},{320,256},{384,448},{4... | collective-permute-start | bytes 1597448 | tf_op jit(solution)/shard_map/ppermute | solution.py:12
  73.2 65.4 %all-to-all-start = ((bf16[64,64,128]{2,1,0:T(8,128)(2,1)}), bf16[64,64,128]{2,1,0:T(8,128)(2,1)}, u32[]{:S(2)}, u32[]{:S(2)}) async-start(bf16[64,64,128]{2,1,0:T(8,128)(2,1)} %bitcast.72), calls=%async_computation | async-start | bytes 2097152 | tf_op jit(solution)/shard_map/all_to_all | solution.py:65
  111.6 28.9 %collective-permute-start.5 = (f32[512,256]{0,1:T(8,128)S(1)}, f32[512,256]{0,1:T(8,128)}, u32[]{:S(2)}, u32[]{:S(2)}) collective-permute-start(f32[512,256]{0,1:T(8,128)S(1)} %convolution_bitcast_fusion), channel_id=1, source_target_pairs={{0,1},{1,0},{2,3},{3,2},{4,5},{5,4},{6,7},{7,6},{8,9},{9,8},{10,11... | collective-permute-start | bytes 1572872 | tf_op jit(solution)/shard_map/ppermute | solution.py:12
  138.5 32.2 %collective-permute-start.4 = (bf16[64,64,128]{2,1,0:T(8,128)(2,1)}, bf16[64,64,128]{2,1,0:T(8,128)(2,1)}, u32[]{:S(2)}, u32[]{:S(2)}) collective-permute-start(bf16[64,64,128]{2,1,0:T(8,128)(2,1)} %all-to-all-done), channel_id=1, source_target_pairs={{0,1},{1,0},{2,3},{3,2},{4,5},{5,4},{6,7},{7,6},{8,9},{9,8},{10,11... | collective-permute-start | bytes 3145736 | tf_op jit(solution)/shard_map/ppermute | solution.py:12
  143.1 8.0 %copy-start.1 = (bf16[4,1040,128]{2,1,0:T(8,128)(2,1)S(1)}, bf16[4,1040,128]{2,1,0:T(8,128)(2,1)}, u32[]{:S(2)}) copy-start(bf16[4,1040,128]{2,1,0:T(8,128)(2,1)} %pad_maximum_fusion) | copy-start | bytes 3194884
  145.3 22.9 %all-to-all-start.1 = ((f32[64,8,256]{2,1,0:T(8,128)}), f32[64,8,256]{2,1,0:T(8,128)S(1)}, u32[]{:S(2)}, u32[]{:S(2)}) async-start(f32[64,8,256]{2,1,0:T(8,128)} %bitcast.75), calls=%async_computation.1 | async-start | bytes 1048576 | tf_op jit(solution)/shard_map/all_to_all | solution.py:83
  152.2 21.2 %copy-start.2 = (bf16[4,1024,128]{2,1,0:T(8,128)(2,1)S(1)}, bf16[4,1024,128]{2,1,0:T(8,128)(2,1)}, u32[]{:S(2)}) copy-start(bf16[4,1024,128]{2,1,0:T(8,128)(2,1)} %slice.41) | copy-start | bytes 3145732
  173.4 1.8 %copy-start.3 = (bf16[32,64,128]{2,1,0:T(8,128)(2,1)S(1)}, bf16[32,64,128]{2,1,0:T(8,128)(2,1)}, u32[]{:S(2)}) copy-start(bf16[32,64,128]{2,1,0:T(8,128)(2,1)} %gather_fusion.1) | copy-start | bytes 1572868

commit v6 on v5

--- a/solution.py
+++ b/solution.py
@@ -62,7 +62,25 @@
     vals_all = carried[:, : n_parent * block_size].reshape(-1, block_size, block_size)
     rows_all = carried[:, n_parent * block_size, :n_parent].reshape(-1).astype(jnp.int32)
     outgoing = jnp.tile(head.reshape(2, half_rows, quarter), (n_sub // 2, 1, 1))
-    mine = lax.all_to_all(outgoing, "sub", 0, 0, tiled=True)
+
+    half = width // 2
+    keep_cols = lax.dynamic_slice_in_dim(panel, core * half, half, 1)
+    send_cols = lax.dynamic_slice_in_dim(panel, (1 - core) * half, half, 1)
+    contract = (((0,), (0,)), ((), ()))
+    keep = lax.dot_general(psi, keep_cols, contract, preferred_element_type=jnp.float32)
+    send = lax.dot_general(psi, send_cols, contract, preferred_element_type=jnp.float32)
+    chip_sum = (keep + from_partner(send, "sub", 1)).reshape(n_sub, width // n_sub, half)
+    high = lax.reduce_precision(chip_sum, exponent_bits=8, mantissa_bits=7)
+    low = chip_sum - high
+    split = jnp.stack([high.astype(jnp.bfloat16), low.astype(jnp.bfloat16)], axis=1).reshape(n_sub, -1, quarter)
+    outgoing = jnp.concatenate([outgoing, split], axis=1)
+    arrived = lax.all_to_all(outgoing, "sub", 0, 0, tiled=True)
+    mine = arrived[:, :half_rows]
+    parts = arrived[:, half_rows:].reshape(n_sub, 2, width // n_sub, half).astype(jnp.float32)
+    spread = parts[:, 0] + parts[:, 1]
+    by_half = spread.reshape(n_sub // 2, 2, width // n_sub, half).sum(axis=0)
+    projected = by_half.transpose(1, 0, 2).reshape(width // n_sub, width)
+
     theirs = from_partner(mine, "sub", 1)
     picked_mine = jnp.take(mine, rows_all, axis=0)
     picked_theirs = jnp.take(theirs, rows_all, axis=0)
@@ -72,17 +90,6 @@
         "kab,kbm->am", vals_all[:, :, :half_rows], picked_low, preferred_element_type=jnp.float32
     ) + jnp.einsum("kab,kbm->am", vals_all[:, :, half_rows:], picked_high, preferred_element_type=jnp.float32)
     parent_out = parent_sum.astype(jnp.bfloat16)
-
-    half = width // 2
-    keep_cols = lax.dynamic_slice_in_dim(panel, core * half, half, 1)
-    send_cols = lax.dynamic_slice_in_dim(panel, (1 - core) * half, half, 1)
-    contract = (((0,), (0,)), ((), ()))
-    keep = lax.dot_general(psi, keep_cols, contract, preferred_element_type=jnp.float32)
-    send = lax.dot_general(psi, send_cols, contract, preferred_element_type=jnp.float32)
-    chip_sum = keep + from_partner(send, "sub", 1)
-    spread = lax.all_to_all(chip_sum.reshape(n_sub, width // n_sub, half), "sub", 0, 0, tiled=True)
-    by_half = spread.reshape(n_sub // 2, 2, width // n_sub, half).sum(axis=0)
-    projected = by_half.transpose(1, 0, 2).reshape(width // n_sub, width)
     return (parent_out, projected)
 
 

time: 179 us -> 169 us (0.944)
  waiting for transfers between devices: 80.1 us -> 73 us
  starting transfers between devices: 69.6 us -> 63.6 us
  other arithmetic: 4.68 us -> 9.04 us
    all_to_all x2 -> x1, starting transfers between devices: 42.6 us -> 23.7 us  [on_device(): arrived = lax.all_to_all(outgoing, 'sub', 0, 0, tiled=True)]
    ppermute x6, starting transfers between devices: 27 us -> 39.9 us  [from_partner(): return lax.ppermute(value, axis, pairs)]
    ppermute x6, waiting for transfers between devices: 39.8 us -> 34.4 us  [from_partner(): return lax.ppermute(value, axis, pairs)]
    add x1, local copies, waits for them, and re-layouts: 2.15 us -> 0.2 us  [on_device(): keep + from_partner(send, 'sub', 1)]
    all_to_all x2 -> x1, waiting for transfers between devices: 40.3 us -> 38.5 us  [on_device(): arrived = lax.all_to_all(outgoing, 'sub', 0, 0, tiled=True)]
  transfers between devices with their start and end apart: 8 -> 7, of which waited for: 4 -> 3; matrix products, arithmetic and copies ran while one was open for 7% -> 8% of each run, Pallas kernels for 0% -> 0%
where the time goes in v6:
time: 169 us; the launch traced here: 166 us
  waiting for transfers between devices  73 us (43%)
  starting transfers between devices  63.6 us (38%)
  local copies, waits for them, and re-layouts  10.1 us (6%)
  other arithmetic  9.04 us (5%)
  matrix products  8.94 us (5%)
    ppermute x6, starting transfers between devices, from_partner(): return lax.ppermute(value, axis, pairs)  39.9 us
    all_to_all x1, waiting for transfers between devices, on_device(): arrived = lax.all_to_all(outgoing, 'sub', 0, 0, tiled=True)  38.5 us
    ppermute x6, waiting for transfers between devices, from_partner(): return lax.ppermute(value, axis, pairs)  34.4 us
    all_to_all x1, starting transfers between devices, on_device(): arrived = lax.all_to_all(outgoing, 'sub', 0, 0, tiled=True)  23.7 us
  transfers between devices with their start and end apart: 7, of which 3 were waited for; matrix products, arithmetic and copies ran while one was open for 8% of the time, Pallas kernels for 0%

profile of v6, /device:TPU:1, one launch (start us, length us, event | category | flops | bytes accessed | tf_op | source)
XLA Modules:
  0.0 165.7 jit_solution(12495424651907942874)
XLA Ops:
  0.6 0.8 eq.22
  1.5 0.6 copy-done
  2.1 1.0 fusion.5
  3.3 1.2 fusion.8
  4.5 8.4 %collective-permute-start.1 = (bf16[1024,512]{1,0:T(8,128)(2,1)S(1)}, bf16[1024,512]{1,0:T(8,128)(2,1)S(1)}, u32[]{:S(2)}, u32[]{:S(2)}) collective-permute-start(bf16[1024,512]{1,0:T(8,128)(2,1)S(1)} %fusion.8), channel_id=1, source_target_pairs={{0,64},{64,0},{128,192},{192,128},{256,320},{320,256},{384,448},{4... | collective-permute-start | bytes 3145736 | tf_op jit(solution)/shard_map/ppermute | solution.py:12
  13.0 3.1 %collective-permute-start = (bf16[1,1040,128]{2,1,0:T(8,128)(2,1)S(1)}, bf16[1,1040,128]{2,1,0:T(8,128)(2,1)S(1)}, u32[]{:S(2)}, u32[]{:S(2)}) collective-permute-start(bf16[1,1040,128]{2,1,0:T(8,128)(2,1)S(1)} %fusion.25), channel_id=1, source_target_pairs={{0,128},{64,192},{128,0},{192,64},{256,384},{320,448},{384,256},{4... | collective-permute-start | bytes 798728 | tf_op jit(solution)/shard_map/ppermute | solution.py:12
  16.1 30.8 %collective-permute-done.1 = bf16[1024,512]{1,0:T(8,128)(2,1)S(1)} collective-permute-done((bf16[1024,512]{1,0:T(8,128)(2,1)S(1)}, bf16[1024,512]{1,0:T(8,128)(2,1)S(1)}, u32[]{:S(2)}, u32[]{:S(2)}) %collective-permute-start.1) | collective-permute-done | bytes 1048608 | tf_op jit(solution)/shard_map/ppermute | solution.py:12
  47.3 0.4 convolution_convert_fusion.1
  48.0 3.6 %collective-permute-start.3 = (bf16[1024,512]{1,0:T(8,128)(2,1)S(1)}, bf16[1024,512]{1,0:T(8,128)(2,1)}, u32[]{:S(2)}, u32[]{:S(2)}) collective-permute-start(bf16[1024,512]{1,0:T(8,128)(2,1)S(1)} %bitcast.74), channel_id=1, source_target_pairs={{0,128},{64,192},{128,0},{192,64},{256,384},{320,448},{384,256},{4... | collective-permute-start | bytes 3145736 | tf_op jit(solution)/shard_map/ppermute | solution.py:12
  51.6 1.0 pad_maximum_fusion.2
  52.6 7.6 %collective-permute-start.2 = (bf16[2,1040,128]{2,1,0:T(8,128)(2,1)S(1)}, bf16[2,1040,128]{2,1,0:T(8,128)(2,1)}, u32[]{:S(2)}, u32[]{:S(2)}) collective-permute-start(bf16[2,1040,128]{2,1,0:T(8,128)(2,1)S(1)} %pad_maximum_fusion.2), channel_id=1, source_target_pairs={{0,64},{64,0},{128,192},{192,128},{256,320},{320,256},{384,448},{4... | collective-permute-start | bytes 1597448 | tf_op jit(solution)/shard_map/ppermute | solution.py:12
  60.2 3.6 %collective-permute-done.3 = bf16[1024,512]{1,0:T(8,128)(2,1)} collective-permute-done((bf16[1024,512]{1,0:T(8,128)(2,1)S(1)}, bf16[1024,512]{1,0:T(8,128)(2,1)}, u32[]{:S(2)}, u32[]{:S(2)}) %collective-permute-start.3) | collective-permute-done | bytes 1048608 | tf_op jit(solution)/shard_map/ppermute | solution.py:12
  63.9 1.5 add_convert_fusion
  65.4 0.4 convolution_convert_fusion
  65.8 1.3 convolution_bitcast_fusion
  67.1 14.9 %collective-permute-start.4 = (f32[512,256]{0,1:T(8,128)}, f32[512,256]{0,1:T(8,128)}, u32[]{:S(2)}, u32[]{:S(2)}) collective-permute-start(f32[512,256]{0,1:T(8,128)} %convolution_bitcast_fusion), channel_id=1, source_target_pairs={{0,1},{1,0},{2,3},{3,2},{4,5},{5,4},{6,7},{7,6},{8,9},{9,8},{10,11... | collective-permute-start | bytes 1572872 | tf_op jit(solution)/shard_map/ppermute | solution.py:12
  82.0 2.2 %pad_maximum_fusion.1 = bf16[4,1040,128]{2,1,0:T(8,128)(2,1)} fusion(bf16[2,1040,128]{2,1,0:T(8,128)(2,1)} %collective-permute-done.2, bf16[2,1040,128]{2,1,0:T(8,128)(2,1)S(1)} %pad_maximum_fusion.2), kind=kLoop, calls=%fused_computation.21 | loop fusion | flops 532480 | bytes 2129920 | tf_op jit(solution)/shard_map/concatenate | solution.py:49
  84.3 1.5 fusion.11
  86.6 1.3 pad_maximum_fusion
  87.9 23.7 %all-to-all-start = ((bf16[64,96,128]{2,1,0:T(8,128)(2,1)}), bf16[64,96,128]{2,1,0:T(8,128)(2,1)S(1)}, u32[]{:S(2)}, u32[]{:S(2)}) async-start(bf16[64,96,128]{2,1,0:T(8,128)(2,1)} %pad_maximum_fusion), calls=%async_computation | async-start | bytes 3145728 | tf_op jit(solution)/shard_map/all_to_all | solution.py:77
  111.6 0.7 convert_reduce_fusion
  112.4 38.5 %all-to-all-done = bf16[64,96,128]{2,1,0:T(8,128)(2,1)S(1)} async-done(((bf16[64,96,128]{2,1,0:T(8,128)(2,1)}), bf16[64,96,128]{2,1,0:T(8,128)(2,1)S(1)}, u32[]{:S(2)}, u32[]{:S(2)}) %all-to-all-start) | async-done | bytes 1572896 | tf_op jit(solution)/shard_map/all_to_all | solution.py:77
  151.0 1.2 slice.67
  152.1 2.3 %collective-permute-start.5 = (bf16[64,64,128]{2,1,0:T(8,128)(2,1)}, bf16[64,64,128]{2,1,0:T(8,128)(2,1)}, u32[]{:S(2)}, u32[]{:S(2)}) collective-permute-start(bf16[64,64,128]{2,1,0:T(8,128)(2,1)} %slice.67), channel_id=1, source_target_pairs={{0,1},{1,0},{2,3},{3,2},{4,5},{5,4},{6,7},{7,6},{8,9},{9,8},{10,11... | collective-permute-start | bytes 3145736 | tf_op jit(solution)/shard_map/ppermute | solution.py:12
  154.5 1.0 slice.53
  155.5 1.1 slice_convert_fusion
  156.7 1.5 reshape.124
  158.2 1.9 %gather_fusion = bf16[32,64,128]{2,1,0:T(8,128)(2,1)S(1)} fusion(bf16[64,64,128]{2,1,0:T(8,128)(2,1)} %slice.67, s32[1024]{0:T(1024)S(1)} %pad_clamp_fusion), kind=kCustom, calls=%fused_computation.clone | custom fusion | bytes 1048704 | tf_op jit(solution)/shard_map/jit(_take)/gather | solution.py:85
  160.1 0.6 bitcast_reduce_fusion
  160.8 1.9 %gather_fusion.1 = bf16[32,64,128]{2,1,0:T(8,128)(2,1)S(1)} fusion(bf16[64,64,128]{2,1,0:T(8,128)(2,1)} %collective-permute-done.5, s32[1024]{0:T(1024)S(1)} %pad_clamp_fusion), kind=kCustom, calls=%fused_computation.1.clone | custom fusion | bytes 1048704 | tf_op jit(solution)/shard_map/jit(_take)/gather | solution.py:86
  162.7 2.0 %convolution_bitcast_fusion.2 = f32[128,128]{1,0:T(8,128)S(1)} fusion(bf16[32,128,128]{2,1,0:T(8,128)(2,1)} %bitcast.81, pred[]{:T(512)S(6)} %eq.26, bf16[32,64,128]{2,1,0:T(8,128)(2,1)S(1)} %gather_fusion, pred[32]{0:T(512)(128)(4,1)S(1)} %compare_and_fusion, bf16[32,64,128]{2,1,0:T(8,128)(2,1)S(1)} %gather_fusion.1), kind=kOutput, calls=%fused_computation.17 | convolution fusion | flops 67895296 | bytes 2162721 | tf_op jit(solution)/shard_map/kab,kbm->am/dot_general | solution.py:91
  164.7 1.0 fusion.13
  (39 shorter events, 1.8 us)
Async XLA Ops:
  0.6 1.4 copy-start
  2.1 1.2 copy-start.8
  3.3 9.7 %copy-start.9 = (s32[8]{0:T(128)S(1)}, s32[8]{0:T(128)}, u32[]{:S(2)}) copy-start(s32[8]{0:T(128)} %param.17) | copy-start | bytes 100
  3.3 9.7 %copy-start.6 = (bf16[8,128,128]{2,1,0:T(8,128)(2,1)S(1)}, bf16[8,128,128]{2,1,0:T(8,128)(2,1)}, u32[]{:S(2)}) copy-start(bf16[8,128,128]{2,1,0:T(8,128)(2,1)} %param.16) | copy-start | bytes 786436
  4.5 42.7 %copy-start.7 = (bf16[2,128,128]{2,1,0:T(8,128)(2,1)S(1)}, bf16[2,128,128]{2,1,0:T(8,128)(2,1)}, u32[]{:S(2)}) copy-start(bf16[2,128,128]{2,1,0:T(8,128)(2,1)} %param.14) | copy-start | bytes 196612
  4.5 42.4 %collective-permute-start.1 = (bf16[1024,512]{1,0:T(8,128)(2,1)S(1)}, bf16[1024,512]{1,0:T(8,128)(2,1)S(1)}, u32[]{:S(2)}, u32[]{:S(2)}) collective-permute-start(bf16[1024,512]{1,0:T(8,128)(2,1)S(1)} %fusion.8), channel_id=1, source_target_pairs={{0,64},{64,0},{128,192},{192,128},{256,320},{320,256},{384,448},{4... | collective-permute-start | bytes 3145736 | tf_op jit(solution)/shard_map/ppermute | solution.py:12
  13.0 34.2 %collective-permute-start = (bf16[1,1040,128]{2,1,0:T(8,128)(2,1)S(1)}, bf16[1,1040,128]{2,1,0:T(8,128)(2,1)S(1)}, u32[]{:S(2)}, u32[]{:S(2)}) collective-permute-start(bf16[1,1040,128]{2,1,0:T(8,128)(2,1)S(1)} %fusion.25), channel_id=1, source_target_pairs={{0,128},{64,192},{128,0},{192,64},{256,384},{320,448},{384,256},{4... | collective-permute-start | bytes 798728 | tf_op jit(solution)/shard_map/ppermute | solution.py:12
  47.3 0.7 copy-start.5
  48.0 15.9 %collective-permute-start.3 = (bf16[1024,512]{1,0:T(8,128)(2,1)S(1)}, bf16[1024,512]{1,0:T(8,128)(2,1)}, u32[]{:S(2)}, u32[]{:S(2)}) collective-permute-start(bf16[1024,512]{1,0:T(8,128)(2,1)S(1)} %bitcast.74), channel_id=1, source_target_pairs={{0,128},{64,192},{128,0},{192,64},{256,384},{320,448},{384,256},{4... | collective-permute-start | bytes 3145736 | tf_op jit(solution)/shard_map/ppermute | solution.py:12
  52.6 13.2 %copy-start.2 = (bf16[1024,512]{1,0:T(8,128)(2,1)S(1)}, bf16[1024,512]{1,0:T(8,128)(2,1)}, u32[]{:S(2)}) copy-start(bf16[1024,512]{1,0:T(8,128)(2,1)} %param.15) | copy-start | bytes 3145732
  52.6 29.4 %collective-permute-start.2 = (bf16[2,1040,128]{2,1,0:T(8,128)(2,1)S(1)}, bf16[2,1040,128]{2,1,0:T(8,128)(2,1)}, u32[]{:S(2)}, u32[]{:S(2)}) collective-permute-start(bf16[2,1040,128]{2,1,0:T(8,128)(2,1)S(1)} %pad_maximum_fusion.2), channel_id=1, source_target_pairs={{0,64},{64,0},{128,192},{192,128},{256,320},{320,256},{384,448},{4... | collective-permute-start | bytes 1597448 | tf_op jit(solution)/shard_map/ppermute | solution.py:12
  67.1 17.2 %collective-permute-start.4 = (f32[512,256]{0,1:T(8,128)}, f32[512,256]{0,1:T(8,128)}, u32[]{:S(2)}, u32[]{:S(2)}) collective-permute-start(f32[512,256]{0,1:T(8,128)} %convolution_bitcast_fusion), channel_id=1, source_target_pairs={{0,1},{1,0},{2,3},{3,2},{4,5},{5,4},{6,7},{7,6},{8,9},{9,8},{10,11... | collective-permute-start | bytes 1572872 | tf_op jit(solution)/shard_map/ppermute | solution.py:12
  82.0 2.3 %copy-start.3 = (bf16[1024,512]{1,0:T(8,128)(2,1)S(1)}, bf16[1024,512]{1,0:T(8,128)(2,1)}, u32[]{:S(2)}) copy-start(bf16[1024,512]{1,0:T(8,128)(2,1)} %param.15) | copy-start | bytes 3145732
  87.9 63.1 %all-to-all-start = ((bf16[64,96,128]{2,1,0:T(8,128)(2,1)}), bf16[64,96,128]{2,1,0:T(8,128)(2,1)S(1)}, u32[]{:S(2)}, u32[]{:S(2)}) async-start(bf16[64,96,128]{2,1,0:T(8,128)(2,1)} %pad_maximum_fusion), calls=%async_computation | async-start | bytes 3145728 | tf_op jit(solution)/shard_map/all_to_all | solution.py:77
  151.0 3.5 %copy-start.1 = (bf16[4,1040,128]{2,1,0:T(8,128)(2,1)S(1)}, bf16[4,1040,128]{2,1,0:T(8,128)(2,1)}, u32[]{:S(2)}) copy-start(bf16[4,1040,128]{2,1,0:T(8,128)(2,1)} %pad_maximum_fusion.1) | copy-start | bytes 3194884
  152.1 8.7 %collective-permute-start.5 = (bf16[64,64,128]{2,1,0:T(8,128)(2,1)}, bf16[64,64,128]{2,1,0:T(8,128)(2,1)}, u32[]{:S(2)}, u32[]{:S(2)}) collective-permute-start(bf16[64,64,128]{2,1,0:T(8,128)(2,1)} %slice.67), channel_id=1, source_target_pairs={{0,1},{1,0},{2,3},{3,2},{4,5},{5,4},{6,7},{7,6},{8,9},{9,8},{10,11... | collective-permute-start | bytes 3145736 | tf_op jit(solution)/shard_map/ppermute | solution.py:12
  162.7 2.0 %copy-start.4 = (bf16[4,1024,128]{2,1,0:T(8,128)(2,1)S(1)}, bf16[4,1024,128]{2,1,0:T(8,128)(2,1)}, u32[]{:S(2)}) copy-start(bf16[4,1024,128]{2,1,0:T(8,128)(2,1)} %slice.53) | copy-start | bytes 3145732

commit v7 on v6

--- a/solution.py
+++ b/solution.py
@@ -46,7 +46,10 @@
         total = (panel.astype(jnp.float32) + sibling.astype(jnp.float32)).astype(jnp.bfloat16)
         if level < levels - 1:
             arrived, total = lax.optimization_barrier((arrived, total))
-        carried = jnp.concatenate([carried, arrived], axis=0)
+        if level < levels - 1:
+            carried = jnp.concatenate([carried, arrived], axis=0)
+        else:
+            last_arrival = arrived
         mapped = jnp.einsum(
             "ab,rbm->ram",
             level_maps[level],
@@ -58,9 +61,6 @@
     half_rows = block_size // 2
     column = (group_index % merged) * quarter
     head = lax.dynamic_slice_in_dim(panel[:block_size], column, quarter, 1)
-    carried, head = lax.optimization_barrier((carried, head))
-    vals_all = carried[:, : n_parent * block_size].reshape(-1, block_size, block_size)
-    rows_all = carried[:, n_parent * block_size, :n_parent].reshape(-1).astype(jnp.int32)
     outgoing = jnp.tile(head.reshape(2, half_rows, quarter), (n_sub // 2, 1, 1))
 
     half = width // 2
@@ -74,7 +74,11 @@
     low = chip_sum - high
     split = jnp.stack([high.astype(jnp.bfloat16), low.astype(jnp.bfloat16)], axis=1).reshape(n_sub, -1, quarter)
     outgoing = jnp.concatenate([outgoing, split], axis=1)
+    last_arrival, outgoing = lax.optimization_barrier((last_arrival, outgoing))
     arrived = lax.all_to_all(outgoing, "sub", 0, 0, tiled=True)
+    carried = jnp.concatenate([carried, last_arrival], axis=0)
+    vals_all = carried[:, : n_parent * block_size].reshape(-1, block_size, block_size)
+    rows_all = carried[:, n_parent * block_size, :n_parent].reshape(-1).astype(jnp.int32)
     mine = arrived[:, :half_rows]
     parts = arrived[:, half_rows:].reshape(n_sub, 2, width // n_sub, half).astype(jnp.float32)
     spread = parts[:, 0] + parts[:, 1]

time: 169 us -> 191 us (1.13)
  waiting for transfers between devices: 73 us -> 84.8 us
  starting transfers between devices: 63.6 us -> 72 us
  local copies, waits for them, and re-layouts: 10.1 us -> 14.3 us
  other arithmetic: 9.04 us -> 6.13 us
    ppermute x6, waiting for transfers between devices: 34.4 us -> 48.7 us  [from_partner(): return lax.ppermute(value, axis, pairs)]
    all_to_all x1, starting transfers between devices: 23.7 us -> 31.6 us  [on_device(): arrived = lax.all_to_all(outgoing, 'sub', 0, 0, tiled=True)]
    all_to_all x1, waiting for transfers between devices: 38.5 us -> 36.1 us  [on_device(): arrived = lax.all_to_all(outgoing, 'sub', 0, 0, tiled=True)]
    concatenate x2 -> x1, other arithmetic: 3.21 us -> 1 us  [on_device(): carried = jnp.concatenate([carried, arrived], axis=0)]
    unnamed x20 -> x23, local copies, waits for them, and re-layouts: 1.06 us -> 3.09 us
  transfers between devices with their start and end apart: 7 -> 7, of which waited for: 3 -> 4; matrix products, arithmetic and copies ran while one was open for 8% -> 8% of each run, Pallas kernels for 0% -> 0%
where the time goes in v7:
time: 191 us; the launch traced here: 188 us
  waiting for transfers between devices  84.8 us (44%)
  starting transfers between devices  72 us (38%)
  local copies, waits for them, and re-layouts  14.3 us (7%)
  matrix products  10.1 us (5%)
  other arithmetic  6.13 us (3%)
    ppermute x6, waiting for transfers between devices, from_partner(): return lax.ppermute(value, axis, pairs)  48.7 us
    ppermute x6, starting transfers between devices, from_partner(): return lax.ppermute(value, axis, pairs)  40.4 us
    all_to_all x1, waiting for transfers between devices, on_device(): arrived = lax.all_to_all(outgoing, 'sub', 0, 0, tiled=True)  36.1 us
    all_to_all x1, starting transfers between devices, on_device(): arrived = lax.all_to_all(outgoing, 'sub', 0, 0, tiled=True)  31.6 us
  transfers between devices with their start and end apart: 7, of which 4 were waited for; matrix products, arithmetic and copies ran while one was open for 8% of the time, Pallas kernels for 0%

profile of v7, /device:TPU:1, one launch (start us, length us, event | category | flops | bytes accessed | tf_op | source)
XLA Modules:
  0.0 188.4 jit_solution(718837184102730137)
XLA Ops:
  0.6 0.8 eq.22
  2.1 1.0 fusion.5
  3.3 1.2 fusion.8
  4.5 8.4 %collective-permute-start.1 = (bf16[1024,512]{1,0:T(8,128)(2,1)S(1)}, bf16[1024,512]{1,0:T(8,128)(2,1)S(1)}, u32[]{:S(2)}, u32[]{:S(2)}) collective-permute-start(bf16[1024,512]{1,0:T(8,128)(2,1)S(1)} %fusion.8), channel_id=1, source_target_pairs={{0,64},{64,0},{128,192},{192,128},{256,320},{320,256},{384,448},{4... | collective-permute-start | bytes 3145736 | tf_op jit(solution)/shard_map/ppermute | solution.py:12
  13.0 3.1 %collective-permute-start = (bf16[1,1040,128]{2,1,0:T(8,128)(2,1)S(1)}, bf16[1,1040,128]{2,1,0:T(8,128)(2,1)S(1)}, u32[]{:S(2)}, u32[]{:S(2)}) collective-permute-start(bf16[1,1040,128]{2,1,0:T(8,128)(2,1)S(1)} %fusion.25), channel_id=1, source_target_pairs={{0,128},{64,192},{128,0},{192,64},{256,384},{320,448},{384,256},{4... | collective-permute-start | bytes 798728 | tf_op jit(solution)/shard_map/ppermute | solution.py:12
  16.1 30.8 %collective-permute-done.1 = bf16[1024,512]{1,0:T(8,128)(2,1)S(1)} collective-permute-done((bf16[1024,512]{1,0:T(8,128)(2,1)S(1)}, bf16[1024,512]{1,0:T(8,128)(2,1)S(1)}, u32[]{:S(2)}, u32[]{:S(2)}) %collective-permute-start.1) | collective-permute-done | bytes 1048608 | tf_op jit(solution)/shard_map/ppermute | solution.py:12
  48.0 3.6 %collective-permute-start.3 = (bf16[1024,512]{1,0:T(8,128)(2,1)S(1)}, bf16[1024,512]{1,0:T(8,128)(2,1)}, u32[]{:S(2)}, u32[]{:S(2)}) collective-permute-start(bf16[1024,512]{1,0:T(8,128)(2,1)S(1)} %bitcast.72), channel_id=1, source_target_pairs={{0,128},{64,192},{128,0},{192,64},{256,384},{320,448},{384,256},{4... | collective-permute-start | bytes 3145736 | tf_op jit(solution)/shard_map/ppermute | solution.py:12
  51.6 1.0 pad_maximum_fusion.1
  52.6 11.2 %collective-permute-done.3 = bf16[1024,512]{1,0:T(8,128)(2,1)} collective-permute-done((bf16[1024,512]{1,0:T(8,128)(2,1)S(1)}, bf16[1024,512]{1,0:T(8,128)(2,1)}, u32[]{:S(2)}, u32[]{:S(2)}) %collective-permute-start.3) | collective-permute-done | bytes 1048608 | tf_op jit(solution)/shard_map/ppermute | solution.py:12
  63.9 1.5 add_convert_fusion
  65.8 1.3 convolution_bitcast_fusion
  67.1 14.8 %collective-permute-start.4 = (f32[512,256]{0,1:T(8,128)}, f32[512,256]{0,1:T(8,128)}, u32[]{:S(2)}, u32[]{:S(2)}) collective-permute-start(f32[512,256]{0,1:T(8,128)} %convolution_bitcast_fusion), channel_id=1, source_target_pairs={{0,1},{1,0},{2,3},{3,2},{4,5},{5,4},{6,7},{7,6},{8,9},{9,8},{10,11... | collective-permute-start | bytes 1572872 | tf_op jit(solution)/shard_map/ppermute | solution.py:12
  82.0 8.0 %collective-permute-start.2 = (bf16[2,1040,128]{2,1,0:T(8,128)(2,1)S(1)}, bf16[2,1040,128]{2,1,0:T(8,128)(2,1)}, u32[]{:S(2)}, u32[]{:S(2)}) collective-permute-start(bf16[2,1040,128]{2,1,0:T(8,128)(2,1)S(1)} %pad_maximum_fusion.1), channel_id=1, source_target_pairs={{0,64},{64,0},{128,192},{192,128},{256,320},{320,256},{384,448},{4... | collective-permute-start | bytes 1597448 | tf_op jit(solution)/shard_map/ppermute | solution.py:12
  90.1 2.7 %fusion.11 = f32[512,256]{0,1:T(8,128)} fusion(f32[512,256]{0,1:T(8,128)} %collective-permute-done.4, bf16[1024,512]{1,0:T(8,128)(2,1)} %param.15, bf16[1024,512]{1,0:T(8,128)(2,1)S(1)} %bitcast.71, s32[]{:T(128)S(6)} %select_n.42), kind=kOutput, calls=%fused_computation.16 | convolution fusion | flops 268566528 | bytes 2621444 | tf_op jit(solution)/shard_map/dot_general | solution.py:70
  92.8 1.2 copy.21
  94.6 1.3 pad_maximum_fusion
  95.9 6.7 %collective-permute-done.2 = bf16[2,1040,128]{2,1,0:T(8,128)(2,1)} collective-permute-done((bf16[2,1040,128]{2,1,0:T(8,128)(2,1)S(1)}, bf16[2,1040,128]{2,1,0:T(8,128)(2,1)}, u32[]{:S(2)}, u32[]{:S(2)}) %collective-permute-start.2) | collective-permute-done | bytes 532512 | tf_op jit(solution)/shard_map/ppermute | solution.py:12
  102.6 31.6 %all-to-all-start = ((bf16[64,96,128]{2,1,0:T(8,128)(2,1)}), bf16[64,96,128]{2,1,0:T(8,128)(2,1)S(1)}, u32[]{:S(2)}, u32[]{:S(2)}) async-start(bf16[64,96,128]{2,1,0:T(8,128)(2,1)} %pad_maximum_fusion), calls=%async_computation | async-start | bytes 3145728 | tf_op jit(solution)/shard_map/all_to_all | solution.py:78
  134.2 1.1 constant_dynamic-update-slice_fusion.1
  135.3 1.1 constant_dynamic-update-slice_fusion
  136.5 1.0 copy-done.2
  137.5 36.1 %all-to-all-done = bf16[64,96,128]{2,1,0:T(8,128)(2,1)S(1)} async-done(((bf16[64,96,128]{2,1,0:T(8,128)(2,1)}), bf16[64,96,128]{2,1,0:T(8,128)(2,1)S(1)}, u32[]{:S(2)}, u32[]{:S(2)}) %all-to-all-start) | async-done | bytes 1572896 | tf_op jit(solution)/shard_map/all_to_all | solution.py:78
  173.6 1.1 slice.69
  174.7 2.3 %collective-permute-start.5 = (bf16[64,64,128]{2,1,0:T(8,128)(2,1)}, bf16[64,64,128]{2,1,0:T(8,128)(2,1)}, u32[]{:S(2)}, u32[]{:S(2)}) collective-permute-start(bf16[64,64,128]{2,1,0:T(8,128)(2,1)} %slice.69), channel_id=1, source_target_pairs={{0,1},{1,0},{2,3},{3,2},{4,5},{5,4},{6,7},{7,6},{8,9},{9,8},{10,11... | collective-permute-start | bytes 3145736 | tf_op jit(solution)/shard_map/ppermute | solution.py:12
  177.1 1.0 slice.66
  178.2 1.1 slice_convert_fusion
  179.3 1.5 reshape.125
  180.8 1.9 gather_fusion
  182.8 0.6 bitcast_reduce_fusion
  183.4 1.9 gather_fusion.1
  185.3 2.0 %convolution_bitcast_fusion.2 = f32[128,128]{1,0:T(8,128)S(1)} fusion(bf16[32,128,128]{2,1,0:T(8,128)(2,1)} %bitcast.79, pred[]{:T(512)S(6)} %eq.26, bf16[32,64,128]{2,1,0:T(8,128)(2,1)S(1)} %gather_fusion, pred[32]{0:T(512)(128)(4,1)S(1)} %compare_and_fusion, bf16[32,64,128]{2,1,0:T(8,128)(2,1)S(1)} %gather_fusion.1), kind=kOutput, calls=%fused_computation.17 | convolution fusion | flops 67895296 | bytes 2162721 | tf_op jit(solution)/shard_map/kab,kbm->am/dot_general | solution.py:95
  187.3 1.0 fusion.13
  (42 shorter events, 3.0 us)
Async XLA Ops:
  0.6 1.4 copy-start
  2.1 1.2 copy-start.9
  3.3 9.7 %copy-start.10 = (s32[8]{0:T(128)S(1)}, s32[8]{0:T(128)}, u32[]{:S(2)}) copy-start(s32[8]{0:T(128)} %param.17) | copy-start | bytes 100
  3.3 9.7 %copy-start.7 = (bf16[8,128,128]{2,1,0:T(8,128)(2,1)S(1)}, bf16[8,128,128]{2,1,0:T(8,128)(2,1)}, u32[]{:S(2)}) copy-start(bf16[8,128,128]{2,1,0:T(8,128)(2,1)} %param.16) | copy-start | bytes 786436
  4.5 42.7 %copy-start.8 = (bf16[2,128,128]{2,1,0:T(8,128)(2,1)S(1)}, bf16[2,128,128]{2,1,0:T(8,128)(2,1)}, u32[]{:S(2)}) copy-start(bf16[2,128,128]{2,1,0:T(8,128)(2,1)} %param.14) | copy-start | bytes 196612
  4.5 42.4 %collective-permute-start.1 = (bf16[1024,512]{1,0:T(8,128)(2,1)S(1)}, bf16[1024,512]{1,0:T(8,128)(2,1)S(1)}, u32[]{:S(2)}, u32[]{:S(2)}) collective-permute-start(bf16[1024,512]{1,0:T(8,128)(2,1)S(1)} %fusion.8), channel_id=1, source_target_pairs={{0,64},{64,0},{128,192},{192,128},{256,320},{320,256},{384,448},{4... | collective-permute-start | bytes 3145736 | tf_op jit(solution)/shard_map/ppermute | solution.py:12
  13.0 34.2 %collective-permute-start = (bf16[1,1040,128]{2,1,0:T(8,128)(2,1)S(1)}, bf16[1,1040,128]{2,1,0:T(8,128)(2,1)S(1)}, u32[]{:S(2)}, u32[]{:S(2)}) collective-permute-start(bf16[1,1040,128]{2,1,0:T(8,128)(2,1)S(1)} %fusion.25), channel_id=1, source_target_pairs={{0,128},{64,192},{128,0},{192,64},{256,384},{320,448},{384,256},{4... | collective-permute-start | bytes 798728 | tf_op jit(solution)/shard_map/ppermute | solution.py:12
  47.3 0.7 copy-start.6
  48.0 15.9 %collective-permute-start.3 = (bf16[1024,512]{1,0:T(8,128)(2,1)S(1)}, bf16[1024,512]{1,0:T(8,128)(2,1)}, u32[]{:S(2)}, u32[]{:S(2)}) collective-permute-start(bf16[1024,512]{1,0:T(8,128)(2,1)S(1)} %bitcast.72), channel_id=1, source_target_pairs={{0,128},{64,192},{128,0},{192,64},{256,384},{320,448},{384,256},{4... | collective-permute-start | bytes 3145736 | tf_op jit(solution)/shard_map/ppermute | solution.py:12
  52.6 29.4 %copy-start.4 = (bf16[2,1040,128]{2,1,0:T(8,128)(2,1)}, bf16[2,1040,128]{2,1,0:T(8,128)(2,1)S(1)}, u32[]{:S(2)}) copy-start(bf16[2,1040,128]{2,1,0:T(8,128)(2,1)S(1)} %pad_maximum_fusion.1) | copy-start | bytes 1597444
  52.6 13.2 %copy-start.1 = (bf16[1024,512]{1,0:T(8,128)(2,1)S(1)}, bf16[1024,512]{1,0:T(8,128)(2,1)}, u32[]{:S(2)}) copy-start(bf16[1024,512]{1,0:T(8,128)(2,1)} %param.15) | copy-start | bytes 3145732
  67.1 23.0 %collective-permute-start.4 = (f32[512,256]{0,1:T(8,128)}, f32[512,256]{0,1:T(8,128)}, u32[]{:S(2)}, u32[]{:S(2)}) collective-permute-start(f32[512,256]{0,1:T(8,128)} %convolution_bitcast_fusion), channel_id=1, source_target_pairs={{0,1},{1,0},{2,3},{3,2},{4,5},{5,4},{6,7},{7,6},{8,9},{9,8},{10,11... | collective-permute-start | bytes 1572872 | tf_op jit(solution)/shard_map/ppermute | solution.py:12
  82.0 20.6 %collective-permute-start.2 = (bf16[2,1040,128]{2,1,0:T(8,128)(2,1)S(1)}, bf16[2,1040,128]{2,1,0:T(8,128)(2,1)}, u32[]{:S(2)}, u32[]{:S(2)}) collective-permute-start(bf16[2,1040,128]{2,1,0:T(8,128)(2,1)S(1)} %pad_maximum_fusion.1), channel_id=1, source_target_pairs={{0,64},{64,0},{128,192},{192,128},{256,320},{320,256},{384,448},{4... | collective-permute-start | bytes 1597448 | tf_op jit(solution)/shard_map/ppermute | solution.py:12
  102.6 71.0 %all-to-all-start = ((bf16[64,96,128]{2,1,0:T(8,128)(2,1)}), bf16[64,96,128]{2,1,0:T(8,128)(2,1)S(1)}, u32[]{:S(2)}, u32[]{:S(2)}) async-start(bf16[64,96,128]{2,1,0:T(8,128)(2,1)} %pad_maximum_fusion), calls=%async_computation | async-start | bytes 3145728 | tf_op jit(solution)/shard_map/all_to_all | solution.py:78
  136.4 1.0 copy-start.2
  173.6 3.5 %copy-start.3 = (bf16[4,1040,128]{2,1,0:T(8,128)(2,1)S(1)}, bf16[4,1040,128]{2,1,0:T(8,128)(2,1)}, u32[]{:S(2)}) copy-start(bf16[4,1040,128]{2,1,0:T(8,128)(2,1)} %copy-done.2) | copy-start | bytes 3194884
  174.7 8.7 %collective-permute-start.5 = (bf16[64,64,128]{2,1,0:T(8,128)(2,1)}, bf16[64,64,128]{2,1,0:T(8,128)(2,1)}, u32[]{:S(2)}, u32[]{:S(2)}) collective-permute-start(bf16[64,64,128]{2,1,0:T(8,128)(2,1)} %slice.69), channel_id=1, source_target_pairs={{0,1},{1,0},{2,3},{3,2},{4,5},{5,4},{6,7},{7,6},{8,9},{9,8},{10,11... | collective-permute-start | bytes 3145736 | tf_op jit(solution)/shard_map/ppermute | solution.py:12
  185.3 2.0 %copy-start.5 = (bf16[4,1024,128]{2,1,0:T(8,128)(2,1)S(1)}, bf16[4,1024,128]{2,1,0:T(8,128)(2,1)}, u32[]{:S(2)}) copy-start(bf16[4,1024,128]{2,1,0:T(8,128)(2,1)} %slice.66) | copy-start | bytes 3145732

commit v8 on v6

--- a/solution.py
+++ b/solution.py
@@ -37,16 +37,19 @@
         .astype(jnp.bfloat16)
     )
     panel = jnp.dot(dense, modes, preferred_element_type=jnp.float32).astype(jnp.bfloat16)
-    carried = packed[None]
+    packed, panel = lax.optimization_barrier((packed, panel))
+    held = [packed]
     for level in range(levels):
         sibling = from_partner(panel, "group", 2**level)
-        partner = levels - 1 - level
-        carried, panel = lax.optimization_barrier((carried, panel))
-        arrived = from_partner(carried, "group", 2**partner)
+        if level == 0:
+            sent = [from_partner(packed, "group", 2**lev) for lev in range(levels)]
+        else:
+            relay, panel = lax.optimization_barrier((held[1], panel))
+            sent = [from_partner(relay, "group", 2**level)]
         total = (panel.astype(jnp.float32) + sibling.astype(jnp.float32)).astype(jnp.bfloat16)
         if level < levels - 1:
-            arrived, total = lax.optimization_barrier((arrived, total))
-        carried = jnp.concatenate([carried, arrived], axis=0)
+            sent, total = lax.optimization_barrier((sent, total))
+        held = held + sent
         mapped = jnp.einsum(
             "ab,rbm->ram",
             level_maps[level],
@@ -54,6 +57,8 @@
             preferred_element_type=jnp.float32,
         )
         panel = mapped.reshape(row_blocks * block_size, width).astype(jnp.bfloat16)
+    carried = jnp.stack(held)
+
     quarter = width // merged
     half_rows = block_size // 2
     column = (group_index % merged) * quarter

time: 169 us -> 180 us (1.065)
  waiting for transfers between devices: 73 us -> 87.7 us
    ppermute x6 -> x7, waiting for transfers between devices: 34.4 us -> 49.2 us  [from_partner(): return lax.ppermute(value, axis, pairs)]
    another operation x1 -> x2, other arithmetic: 0.01 us -> 3.09 us  [the longest x1 2.31 us: on_device(): carried = jnp.stack(held)]
    concatenate x2 -> x1, other arithmetic: 3.21 us -> 0.97 us  [on_device(): jnp.concatenate([parent_vals.reshape(n_parent * block_size, block_size),...]
    ppermute x6 -> x7, starting transfers between devices: 39.9 us -> 38.3 us  [from_partner(): return lax.ppermute(value, axis, pairs)]
  transfers between devices with their start and end apart: 7 -> 8, of which waited for: 3 -> 4; matrix products, arithmetic and copies ran while one was open for 8% -> 7% of each run, Pallas kernels for 0% -> 0%
where the time goes in v8:
time: 180 us; the launch traced here: 178 us
  waiting for transfers between devices  87.7 us (49%)
  starting transfers between devices  62.3 us (35%)
  other arithmetic  9.91 us (6%)
  local copies, waits for them, and re-layouts  9.18 us (5%)
  matrix products  8.16 us (5%)
    ppermute x7, waiting for transfers between devices, from_partner(): return lax.ppermute(value, axis, pairs)  49.2 us
    all_to_all x1, waiting for transfers between devices, on_device(): arrived = lax.all_to_all(outgoing, 'sub', 0, 0, tiled=True)  38.6 us
    ppermute x7, starting transfers between devices, from_partner(): return lax.ppermute(value, axis, pairs)  38.3 us
    all_to_all x1, starting transfers between devices, on_device(): arrived = lax.all_to_all(outgoing, 'sub', 0, 0, tiled=True)  24 us
  transfers between devices with their start and end apart: 8, of which 4 were waited for; matrix products, arithmetic and copies ran while one was open for 7% of the time, Pallas kernels for 0%

profile of v8, /device:TPU:1, one launch (start us, length us, event | category | flops | bytes accessed | tf_op | source)
XLA Modules:
  0.0 178.3 jit_solution(7388024862954966769)
XLA Ops:
  0.6 0.8 convert_bitcast_fusion
  1.4 0.7 eq.22
  2.2 1.0 fusion.24
  3.2 1.0 fusion.5
  4.4 1.2 fusion.8
  5.6 8.4 %collective-permute-start.2 = (bf16[1024,512]{1,0:T(8,128)(2,1)S(1)}, bf16[1024,512]{1,0:T(8,128)(2,1)S(1)}, u32[]{:S(2)}, u32[]{:S(2)}) collective-permute-start(bf16[1024,512]{1,0:T(8,128)(2,1)S(1)} %fusion.8), channel_id=1, source_target_pairs={{0,64},{64,0},{128,192},{192,128},{256,320},{320,256},{384,448},{4... | collective-permute-start | bytes 3145736 | tf_op jit(solution)/shard_map/ppermute | solution.py:12
  14.0 3.1 %collective-permute-start.1 = (bf16[1040,128]{1,0:T(8,128)(2,1)S(1)}, bf16[1040,128]{1,0:T(8,128)(2,1)S(1)}, u32[]{:S(2)}, u32[]{:S(2)}) collective-permute-start(bf16[1040,128]{1,0:T(8,128)(2,1)S(1)} %fusion.24), channel_id=1, source_target_pairs={{0,128},{64,192},{128,0},{192,64},{256,384},{320,448},{384,256},{4... | collective-permute-start | bytes 798728 | tf_op jit(solution)/shard_map/ppermute | solution.py:12
  17.2 1.9 %collective-permute-start = (bf16[1040,128]{1,0:T(8,128)(2,1)S(1)}, bf16[1040,128]{1,0:T(8,128)(2,1)}, u32[]{:S(2)}, u32[]{:S(2)}) collective-permute-start(bf16[1040,128]{1,0:T(8,128)(2,1)S(1)} %fusion.24), channel_id=1, source_target_pairs={{0,64},{64,0},{128,192},{192,128},{256,320},{320,256},{384,448},{4... | collective-permute-start | bytes 798728 | tf_op jit(solution)/shard_map/ppermute | solution.py:12
  19.1 28.8 %collective-permute-done.2 = bf16[1024,512]{1,0:T(8,128)(2,1)S(1)} collective-permute-done((bf16[1024,512]{1,0:T(8,128)(2,1)S(1)}, bf16[1024,512]{1,0:T(8,128)(2,1)S(1)}, u32[]{:S(2)}, u32[]{:S(2)}) %collective-permute-start.2) | collective-permute-done | bytes 1048608 | tf_op jit(solution)/shard_map/ppermute | solution.py:12
  48.2 10.1 %collective-permute-done = bf16[1040,128]{1,0:T(8,128)(2,1)} collective-permute-done((bf16[1040,128]{1,0:T(8,128)(2,1)S(1)}, bf16[1040,128]{1,0:T(8,128)(2,1)}, u32[]{:S(2)}, u32[]{:S(2)}) %collective-permute-start) | collective-permute-done | bytes 266272 | tf_op jit(solution)/shard_map/ppermute | solution.py:12
  58.8 3.8 %collective-permute-start.4 = (bf16[1024,512]{1,0:T(8,128)(2,1)S(1)}, bf16[1024,512]{1,0:T(8,128)(2,1)}, u32[]{:S(2)}, u32[]{:S(2)}) collective-permute-start(bf16[1024,512]{1,0:T(8,128)(2,1)S(1)} %bitcast.76), channel_id=1, source_target_pairs={{0,128},{64,192},{128,0},{192,64},{256,384},{320,448},{384,256},{4... | collective-permute-start | bytes 3145736 | tf_op jit(solution)/shard_map/ppermute | solution.py:12
  62.6 2.1 %collective-permute-start.3 = (bf16[1040,128]{1,0:T(8,128)(2,1)}, bf16[1040,128]{1,0:T(8,128)(2,1)}, u32[]{:S(2)}, u32[]{:S(2)}) collective-permute-start(bf16[1040,128]{1,0:T(8,128)(2,1)} %collective-permute-done), channel_id=1, source_target_pairs={{0,128},{64,192},{128,0},{192,64},{256,384},{320,448},{384,256},{4... | collective-permute-start | bytes 798728 | tf_op jit(solution)/shard_map/ppermute | solution.py:12
  64.7 10.2 %collective-permute-done.4 = bf16[1024,512]{1,0:T(8,128)(2,1)} collective-permute-done((bf16[1024,512]{1,0:T(8,128)(2,1)S(1)}, bf16[1024,512]{1,0:T(8,128)(2,1)}, u32[]{:S(2)}, u32[]{:S(2)}) %collective-permute-start.4) | collective-permute-done | bytes 1048608 | tf_op jit(solution)/shard_map/ppermute | solution.py:12
  74.9 1.6 add_convert_fusion
  76.9 0.5 convolution_bitcast_fusion
  77.4 16.7 %collective-permute-start.5 = (f32[512,256]{0,1:T(8,128)S(1)}, f32[512,256]{0,1:T(8,128)}, u32[]{:S(2)}, u32[]{:S(2)}) collective-permute-start(f32[512,256]{0,1:T(8,128)S(1)} %convolution_bitcast_fusion), channel_id=1, source_target_pairs={{0,1},{1,0},{2,3},{3,2},{4,5},{5,4},{6,7},{7,6},{8,9},{9,8},{10,11... | collective-permute-start | bytes 1572872 | tf_op jit(solution)/shard_map/ppermute | solution.py:12
  94.1 2.3 %pad_maximum_fusion.1 = bf16[4,1040,128]{2,1,0:T(8,128)(2,1)} fusion(bf16[1,1040,128]{2,1,0:T(8,128)(2,1)} %bitcast.14, bf16[1,1040,128]{2,1,0:T(8,128)(2,1)} %bitcast.86, bf16[1,1040,128]{2,1,0:T(8,128)(2,1)} %bitcast.7, bf16[1,1040,128]{2,1,0:T(8,128)(2,1)S(1)} %bitcast.83), kind=kLoop, calls=%fused_computation.21 | loop fusion | flops 1597440 | bytes 2129920 | tf_op jit(solution)/shard_map/stack | solution.py:60
  96.5 1.5 fusion.11
  98.8 1.3 pad_maximum_fusion
  100.1 24.0 %all-to-all-start = ((bf16[64,96,128]{2,1,0:T(8,128)(2,1)}), bf16[64,96,128]{2,1,0:T(8,128)(2,1)S(1)}, u32[]{:S(2)}, u32[]{:S(2)}) async-start(bf16[64,96,128]{2,1,0:T(8,128)(2,1)} %pad_maximum_fusion), calls=%async_computation | async-start | bytes 3145728 | tf_op jit(solution)/shard_map/all_to_all | solution.py:82
  124.1 0.7 convert_reduce_fusion
  124.9 38.6 %all-to-all-done = bf16[64,96,128]{2,1,0:T(8,128)(2,1)S(1)} async-done(((bf16[64,96,128]{2,1,0:T(8,128)(2,1)}), bf16[64,96,128]{2,1,0:T(8,128)(2,1)S(1)}, u32[]{:S(2)}, u32[]{:S(2)}) %all-to-all-start) | async-done | bytes 1572896 | tf_op jit(solution)/shard_map/all_to_all | solution.py:82
  163.5 1.2 slice.67
  164.6 2.3 %collective-permute-start.6 = (bf16[64,64,128]{2,1,0:T(8,128)(2,1)}, bf16[64,64,128]{2,1,0:T(8,128)(2,1)}, u32[]{:S(2)}, u32[]{:S(2)}) collective-permute-start(bf16[64,64,128]{2,1,0:T(8,128)(2,1)} %slice.67), channel_id=1, source_target_pairs={{0,1},{1,0},{2,3},{3,2},{4,5},{5,4},{6,7},{7,6},{8,9},{9,8},{10,11... | collective-permute-start | bytes 3145736 | tf_op jit(solution)/shard_map/ppermute | solution.py:12
  167.0 1.0 slice.53
  168.0 1.1 slice_convert_fusion
  169.2 1.5 reshape.124
  170.7 1.9 %gather_fusion = bf16[32,64,128]{2,1,0:T(8,128)(2,1)S(1)} fusion(bf16[64,64,128]{2,1,0:T(8,128)(2,1)} %slice.67, s32[1024]{0:T(1024)S(1)} %pad_clamp_fusion), kind=kCustom, calls=%fused_computation.clone | custom fusion | bytes 1048704 | tf_op jit(solution)/shard_map/jit(_take)/gather | solution.py:90
  172.7 0.6 bitcast_reduce_fusion
  173.3 1.9 %gather_fusion.1 = bf16[32,64,128]{2,1,0:T(8,128)(2,1)S(1)} fusion(bf16[64,64,128]{2,1,0:T(8,128)(2,1)} %collective-permute-done.6, s32[1024]{0:T(1024)S(1)} %pad_clamp_fusion), kind=kCustom, calls=%fused_computation.1.clone | custom fusion | bytes 1048704 | tf_op jit(solution)/shard_map/jit(_take)/gather | solution.py:91
  175.2 2.0 %convolution_bitcast_fusion.2 = f32[128,128]{1,0:T(8,128)S(1)} fusion(bf16[32,128,128]{2,1,0:T(8,128)(2,1)} %bitcast.84, pred[]{:T(512)S(6)} %eq.26, bf16[32,64,128]{2,1,0:T(8,128)(2,1)S(1)} %gather_fusion, pred[32]{0:T(512)(128)(4,1)S(1)} %compare_and_fusion, bf16[32,64,128]{2,1,0:T(8,128)(2,1)S(1)} %gather_fusion.1), kind=kOutput, calls=%fused_computation.17 | convolution fusion | flops 67895296 | bytes 2162721 | tf_op jit(solution)/shard_map/kab,kbm->am/dot_general | solution.py:96
  177.2 1.1 fusion.13
  (36 shorter events, 2.3 us)
Async XLA Ops:
  0.6 2.5 %copy-start = (bf16[48,128,128]{2,1,0:T(8,128)(2,1)S(1)}, bf16[48,128,128]{2,1,0:T(8,128)(2,1)}, u32[]{:S(2)}) copy-start(bf16[48,128,128]{2,1,0:T(8,128)(2,1)} %param.12) | copy-start | bytes 4718596
  3.1 1.2 copy-start.7
  5.6 52.8 %copy-start.6 = (bf16[2,128,128]{2,1,0:T(8,128)(2,1)S(1)}, bf16[2,128,128]{2,1,0:T(8,128)(2,1)}, u32[]{:S(2)}) copy-start(bf16[2,128,128]{2,1,0:T(8,128)(2,1)} %param.14) | copy-start | bytes 196612
  5.6 42.3 %collective-permute-start.2 = (bf16[1024,512]{1,0:T(8,128)(2,1)S(1)}, bf16[1024,512]{1,0:T(8,128)(2,1)S(1)}, u32[]{:S(2)}, u32[]{:S(2)}) collective-permute-start(bf16[1024,512]{1,0:T(8,128)(2,1)S(1)} %fusion.8), channel_id=1, source_target_pairs={{0,64},{64,0},{128,192},{192,128},{256,320},{320,256},{384,448},{4... | collective-permute-start | bytes 3145736 | tf_op jit(solution)/shard_map/ppermute | solution.py:12
  14.0 34.2 %collective-permute-start.1 = (bf16[1040,128]{1,0:T(8,128)(2,1)S(1)}, bf16[1040,128]{1,0:T(8,128)(2,1)S(1)}, u32[]{:S(2)}, u32[]{:S(2)}) collective-permute-start(bf16[1040,128]{1,0:T(8,128)(2,1)S(1)} %fusion.24), channel_id=1, source_target_pairs={{0,128},{64,192},{128,0},{192,64},{256,384},{320,448},{384,256},{4... | collective-permute-start | bytes 798728 | tf_op jit(solution)/shard_map/ppermute | solution.py:12
  17.2 41.2 %collective-permute-start = (bf16[1040,128]{1,0:T(8,128)(2,1)S(1)}, bf16[1040,128]{1,0:T(8,128)(2,1)}, u32[]{:S(2)}, u32[]{:S(2)}) collective-permute-start(bf16[1040,128]{1,0:T(8,128)(2,1)S(1)} %fusion.24), channel_id=1, source_target_pairs={{0,64},{64,0},{128,192},{192,128},{256,320},{320,256},{384,448},{4... | collective-permute-start | bytes 798728 | tf_op jit(solution)/shard_map/ppermute | solution.py:12
  48.2 10.6 %copy-start.5 = (bf16[1040,128]{1,0:T(8,128)(2,1)}, bf16[1040,128]{1,0:T(8,128)(2,1)S(1)}, u32[]{:S(2)}) copy-start(bf16[1040,128]{1,0:T(8,128)(2,1)S(1)} %collective-permute-done.1) | copy-start | bytes 798724
  58.8 16.1 %collective-permute-start.4 = (bf16[1024,512]{1,0:T(8,128)(2,1)S(1)}, bf16[1024,512]{1,0:T(8,128)(2,1)}, u32[]{:S(2)}, u32[]{:S(2)}) collective-permute-start(bf16[1024,512]{1,0:T(8,128)(2,1)S(1)} %bitcast.76), channel_id=1, source_target_pairs={{0,128},{64,192},{128,0},{192,64},{256,384},{320,448},{384,256},{4... | collective-permute-start | bytes 3145736 | tf_op jit(solution)/shard_map/ppermute | solution.py:12
  62.6 14.3 %copy-start.2 = (bf16[1024,512]{1,0:T(8,128)(2,1)S(1)}, bf16[1024,512]{1,0:T(8,128)(2,1)}, u32[]{:S(2)}) copy-start(bf16[1024,512]{1,0:T(8,128)(2,1)} %param.15) | copy-start | bytes 3145732
  62.6 31.5 %collective-permute-start.3 = (bf16[1040,128]{1,0:T(8,128)(2,1)}, bf16[1040,128]{1,0:T(8,128)(2,1)}, u32[]{:S(2)}, u32[]{:S(2)}) collective-permute-start(bf16[1040,128]{1,0:T(8,128)(2,1)} %collective-permute-done), channel_id=1, source_target_pairs={{0,128},{64,192},{128,0},{192,64},{256,384},{320,448},{384,256},{4... | collective-permute-start | bytes 798728 | tf_op jit(solution)/shard_map/ppermute | solution.py:12
  77.4 19.1 %collective-permute-start.5 = (f32[512,256]{0,1:T(8,128)S(1)}, f32[512,256]{0,1:T(8,128)}, u32[]{:S(2)}, u32[]{:S(2)}) collective-permute-start(f32[512,256]{0,1:T(8,128)S(1)} %convolution_bitcast_fusion), channel_id=1, source_target_pairs={{0,1},{1,0},{2,3},{3,2},{4,5},{5,4},{6,7},{7,6},{8,9},{9,8},{10,11... | collective-permute-start | bytes 1572872 | tf_op jit(solution)/shard_map/ppermute | solution.py:12
  94.1 2.4 %copy-start.3 = (bf16[1024,512]{1,0:T(8,128)(2,1)S(1)}, bf16[1024,512]{1,0:T(8,128)(2,1)}, u32[]{:S(2)}) copy-start(bf16[1024,512]{1,0:T(8,128)(2,1)} %param.15) | copy-start | bytes 3145732
  100.1 63.4 %all-to-all-start = ((bf16[64,96,128]{2,1,0:T(8,128)(2,1)}), bf16[64,96,128]{2,1,0:T(8,128)(2,1)S(1)}, u32[]{:S(2)}, u32[]{:S(2)}) async-start(bf16[64,96,128]{2,1,0:T(8,128)(2,1)} %pad_maximum_fusion), calls=%async_computation | async-start | bytes 3145728 | tf_op jit(solution)/shard_map/all_to_all | solution.py:82
  163.5 3.5 %copy-start.1 = (bf16[4,1040,128]{2,1,0:T(8,128)(2,1)S(1)}, bf16[4,1040,128]{2,1,0:T(8,128)(2,1)}, u32[]{:S(2)}) copy-start(bf16[4,1040,128]{2,1,0:T(8,128)(2,1)} %pad_maximum_fusion.1) | copy-start | bytes 3194884
  164.6 8.7 %collective-permute-start.6 = (bf16[64,64,128]{2,1,0:T(8,128)(2,1)}, bf16[64,64,128]{2,1,0:T(8,128)(2,1)}, u32[]{:S(2)}, u32[]{:S(2)}) collective-permute-start(bf16[64,64,128]{2,1,0:T(8,128)(2,1)} %slice.67), channel_id=1, source_target_pairs={{0,1},{1,0},{2,3},{3,2},{4,5},{5,4},{6,7},{7,6},{8,9},{9,8},{10,11... | collective-permute-start | bytes 3145736 | tf_op jit(solution)/shard_map/ppermute | solution.py:12
  175.2 2.0 %copy-start.4 = (bf16[4,1024,128]{2,1,0:T(8,128)(2,1)S(1)}, bf16[4,1024,128]{2,1,0:T(8,128)(2,1)}, u32[]{:S(2)}) copy-start(bf16[4,1024,128]{2,1,0:T(8,128)(2,1)} %slice.53) | copy-start | bytes 3145732

commit v9 on v6

--- a/solution.py
+++ b/solution.py
@@ -69,17 +69,21 @@
     contract = (((0,), (0,)), ((), ()))
     keep = lax.dot_general(psi, keep_cols, contract, preferred_element_type=jnp.float32)
     send = lax.dot_general(psi, send_cols, contract, preferred_element_type=jnp.float32)
-    chip_sum = (keep + from_partner(send, "sub", 1)).reshape(n_sub, width // n_sub, half)
-    high = lax.reduce_precision(chip_sum, exponent_bits=8, mantissa_bits=7)
-    low = chip_sum - high
-    split = jnp.stack([high.astype(jnp.bfloat16), low.astype(jnp.bfloat16)], axis=1).reshape(n_sub, -1, quarter)
-    outgoing = jnp.concatenate([outgoing, split], axis=1)
+    chip_sum = keep + from_partner(send, "sub", 1)
+    lanes = 128
+    tiles = half // lanes
+    out_rows = width // n_sub
+    col_tiles = [chip_sum[:, i * lanes : (i + 1) * lanes].reshape(n_sub, out_rows, lanes) for i in range(tiles)]
+    highs = [lax.reduce_precision(t, exponent_bits=8, mantissa_bits=7) for t in col_tiles]
+    lows = [t - h for t, h in zip(col_tiles, highs)]
+    split = jnp.concatenate([h.astype(jnp.bfloat16) for h in highs] + [l.astype(jnp.bfloat16) for l in lows], axis=1)
+    outgoing = jnp.concatenate([outgoing, split.reshape(n_sub, -1, quarter)], axis=1)
     arrived = lax.all_to_all(outgoing, "sub", 0, 0, tiled=True)
     mine = arrived[:, :half_rows]
-    parts = arrived[:, half_rows:].reshape(n_sub, 2, width // n_sub, half).astype(jnp.float32)
-    spread = parts[:, 0] + parts[:, 1]
-    by_half = spread.reshape(n_sub // 2, 2, width // n_sub, half).sum(axis=0)
-    projected = by_half.transpose(1, 0, 2).reshape(width // n_sub, width)
+    parts = arrived[:, half_rows:].astype(jnp.float32).reshape(n_sub, 2 * tiles, out_rows, lanes)
+    spread = parts[:, :tiles] + parts[:, tiles:]
+    by_half = spread.reshape(n_sub // 2, 2, tiles, out_rows, lanes).sum(axis=0)
+    projected = by_half.transpose(2, 0, 1, 3).reshape(out_rows, width)
 
     theirs = from_partner(mine, "sub", 1)
     picked_mine = jnp.take(mine, rows_all, axis=0)

time: 169 us -> 164 us (0.970); the launches traced: 166 us -> 163 us
  local copies, waits for them, and re-layouts: 10.1 us -> 12.2 us
  matrix products: 8.94 us -> 6.89 us
    all_to_all x1, waiting for transfers between devices: 38.5 us -> 36.3 us  [on_device(): arrived = lax.all_to_all(outgoing, 'sub', 0, 0, tiled=True)]
    unnamed x0 -> x3, other arithmetic: none -> 2.12 us
    concatenate x2, other arithmetic: 3.21 us -> 1.14 us  [on_device(): carried = jnp.concatenate([carried, arrived], axis=0)]
    unnamed x20 -> x17, local copies, waits for them, and re-layouts: 1.06 us -> 2.8 us
  transfers between devices with their start and end apart: 7 -> 7, of which waited for: 3 -> 3; matrix products, arithmetic and copies ran while one was open for 8% -> 7% of each run, Pallas kernels for 0% -> 0%
where the time goes in v9:
time: 164 us; the launch traced here: 163 us
  waiting for transfers between devices  71.6 us (44%)
  starting transfers between devices  63.5 us (39%)
  local copies, waits for them, and re-layouts  12.2 us (7%)
  other arithmetic  7.42 us (5%)
  matrix products  6.89 us (4%)
    ppermute x6, starting transfers between devices, from_partner(): return lax.ppermute(value, axis, pairs)  39.8 us
    all_to_all x1, waiting for transfers between devices, on_device(): arrived = lax.all_to_all(outgoing, 'sub', 0, 0, tiled=True)  36.3 us
    ppermute x6, waiting for transfers between devices, from_partner(): return lax.ppermute(value, axis, pairs)  35.4 us
    all_to_all x1, starting transfers between devices, on_device(): arrived = lax.all_to_all(outgoing, 'sub', 0, 0, tiled=True)  23.6 us
  transfers between devices with their start and end apart: 7, of which 3 were waited for; matrix products, arithmetic and copies ran while one was open for 7% of the time, Pallas kernels for 0%

profile of v9, /device:TPU:1, one launch (start us, length us, event | category | flops | bytes accessed | tf_op | source)
XLA Modules:
  0.0 162.6 jit_solution(16743685206493216635)
XLA Ops:
  0.6 0.8 eq.22
  1.5 0.6 copy-done
  2.1 1.0 fusion.5
  3.3 1.2 fusion.8
  4.5 8.3 %collective-permute-start.1 = (bf16[1024,512]{1,0:T(8,128)(2,1)S(1)}, bf16[1024,512]{1,0:T(8,128)(2,1)S(1)}, u32[]{:S(2)}, u32[]{:S(2)}) collective-permute-start(bf16[1024,512]{1,0:T(8,128)(2,1)S(1)} %fusion.8), channel_id=1, source_target_pairs={{0,64},{64,0},{128,192},{192,128},{256,320},{320,256},{384,448},{4... | collective-permute-start | bytes 3145736 | tf_op jit(solution)/shard_map/ppermute | solution.py:12
  12.9 3.2 %collective-permute-start = (bf16[1,1040,128]{2,1,0:T(8,128)(2,1)S(1)}, bf16[1,1040,128]{2,1,0:T(8,128)(2,1)S(1)}, u32[]{:S(2)}, u32[]{:S(2)}) collective-permute-start(bf16[1,1040,128]{2,1,0:T(8,128)(2,1)S(1)} %fusion.25), channel_id=1, source_target_pairs={{0,128},{64,192},{128,0},{192,64},{256,384},{320,448},{384,256},{4... | collective-permute-start | bytes 798728 | tf_op jit(solution)/shard_map/ppermute | solution.py:12
  16.1 30.6 %collective-permute-done.1 = bf16[1024,512]{1,0:T(8,128)(2,1)S(1)} collective-permute-done((bf16[1024,512]{1,0:T(8,128)(2,1)S(1)}, bf16[1024,512]{1,0:T(8,128)(2,1)S(1)}, u32[]{:S(2)}, u32[]{:S(2)}) %collective-permute-start.1) | collective-permute-done | bytes 1048608 | tf_op jit(solution)/shard_map/ppermute | solution.py:12
  47.5 3.6 %collective-permute-start.3 = (bf16[1024,512]{1,0:T(8,128)(2,1)S(1)}, bf16[1024,512]{1,0:T(8,128)(2,1)}, u32[]{:S(2)}, u32[]{:S(2)}) collective-permute-start(bf16[1024,512]{1,0:T(8,128)(2,1)S(1)} %bitcast.86), channel_id=1, source_target_pairs={{0,128},{64,192},{128,0},{192,64},{256,384},{320,448},{384,256},{4... | collective-permute-start | bytes 3145736 | tf_op jit(solution)/shard_map/ppermute | solution.py:12
  51.3 7.5 %collective-permute-start.2 = (bf16[2,1040,128]{2,1,0:T(8,128)(2,1)S(1)}, bf16[2,1040,128]{2,1,0:T(8,128)(2,1)S(1)}, u32[]{:S(2)}, u32[]{:S(2)}) collective-permute-start(bf16[2,1040,128]{2,1,0:T(8,128)(2,1)S(1)} %pad_maximum_fusion.1), channel_id=1, source_target_pairs={{0,64},{64,0},{128,192},{192,128},{256,320},{320,256},{384,448},{4... | collective-permute-start | bytes 1597448 | tf_op jit(solution)/shard_map/ppermute | solution.py:12
  58.8 4.7 %collective-permute-done.3 = bf16[1024,512]{1,0:T(8,128)(2,1)} collective-permute-done((bf16[1024,512]{1,0:T(8,128)(2,1)S(1)}, bf16[1024,512]{1,0:T(8,128)(2,1)}, u32[]{:S(2)}, u32[]{:S(2)}) %collective-permute-start.3) | collective-permute-done | bytes 1048608 | tf_op jit(solution)/shard_map/ppermute | solution.py:12
  63.5 1.5 add_convert_fusion
  65.4 0.8 copy-done.1
  66.2 0.5 convolution_bitcast_fusion
  66.7 14.9 %collective-permute-start.4 = (f32[512,256]{0,1:T(8,128)S(1)}, f32[512,256]{0,1:T(8,128)S(1)}, u32[]{:S(2)}, u32[]{:S(2)}) collective-permute-start(f32[512,256]{0,1:T(8,128)S(1)} %convolution_bitcast_fusion), channel_id=1, source_target_pairs={{0,1},{1,0},{2,3},{3,2},{4,5},{5,4},{6,7},{7,6},{8,9},{9,8},{10,11... | collective-permute-start | bytes 1572872 | tf_op jit(solution)/shard_map/ppermute | solution.py:12
  81.6 1.1 pad_maximum_fusion
  83.0 1.2 constant_dynamic-update-slice_fusion
  84.2 0.5 fusion.11
  85.0 0.7 fusion.30
  85.7 0.7 fusion.31
  86.4 0.7 fusion.29
  87.1 0.7 fusion.28
  87.8 23.6 %all-to-all-start = ((bf16[64,96,128]{2,1,0:T(8,128)(2,1)}), bf16[64,96,128]{2,1,0:T(8,128)(2,1)S(1)}, u32[]{:S(2)}, u32[]{:S(2)}) async-start(bf16[64,96,128]{2,1,0:T(8,128)(2,1)} %fusion.28), calls=%async_computation | async-start | bytes 3145728 | tf_op jit(solution)/shard_map/all_to_all | solution.py:81
  111.5 2.3 %slice.59 = bf16[4,1024,128]{2,1,0:T(8,128)(2,1)} slice(bf16[4,1040,128]{2,1,0:T(8,128)(2,1)} %pad_maximum_fusion), slice={[0:4], [0:1024], [0:128]} | slice | bytes 2097152 | tf_op jit(solution)/shard_map/slice | solution.py:62
  113.8 0.7 convert_reduce_fusion
  114.6 36.3 %all-to-all-done = bf16[64,96,128]{2,1,0:T(8,128)(2,1)S(1)} async-done(((bf16[64,96,128]{2,1,0:T(8,128)(2,1)}), bf16[64,96,128]{2,1,0:T(8,128)(2,1)S(1)}, u32[]{:S(2)}, u32[]{:S(2)}) %all-to-all-start) | async-done | bytes 1572896 | tf_op jit(solution)/shard_map/all_to_all | solution.py:81
  150.9 1.1 slice.77
  152.0 2.3 %collective-permute-start.5 = (bf16[64,64,128]{2,1,0:T(8,128)(2,1)}, bf16[64,64,128]{2,1,0:T(8,128)(2,1)}, u32[]{:S(2)}, u32[]{:S(2)}) collective-permute-start(bf16[64,64,128]{2,1,0:T(8,128)(2,1)} %slice.77), channel_id=1, source_target_pairs={{0,1},{1,0},{2,3},{3,2},{4,5},{5,4},{6,7},{7,6},{8,9},{9,8},{10,11... | collective-permute-start | bytes 3145736 | tf_op jit(solution)/shard_map/ppermute | solution.py:12
  154.4 2.6 %gather_fusion = bf16[32,64,128]{2,1,0:T(8,128)(2,1)} fusion(bf16[64,64,128]{2,1,0:T(8,128)(2,1)} %slice.77, s32[1024]{0:T(1024)S(1)} %pad_clamp_fusion), kind=kCustom, calls=%fused_computation.clone | custom fusion | bytes 1048704 | tf_op jit(solution)/shard_map/jit(_take)/gather | solution.py:89
  157.2 0.7 reduce_sum.9
  157.9 1.9 %gather_fusion.1 = bf16[32,64,128]{2,1,0:T(8,128)(2,1)S(1)} fusion(bf16[64,64,128]{2,1,0:T(8,128)(2,1)} %collective-permute-done.5, s32[1024]{0:T(1024)S(1)} %pad_clamp_fusion), kind=kCustom, calls=%fused_computation.1.clone | custom fusion | bytes 1048704 | tf_op jit(solution)/shard_map/jit(_take)/gather | solution.py:90
  159.8 1.8 %convolution_bitcast_fusion.2 = f32[128,128]{1,0:T(8,128)S(1)} fusion(bf16[32,128,128]{2,1,0:T(8,128)(2,1)S(1)} %bitcast.93, pred[]{:T(512)S(6)} %eq.26, bf16[32,64,128]{2,1,0:T(8,128)(2,1)} %gather_fusion, pred[32]{0:T(512)(128)(4,1)S(1)} %compare_and_fusion, bf16[32,64,128]{2,1,0:T(8,128)(2,1)S(1)} %gather_fusion.1), kind=kOutput, calls=%fused_computation.16 | convolution fusion | flops 67895296 | bytes 2162721 | tf_op jit(solution)/shard_map/kab,kbm->am/dot_general | solution.py:95
  161.6 1.0 fusion.13
  (36 shorter events, 2.3 us)
Async XLA Ops:
  0.6 1.4 copy-start
  2.1 1.2 copy-start.6
  3.3 9.5 %copy-start.7 = (s32[8]{0:T(128)S(1)}, s32[8]{0:T(128)}, u32[]{:S(2)}) copy-start(s32[8]{0:T(128)} %param.17) | copy-start | bytes 100
  3.3 9.6 %copy-start.4 = (bf16[8,128,128]{2,1,0:T(8,128)(2,1)S(1)}, bf16[8,128,128]{2,1,0:T(8,128)(2,1)}, u32[]{:S(2)}) copy-start(bf16[8,128,128]{2,1,0:T(8,128)(2,1)} %param.16) | copy-start | bytes 786436
  4.5 42.2 %collective-permute-start.1 = (bf16[1024,512]{1,0:T(8,128)(2,1)S(1)}, bf16[1024,512]{1,0:T(8,128)(2,1)S(1)}, u32[]{:S(2)}, u32[]{:S(2)}) collective-permute-start(bf16[1024,512]{1,0:T(8,128)(2,1)S(1)} %fusion.8), channel_id=1, source_target_pairs={{0,64},{64,0},{128,192},{192,128},{256,320},{320,256},{384,448},{4... | collective-permute-start | bytes 3145736 | tf_op jit(solution)/shard_map/ppermute | solution.py:12
  12.9 34.2 %copy-start.5 = (bf16[2,128,128]{2,1,0:T(8,128)(2,1)S(1)}, bf16[2,128,128]{2,1,0:T(8,128)(2,1)}, u32[]{:S(2)}) copy-start(bf16[2,128,128]{2,1,0:T(8,128)(2,1)} %param.14) | copy-start | bytes 196612
  12.9 34.2 %collective-permute-start = (bf16[1,1040,128]{2,1,0:T(8,128)(2,1)S(1)}, bf16[1,1040,128]{2,1,0:T(8,128)(2,1)S(1)}, u32[]{:S(2)}, u32[]{:S(2)}) collective-permute-start(bf16[1,1040,128]{2,1,0:T(8,128)(2,1)S(1)} %fusion.25), channel_id=1, source_target_pairs={{0,128},{64,192},{128,0},{192,64},{256,384},{320,448},{384,256},{4... | collective-permute-start | bytes 798728 | tf_op jit(solution)/shard_map/ppermute | solution.py:12
  47.5 15.9 %collective-permute-start.3 = (bf16[1024,512]{1,0:T(8,128)(2,1)S(1)}, bf16[1024,512]{1,0:T(8,128)(2,1)}, u32[]{:S(2)}, u32[]{:S(2)}) collective-permute-start(bf16[1024,512]{1,0:T(8,128)(2,1)S(1)} %bitcast.86), channel_id=1, source_target_pairs={{0,128},{64,192},{128,0},{192,64},{256,384},{320,448},{384,256},{4... | collective-permute-start | bytes 3145736 | tf_op jit(solution)/shard_map/ppermute | solution.py:12
  51.3 30.3 %collective-permute-start.2 = (bf16[2,1040,128]{2,1,0:T(8,128)(2,1)S(1)}, bf16[2,1040,128]{2,1,0:T(8,128)(2,1)S(1)}, u32[]{:S(2)}, u32[]{:S(2)}) collective-permute-start(bf16[2,1040,128]{2,1,0:T(8,128)(2,1)S(1)} %pad_maximum_fusion.1), channel_id=1, source_target_pairs={{0,64},{64,0},{128,192},{192,128},{256,320},{320,256},{384,448},{4... | collective-permute-start | bytes 1597448 | tf_op jit(solution)/shard_map/ppermute | solution.py:12
  65.0 1.2 copy-start.1
  66.7 17.5 %collective-permute-start.4 = (f32[512,256]{0,1:T(8,128)S(1)}, f32[512,256]{0,1:T(8,128)S(1)}, u32[]{:S(2)}, u32[]{:S(2)}) collective-permute-start(f32[512,256]{0,1:T(8,128)S(1)} %convolution_bitcast_fusion), channel_id=1, source_target_pairs={{0,1},{1,0},{2,3},{3,2},{4,5},{5,4},{6,7},{7,6},{8,9},{9,8},{10,11... | collective-permute-start | bytes 1572872 | tf_op jit(solution)/shard_map/ppermute | solution.py:12
  87.8 63.0 %all-to-all-start = ((bf16[64,96,128]{2,1,0:T(8,128)(2,1)}), bf16[64,96,128]{2,1,0:T(8,128)(2,1)S(1)}, u32[]{:S(2)}, u32[]{:S(2)}) async-start(bf16[64,96,128]{2,1,0:T(8,128)(2,1)} %fusion.28), calls=%async_computation | async-start | bytes 3145728 | tf_op jit(solution)/shard_map/all_to_all | solution.py:81
  152.0 5.9 %collective-permute-start.5 = (bf16[64,64,128]{2,1,0:T(8,128)(2,1)}, bf16[64,64,128]{2,1,0:T(8,128)(2,1)}, u32[]{:S(2)}, u32[]{:S(2)}) collective-permute-start(bf16[64,64,128]{2,1,0:T(8,128)(2,1)} %slice.77), channel_id=1, source_target_pairs={{0,1},{1,0},{2,3},{3,2},{4,5},{5,4},{6,7},{7,6},{8,9},{9,8},{10,11... | collective-permute-start | bytes 3145736 | tf_op jit(solution)/shard_map/ppermute | solution.py:12
  157.1 2.6 %copy-start.2 = (bf16[4,1024,128]{2,1,0:T(8,128)(2,1)S(1)}, bf16[4,1024,128]{2,1,0:T(8,128)(2,1)}, u32[]{:S(2)}) copy-start(bf16[4,1024,128]{2,1,0:T(8,128)(2,1)} %slice.59) | copy-start | bytes 3145732
  159.7 1.8 %copy-start.3 = (bf16[32,64,128]{2,1,0:T(8,128)(2,1)S(1)}, bf16[32,64,128]{2,1,0:T(8,128)(2,1)}, u32[]{:S(2)}) copy-start(bf16[32,64,128]{2,1,0:T(8,128)(2,1)} %gather_fusion) | copy-start | bytes 1572868

commit v10 on v9

--- a/solution.py
+++ b/solution.py
@@ -58,10 +58,8 @@
     half_rows = block_size // 2
     column = (group_index % merged) * quarter
     head = lax.dynamic_slice_in_dim(panel[:block_size], column, quarter, 1)
-    carried, head = lax.optimization_barrier((carried, head))
     vals_all = carried[:, : n_parent * block_size].reshape(-1, block_size, block_size)
     rows_all = carried[:, n_parent * block_size, :n_parent].reshape(-1).astype(jnp.int32)
-    outgoing = jnp.tile(head.reshape(2, half_rows, quarter), (n_sub // 2, 1, 1))
 
     half = width // 2
     keep_cols = lax.dynamic_slice_in_dim(panel, core * half, half, 1)
@@ -77,6 +75,8 @@
     highs = [lax.reduce_precision(t, exponent_bits=8, mantissa_bits=7) for t in col_tiles]
     lows = [t - h for t, h in zip(col_tiles, highs)]
     split = jnp.concatenate([h.astype(jnp.bfloat16) for h in highs] + [l.astype(jnp.bfloat16) for l in lows], axis=1)
+    carried, head, split = lax.optimization_barrier((carried, head, split))
+    outgoing = jnp.tile(head.reshape(2, half_rows, quarter), (n_sub // 2, 1, 1))
     outgoing = jnp.concatenate([outgoing, split.reshape(n_sub, -1, quarter)], axis=1)
     arrived = lax.all_to_all(outgoing, "sub", 0, 0, tiled=True)
     mine = arrived[:, :half_rows]

time: 164 us -> 162 us (0.988)
  other arithmetic: 7.42 us -> 4.94 us
  local copies, waits for them, and re-layouts: 12.2 us -> 10.3 us
    unnamed x3 -> x0, other arithmetic: 2.12 us -> none
    unnamed x17 -> x19, local copies, waits for them, and re-layouts: 2.8 us -> 0.82 us
  transfers between devices with their start and end apart: 7 -> 7, of which waited for: 3 -> 4; matrix products, arithmetic and copies ran while one was open for 7% -> 6% of each run, Pallas kernels for 0% -> 0%
where the time goes in v10:
time: 162 us; the launch traced here: 160 us
  waiting for transfers between devices  73 us (45%)
  starting transfers between devices  63.8 us (39%)
  local copies, waits for them, and re-layouts  10.3 us (6%)
  matrix products  6.89 us (4%)
  other arithmetic  4.94 us (3%)
    ppermute x6, starting transfers between devices, from_partner(): return lax.ppermute(value, axis, pairs)  40 us
    ppermute x6, waiting for transfers between devices, from_partner(): return lax.ppermute(value, axis, pairs)  36.7 us
    all_to_all x1, waiting for transfers between devices, on_device(): arrived = lax.all_to_all(outgoing, 'sub', 0, 0, tiled=True)  36.3 us
    all_to_all x1, starting transfers between devices, on_device(): arrived = lax.all_to_all(outgoing, 'sub', 0, 0, tiled=True)  23.9 us
  transfers between devices with their start and end apart: 7, of which 4 were waited for; matrix products, arithmetic and copies ran while one was open for 6% of the time, Pallas kernels for 0%

profile of v10, /device:TPU:1, one launch (start us, length us, event | category | flops | bytes accessed | tf_op | source)
XLA Modules:
  0.0 160.0 jit_solution(18191250691620914729)
XLA Ops:
  0.6 0.8 eq.22
  1.5 0.6 copy-done
  2.1 1.0 fusion.5
  3.1 0.2 copy-done.7
  3.3 1.2 fusion.8
  4.5 8.4 %collective-permute-start.1 = (bf16[1024,512]{1,0:T(8,128)(2,1)S(1)}, bf16[1024,512]{1,0:T(8,128)(2,1)S(1)}, u32[]{:S(2)}, u32[]{:S(2)}) collective-permute-start(bf16[1024,512]{1,0:T(8,128)(2,1)S(1)} %fusion.8), channel_id=1, source_target_pairs={{0,64},{64,0},{128,192},{192,128},{256,320},{320,256},{384,448},{4... | collective-permute-start | bytes 3145736 | tf_op jit(solution)/shard_map/ppermute | solution.py:12
  13.0 3.1 %collective-permute-start = (bf16[1,1040,128]{2,1,0:T(8,128)(2,1)S(1)}, bf16[1,1040,128]{2,1,0:T(8,128)(2,1)S(1)}, u32[]{:S(2)}, u32[]{:S(2)}) collective-permute-start(bf16[1,1040,128]{2,1,0:T(8,128)(2,1)S(1)} %fusion.25), channel_id=1, source_target_pairs={{0,128},{64,192},{128,0},{192,64},{256,384},{320,448},{384,256},{4... | collective-permute-start | bytes 798728 | tf_op jit(solution)/shard_map/ppermute | solution.py:12
  16.1 30.8 %collective-permute-done.1 = bf16[1024,512]{1,0:T(8,128)(2,1)S(1)} collective-permute-done((bf16[1024,512]{1,0:T(8,128)(2,1)S(1)}, bf16[1024,512]{1,0:T(8,128)(2,1)S(1)}, u32[]{:S(2)}, u32[]{:S(2)}) %collective-permute-start.1) | collective-permute-done | bytes 1048608 | tf_op jit(solution)/shard_map/ppermute | solution.py:12
  46.9 0.3 add_convert_fusion.1
  47.3 0.4 convolution_convert_fusion.1
  47.7 3.6 %collective-permute-start.3 = (bf16[1024,512]{1,0:T(8,128)(2,1)S(1)}, bf16[1024,512]{1,0:T(8,128)(2,1)}, u32[]{:S(2)}, u32[]{:S(2)}) collective-permute-start(bf16[1024,512]{1,0:T(8,128)(2,1)S(1)} %bitcast.78), channel_id=1, source_target_pairs={{0,128},{64,192},{128,0},{192,64},{256,384},{320,448},{384,256},{4... | collective-permute-start | bytes 3145736 | tf_op jit(solution)/shard_map/ppermute | solution.py:12
  51.4 7.6 %collective-permute-start.2 = (bf16[2,1040,128]{2,1,0:T(8,128)(2,1)S(1)}, bf16[2,1040,128]{2,1,0:T(8,128)(2,1)S(1)}, u32[]{:S(2)}, u32[]{:S(2)}) collective-permute-start(bf16[2,1040,128]{2,1,0:T(8,128)(2,1)S(1)} %pad_maximum_fusion.1), channel_id=1, source_target_pairs={{0,64},{64,0},{128,192},{192,128},{256,320},{320,256},{384,448},{4... | collective-permute-start | bytes 1597448 | tf_op jit(solution)/shard_map/ppermute | solution.py:12
  59.0 4.6 %collective-permute-done.3 = bf16[1024,512]{1,0:T(8,128)(2,1)} collective-permute-done((bf16[1024,512]{1,0:T(8,128)(2,1)S(1)}, bf16[1024,512]{1,0:T(8,128)(2,1)}, u32[]{:S(2)}, u32[]{:S(2)}) %collective-permute-start.3) | collective-permute-done | bytes 1048608 | tf_op jit(solution)/shard_map/ppermute | solution.py:12
  63.6 1.5 add_convert_fusion
  65.1 0.4 convolution_convert_fusion
  65.6 0.5 convolution_bitcast_fusion
  66.1 14.9 %collective-permute-start.4 = (f32[512,256]{0,1:T(8,128)S(1)}, f32[512,256]{0,1:T(8,128)S(1)}, u32[]{:S(2)}, u32[]{:S(2)}) collective-permute-start(f32[512,256]{0,1:T(8,128)S(1)} %convolution_bitcast_fusion), channel_id=1, source_target_pairs={{0,1},{1,0},{2,3},{3,2},{4,5},{5,4},{6,7},{7,6},{8,9},{9,8},{10,11... | collective-permute-start | bytes 1572872 | tf_op jit(solution)/shard_map/ppermute | solution.py:12
  81.1 1.3 collective-permute-done.4
  82.5 0.5 fusion.11
  83.5 0.2 tile.11
  83.7 1.3 pad_maximum_fusion
  85.0 23.9 %all-to-all-start = ((bf16[64,96,128]{2,1,0:T(8,128)(2,1)}), bf16[64,96,128]{2,1,0:T(8,128)(2,1)S(1)}, u32[]{:S(2)}, u32[]{:S(2)}) async-start(bf16[64,96,128]{2,1,0:T(8,128)(2,1)} %pad_maximum_fusion), calls=%async_computation | async-start | bytes 3145728 | tf_op jit(solution)/shard_map/all_to_all | solution.py:81
  108.9 2.3 %slice.73 = bf16[4,1024,128]{2,1,0:T(8,128)(2,1)} slice(bf16[4,1040,128]{2,1,0:T(8,128)(2,1)} %copy-done.2), slice={[0:4], [0:1024], [0:128]} | slice | bytes 2097152 | tf_op jit(solution)/shard_map/slice | solution.py:61
  111.1 0.7 fusion.35
  111.9 36.3 %all-to-all-done = bf16[64,96,128]{2,1,0:T(8,128)(2,1)S(1)} async-done(((bf16[64,96,128]{2,1,0:T(8,128)(2,1)}), bf16[64,96,128]{2,1,0:T(8,128)(2,1)S(1)}, u32[]{:S(2)}, u32[]{:S(2)}) %all-to-all-start) | async-done | bytes 1572896 | tf_op jit(solution)/shard_map/all_to_all | solution.py:81
  148.2 1.1 slice.79
  149.3 2.3 %collective-permute-start.5 = (bf16[64,64,128]{2,1,0:T(8,128)(2,1)}, bf16[64,64,128]{2,1,0:T(8,128)(2,1)}, u32[]{:S(2)}, u32[]{:S(2)}) collective-permute-start(bf16[64,64,128]{2,1,0:T(8,128)(2,1)} %slice.79), channel_id=1, source_target_pairs={{0,1},{1,0},{2,3},{3,2},{4,5},{5,4},{6,7},{7,6},{8,9},{9,8},{10,11... | collective-permute-start | bytes 3145736 | tf_op jit(solution)/shard_map/ppermute | solution.py:12
  151.7 2.6 %gather_fusion = bf16[32,64,128]{2,1,0:T(8,128)(2,1)} fusion(bf16[64,64,128]{2,1,0:T(8,128)(2,1)} %slice.79, s32[1024]{0:T(1024)S(1)} %pad_clamp_fusion), kind=kCustom, calls=%fused_computation.clone | custom fusion | bytes 1048704 | tf_op jit(solution)/shard_map/jit(_take)/gather | solution.py:89
  154.6 0.7 reduce_sum.9
  155.2 1.9 %gather_fusion.1 = bf16[32,64,128]{2,1,0:T(8,128)(2,1)S(1)} fusion(bf16[64,64,128]{2,1,0:T(8,128)(2,1)} %collective-permute-done.5, s32[1024]{0:T(1024)S(1)} %pad_clamp_fusion), kind=kCustom, calls=%fused_computation.1.clone | custom fusion | bytes 1048704 | tf_op jit(solution)/shard_map/jit(_take)/gather | solution.py:90
  157.1 1.8 %convolution_bitcast_fusion.2 = f32[128,128]{1,0:T(8,128)S(1)} fusion(bf16[32,128,128]{2,1,0:T(8,128)(2,1)S(1)} %bitcast.85, pred[]{:T(512)S(6)} %eq.26, bf16[32,64,128]{2,1,0:T(8,128)(2,1)} %gather_fusion, pred[32]{0:T(512)(128)(4,1)S(1)} %compare_and_fusion, bf16[32,64,128]{2,1,0:T(8,128)(2,1)S(1)} %gather_fusion.1), kind=kOutput, calls=%fused_computation.17 | convolution fusion | flops 67895296 | bytes 2162721 | tf_op jit(solution)/shard_map/kab,kbm->am/dot_general | solution.py:95
  158.9 1.0 fusion.13
  (37 shorter events, 1.0 us)
Async XLA Ops:
  0.6 1.4 copy-start
  2.1 1.2 copy-start.7
  3.3 9.7 %copy-start.8 = (s32[8]{0:T(128)S(1)}, s32[8]{0:T(128)}, u32[]{:S(2)}) copy-start(s32[8]{0:T(128)} %param.17) | copy-start | bytes 100
  3.3 9.7 %copy-start.5 = (bf16[8,128,128]{2,1,0:T(8,128)(2,1)S(1)}, bf16[8,128,128]{2,1,0:T(8,128)(2,1)}, u32[]{:S(2)}) copy-start(bf16[8,128,128]{2,1,0:T(8,128)(2,1)} %param.16) | copy-start | bytes 786436
  4.5 42.7 %copy-start.6 = (bf16[2,128,128]{2,1,0:T(8,128)(2,1)S(1)}, bf16[2,128,128]{2,1,0:T(8,128)(2,1)}, u32[]{:S(2)}) copy-start(bf16[2,128,128]{2,1,0:T(8,128)(2,1)} %param.14) | copy-start | bytes 196612
  4.5 42.4 %collective-permute-start.1 = (bf16[1024,512]{1,0:T(8,128)(2,1)S(1)}, bf16[1024,512]{1,0:T(8,128)(2,1)S(1)}, u32[]{:S(2)}, u32[]{:S(2)}) collective-permute-start(bf16[1024,512]{1,0:T(8,128)(2,1)S(1)} %fusion.8), channel_id=1, source_target_pairs={{0,64},{64,0},{128,192},{192,128},{256,320},{320,256},{384,448},{4... | collective-permute-start | bytes 3145736 | tf_op jit(solution)/shard_map/ppermute | solution.py:12
  13.0 34.2 %collective-permute-start = (bf16[1,1040,128]{2,1,0:T(8,128)(2,1)S(1)}, bf16[1,1040,128]{2,1,0:T(8,128)(2,1)S(1)}, u32[]{:S(2)}, u32[]{:S(2)}) collective-permute-start(bf16[1,1040,128]{2,1,0:T(8,128)(2,1)S(1)} %fusion.25), channel_id=1, source_target_pairs={{0,128},{64,192},{128,0},{192,64},{256,384},{320,448},{384,256},{4... | collective-permute-start | bytes 798728 | tf_op jit(solution)/shard_map/ppermute | solution.py:12
  47.7 15.9 %collective-permute-start.3 = (bf16[1024,512]{1,0:T(8,128)(2,1)S(1)}, bf16[1024,512]{1,0:T(8,128)(2,1)}, u32[]{:S(2)}, u32[]{:S(2)}) collective-permute-start(bf16[1024,512]{1,0:T(8,128)(2,1)S(1)} %bitcast.78), channel_id=1, source_target_pairs={{0,128},{64,192},{128,0},{192,64},{256,384},{320,448},{384,256},{4... | collective-permute-start | bytes 3145736 | tf_op jit(solution)/shard_map/ppermute | solution.py:12
  51.4 14.1 %copy-start.1 = (bf16[1024,512]{1,0:T(8,128)(2,1)S(1)}, bf16[1024,512]{1,0:T(8,128)(2,1)}, u32[]{:S(2)}) copy-start(bf16[1024,512]{1,0:T(8,128)(2,1)} %param.15) | copy-start | bytes 3145732
  51.4 29.5 %collective-permute-start.2 = (bf16[2,1040,128]{2,1,0:T(8,128)(2,1)S(1)}, bf16[2,1040,128]{2,1,0:T(8,128)(2,1)S(1)}, u32[]{:S(2)}, u32[]{:S(2)}) collective-permute-start(bf16[2,1040,128]{2,1,0:T(8,128)(2,1)S(1)} %pad_maximum_fusion.1), channel_id=1, source_target_pairs={{0,64},{64,0},{128,192},{192,128},{256,320},{320,256},{384,448},{4... | collective-permute-start | bytes 1597448 | tf_op jit(solution)/shard_map/ppermute | solution.py:12
  66.1 16.4 %collective-permute-start.4 = (f32[512,256]{0,1:T(8,128)S(1)}, f32[512,256]{0,1:T(8,128)S(1)}, u32[]{:S(2)}, u32[]{:S(2)}) collective-permute-start(f32[512,256]{0,1:T(8,128)S(1)} %convolution_bitcast_fusion), channel_id=1, source_target_pairs={{0,1},{1,0},{2,3},{3,2},{4,5},{5,4},{6,7},{7,6},{8,9},{9,8},{10,11... | collective-permute-start | bytes 1572872 | tf_op jit(solution)/shard_map/ppermute | solution.py:12
  81.1 1.9 %copy-start.2 = (bf16[4,1040,128]{2,1,0:T(8,128)(2,1)}, bf16[4,1040,128]{2,1,0:T(8,128)(2,1)S(1)}, u32[]{:S(2)}) copy-start(bf16[4,1040,128]{2,1,0:T(8,128)(2,1)S(1)} %constant_dynamic-update-slice_fusion) | copy-start | bytes 3194884
  85.0 63.3 %all-to-all-start = ((bf16[64,96,128]{2,1,0:T(8,128)(2,1)}), bf16[64,96,128]{2,1,0:T(8,128)(2,1)S(1)}, u32[]{:S(2)}, u32[]{:S(2)}) async-start(bf16[64,96,128]{2,1,0:T(8,128)(2,1)} %pad_maximum_fusion), calls=%async_computation | async-start | bytes 3145728 | tf_op jit(solution)/shard_map/all_to_all | solution.py:81
  149.3 5.9 %collective-permute-start.5 = (bf16[64,64,128]{2,1,0:T(8,128)(2,1)}, bf16[64,64,128]{2,1,0:T(8,128)(2,1)}, u32[]{:S(2)}, u32[]{:S(2)}) collective-permute-start(bf16[64,64,128]{2,1,0:T(8,128)(2,1)} %slice.79), channel_id=1, source_target_pairs={{0,1},{1,0},{2,3},{3,2},{4,5},{5,4},{6,7},{7,6},{8,9},{9,8},{10,11... | collective-permute-start | bytes 3145736 | tf_op jit(solution)/shard_map/ppermute | solution.py:12
  154.5 2.6 %copy-start.3 = (bf16[4,1024,128]{2,1,0:T(8,128)(2,1)S(1)}, bf16[4,1024,128]{2,1,0:T(8,128)(2,1)}, u32[]{:S(2)}) copy-start(bf16[4,1024,128]{2,1,0:T(8,128)(2,1)} %slice.73) | copy-start | bytes 3145732
  157.1 1.8 %copy-start.4 = (bf16[32,64,128]{2,1,0:T(8,128)(2,1)S(1)}, bf16[32,64,128]{2,1,0:T(8,128)(2,1)}, u32[]{:S(2)}) copy-start(bf16[32,64,128]{2,1,0:T(8,128)(2,1)} %gather_fusion) | copy-start | bytes 1572868

commit v11 on v10

--- a/solution.py
+++ b/solution.py
@@ -42,7 +42,8 @@
         sibling = from_partner(panel, "group", 2**level)
         partner = levels - 1 - level
         carried, panel = lax.optimization_barrier((carried, panel))
-        arrived = from_partner(carried, "group", 2**partner)
+        outbound = carried if level < levels - 1 else carried[:1]
+        arrived = from_partner(outbound, "group", 2**partner)
         total = (panel.astype(jnp.float32) + sibling.astype(jnp.float32)).astype(jnp.bfloat16)
         if level < levels - 1:
             arrived, total = lax.optimization_barrier((arrived, total))
@@ -58,8 +59,6 @@
     half_rows = block_size // 2
     column = (group_index % merged) * quarter
     head = lax.dynamic_slice_in_dim(panel[:block_size], column, quarter, 1)
-    vals_all = carried[:, : n_parent * block_size].reshape(-1, block_size, block_size)
-    rows_all = carried[:, n_parent * block_size, :n_parent].reshape(-1).astype(jnp.int32)
 
     half = width // 2
     keep_cols = lax.dynamic_slice_in_dim(panel, core * half, half, 1)
@@ -76,6 +75,10 @@
     lows = [t - h for t, h in zip(col_tiles, highs)]
     split = jnp.concatenate([h.astype(jnp.bfloat16) for h in highs] + [l.astype(jnp.bfloat16) for l in lows], axis=1)
     carried, head, split = lax.optimization_barrier((carried, head, split))
+    relayed = from_partner(carried[-1:], "group", 2 ** (levels - 1))
+    carried = jnp.concatenate([carried, relayed], axis=0)
+    vals_all = carried[:, : n_parent * block_size].reshape(-1, block_size, block_size)
+    rows_all = carried[:, n_parent * block_size, :n_parent].reshape(-1).astype(jnp.int32)
     outgoing = jnp.tile(head.reshape(2, half_rows, quarter), (n_sub // 2, 1, 1))
     outgoing = jnp.concatenate([outgoing, split.reshape(n_sub, -1, quarter)], axis=1)
     arrived = lax.all_to_all(outgoing, "sub", 0, 0, tiled=True)

time: 162 us -> 164 us (1.012)
  waiting for transfers between devices: 73 us -> 65.9 us
  starting transfers between devices: 63.8 us -> 66.6 us
  local copies, waits for them, and re-layouts: 10.3 us -> 12.9 us
  other arithmetic: 4.94 us -> 7.2 us
  matrix products: 6.89 us -> 8.71 us
    all_to_all x1, waiting for transfers between devices: 36.3 us -> 26.9 us  [on_device(): arrived = lax.all_to_all(outgoing, 'sub', 0, 0, tiled=True)]
    ppermute x6 -> x7, starting transfers between devices: 40 us -> 43 us  [from_partner(): return lax.ppermute(value, axis, pairs)]
    concatenate x1 -> x2, other arithmetic: 0.05 us -> 3.01 us  [on_device(): carried = jnp.concatenate([carried, arrived], axis=0)]
    slice x0 -> x2, local copies, waits for them, and re-layouts: none -> 2.41 us  [the longest x1 1.68 us: on_device(): relayed = from_partner(carried[-1:], 'group', 2 ** (levels - 1))]
    ppermute x6 -> x7, waiting for transfers between devices: 36.7 us -> 39 us  [from_partner(): return lax.ppermute(value, axis, pairs)]
  transfers between devices with their start and end apart: 7 -> 8, of which waited for: 4 -> 4; matrix products, arithmetic and copies ran while one was open for 6% -> 9% of each run, Pallas kernels for 0% -> 0%
where the time goes in v11:
time: 164 us; the launch traced here: 162 us
  starting transfers between devices  66.6 us (41%)
  waiting for transfers between devices  65.9 us (40%)
  local copies, waits for them, and re-layouts  12.9 us (8%)
  matrix products  8.71 us (5%)
  other arithmetic  7.2 us (4%)
    ppermute x7, starting transfers between devices, from_partner(): return lax.ppermute(value, axis, pairs)  43 us
    ppermute x7, waiting for transfers between devices, from_partner(): return lax.ppermute(value, axis, pairs)  39 us
    all_to_all x1, waiting for transfers between devices, on_device(): arrived = lax.all_to_all(outgoing, 'sub', 0, 0, tiled=True)  26.9 us
    all_to_all x1, starting transfers between devices, on_device(): arrived = lax.all_to_all(outgoing, 'sub', 0, 0, tiled=True)  23.6 us
  transfers between devices with their start and end apart: 8, of which 4 were waited for; matrix products, arithmetic and copies ran while one was open for 9% of the time, Pallas kernels for 0%

profile of v11, /device:TPU:1, one launch (start us, length us, event | category | flops | bytes accessed | tf_op | source)
XLA Modules:
  0.0 162.4 jit_solution(3063271316263944237)
XLA Ops:
  0.6 0.8 eq.22
  1.5 0.6 copy-done
  2.1 1.0 fusion.5
  3.3 1.2 fusion.8
  4.5 8.4 %collective-permute-start.1 = (bf16[1024,512]{1,0:T(8,128)(2,1)S(1)}, bf16[1024,512]{1,0:T(8,128)(2,1)S(1)}, u32[]{:S(2)}, u32[]{:S(2)}) collective-permute-start(bf16[1024,512]{1,0:T(8,128)(2,1)S(1)} %fusion.8), channel_id=1, source_target_pairs={{0,64},{64,0},{128,192},{192,128},{256,320},{320,256},{384,448},{4... | collective-permute-start | bytes 3145736 | tf_op jit(solution)/shard_map/ppermute | solution.py:12
  13.0 3.1 %collective-permute-start = (bf16[1,1040,128]{2,1,0:T(8,128)(2,1)S(1)}, bf16[1,1040,128]{2,1,0:T(8,128)(2,1)S(1)}, u32[]{:S(2)}, u32[]{:S(2)}) collective-permute-start(bf16[1,1040,128]{2,1,0:T(8,128)(2,1)S(1)} %fusion.25), channel_id=1, source_target_pairs={{0,128},{64,192},{128,0},{192,64},{256,384},{320,448},{384,256},{4... | collective-permute-start | bytes 798728 | tf_op jit(solution)/shard_map/ppermute | solution.py:12
  16.1 30.8 %collective-permute-done.1 = bf16[1024,512]{1,0:T(8,128)(2,1)S(1)} collective-permute-done((bf16[1024,512]{1,0:T(8,128)(2,1)S(1)}, bf16[1024,512]{1,0:T(8,128)(2,1)S(1)}, u32[]{:S(2)}, u32[]{:S(2)}) %collective-permute-start.1) | collective-permute-done | bytes 1048608 | tf_op jit(solution)/shard_map/ppermute | solution.py:12
  48.0 3.6 %collective-permute-start.3 = (bf16[1024,512]{1,0:T(8,128)(2,1)S(1)}, bf16[1024,512]{1,0:T(8,128)(2,1)}, u32[]{:S(2)}, u32[]{:S(2)}) collective-permute-start(bf16[1024,512]{1,0:T(8,128)(2,1)S(1)} %bitcast.78), channel_id=1, source_target_pairs={{0,128},{64,192},{128,0},{192,64},{256,384},{320,448},{384,256},{4... | collective-permute-start | bytes 3145736 | tf_op jit(solution)/shard_map/ppermute | solution.py:12
  51.6 1.0 pad_maximum_fusion.2
  52.6 0.7 slice.63
  53.4 7.6 %collective-permute-start.2 = (bf16[1,1040,128]{2,1,0:T(8,128)(2,1)}, bf16[1,1040,128]{2,1,0:T(8,128)(2,1)}, u32[]{:S(2)}, u32[]{:S(2)}) collective-permute-start(bf16[1,1040,128]{2,1,0:T(8,128)(2,1)} %slice.63), channel_id=1, source_target_pairs={{0,64},{64,0},{128,192},{192,128},{256,320},{320,256},{384,448},{4... | collective-permute-start | bytes 798728 | tf_op jit(solution)/shard_map/ppermute | solution.py:12
  60.9 2.9 %collective-permute-done.3 = bf16[1024,512]{1,0:T(8,128)(2,1)} collective-permute-done((bf16[1024,512]{1,0:T(8,128)(2,1)S(1)}, bf16[1024,512]{1,0:T(8,128)(2,1)}, u32[]{:S(2)}, u32[]{:S(2)}) %collective-permute-start.3) | collective-permute-done | bytes 1048608 | tf_op jit(solution)/shard_map/ppermute | solution.py:12
  63.9 1.5 add_convert_fusion
  65.8 1.3 convolution_bitcast_fusion
  67.1 14.9 %collective-permute-start.4 = (f32[512,256]{0,1:T(8,128)}, f32[512,256]{0,1:T(8,128)}, u32[]{:S(2)}, u32[]{:S(2)}) collective-permute-start(f32[512,256]{0,1:T(8,128)} %convolution_bitcast_fusion), channel_id=1, source_target_pairs={{0,1},{1,0},{2,3},{3,2},{4,5},{5,4},{6,7},{7,6},{8,9},{9,8},{10,11... | collective-permute-start | bytes 1572872 | tf_op jit(solution)/shard_map/ppermute | solution.py:12
  82.0 2.0 %pad_maximum_fusion.1 = bf16[3,1040,128]{2,1,0:T(8,128)(2,1)} fusion(bf16[1,1040,128]{2,1,0:T(8,128)(2,1)} %collective-permute-done.2, bf16[2,1040,128]{2,1,0:T(8,128)(2,1)S(1)} %pad_maximum_fusion.2), kind=kLoop, calls=%fused_computation.23 | loop fusion | flops 399360 | bytes 1597440 | tf_op jit(solution)/shard_map/concatenate | solution.py:50
  84.1 1.5 fusion.11
  86.4 1.3 pad_maximum_fusion
  87.6 23.6 %all-to-all-start = ((bf16[64,96,128]{2,1,0:T(8,128)(2,1)}), bf16[64,96,128]{2,1,0:T(8,128)(2,1)S(1)}, u32[]{:S(2)}, u32[]{:S(2)}) async-start(bf16[64,96,128]{2,1,0:T(8,128)(2,1)} %pad_maximum_fusion), calls=%async_computation | async-start | bytes 3145728 | tf_op jit(solution)/shard_map/all_to_all | solution.py:84
  111.2 1.7 %slice.68 = bf16[1,1040,128]{2,1,0:T(8,128)(2,1)} slice(bf16[3,1040,128]{2,1,0:T(8,128)(2,1)} %pad_maximum_fusion.1), slice={[2:3], [0:1040], [0:128]} | slice | bytes 532480 | tf_op jit(solution)/shard_map/slice | solution.py:78
  112.9 3.1 %collective-permute-start.5 = (bf16[1,1040,128]{2,1,0:T(8,128)(2,1)}, bf16[1,1040,128]{2,1,0:T(8,128)(2,1)S(1)}, u32[]{:S(2)}, u32[]{:S(2)}) collective-permute-start(bf16[1,1040,128]{2,1,0:T(8,128)(2,1)} %slice.68), channel_id=1, source_target_pairs={{0,128},{64,192},{128,0},{192,64},{256,384},{320,448},{384,256},{4... | collective-permute-start | bytes 798728 | tf_op jit(solution)/shard_map/ppermute | solution.py:12
  116.0 1.2 constant_dynamic-update-slice_fusion.1
  117.2 5.3 %collective-permute-done.5 = bf16[1,1040,128]{2,1,0:T(8,128)(2,1)S(1)} collective-permute-done((bf16[1,1040,128]{2,1,0:T(8,128)(2,1)}, bf16[1,1040,128]{2,1,0:T(8,128)(2,1)S(1)}, u32[]{:S(2)}, u32[]{:S(2)}) %collective-permute-start.5) | collective-permute-done | bytes 266272 | tf_op jit(solution)/shard_map/ppermute | solution.py:12
  122.6 1.1 slice.84
  123.7 26.9 %all-to-all-done = bf16[64,96,128]{2,1,0:T(8,128)(2,1)S(1)} async-done(((bf16[64,96,128]{2,1,0:T(8,128)(2,1)}), bf16[64,96,128]{2,1,0:T(8,128)(2,1)S(1)}, u32[]{:S(2)}, u32[]{:S(2)}) %all-to-all-start) | async-done | bytes 1572896 | tf_op jit(solution)/shard_map/all_to_all | solution.py:84
  150.6 1.1 slice.87
  151.7 2.3 %collective-permute-start.6 = (bf16[64,64,128]{2,1,0:T(8,128)(2,1)}, bf16[64,64,128]{2,1,0:T(8,128)(2,1)}, u32[]{:S(2)}, u32[]{:S(2)}) collective-permute-start(bf16[64,64,128]{2,1,0:T(8,128)(2,1)} %slice.87), channel_id=1, source_target_pairs={{0,1},{1,0},{2,3},{3,2},{4,5},{5,4},{6,7},{7,6},{8,9},{9,8},{10,11... | collective-permute-start | bytes 3145736 | tf_op jit(solution)/shard_map/ppermute | solution.py:12
  154.1 2.7 %gather_fusion = bf16[32,64,128]{2,1,0:T(8,128)(2,1)} fusion(bf16[64,64,128]{2,1,0:T(8,128)(2,1)} %slice.87, s32[1024]{0:T(1024)S(1)} %pad_clamp_fusion), kind=kCustom, calls=%fused_computation.clone | custom fusion | bytes 1048704 | tf_op jit(solution)/shard_map/jit(_take)/gather | solution.py:92
  157.0 0.7 reduce_sum.9
  157.7 1.9 %gather_fusion.1 = bf16[32,64,128]{2,1,0:T(8,128)(2,1)S(1)} fusion(bf16[64,64,128]{2,1,0:T(8,128)(2,1)} %collective-permute-done.6, s32[1024]{0:T(1024)S(1)} %pad_clamp_fusion), kind=kCustom, calls=%fused_computation.1.clone | custom fusion | bytes 1048704 | tf_op jit(solution)/shard_map/jit(_take)/gather | solution.py:93
  159.6 1.8 %convolution_bitcast_fusion.2 = f32[128,128]{1,0:T(8,128)S(1)} fusion(bf16[32,128,128]{2,1,0:T(8,128)(2,1)S(1)} %bitcast.85, pred[]{:T(512)S(6)} %eq.26, bf16[32,64,128]{2,1,0:T(8,128)(2,1)} %gather_fusion, pred[32]{0:T(512)(128)(4,1)S(1)} %compare_and_fusion, bf16[32,64,128]{2,1,0:T(8,128)(2,1)S(1)} %gather_fusion.1), kind=kOutput, calls=%fused_computation.17 | convolution fusion | flops 67895296 | bytes 2162721 | tf_op jit(solution)/shard_map/kab,kbm->am/dot_general | solution.py:98
  161.3 1.0 fusion.13
  (44 shorter events, 2.8 us)
Async XLA Ops:
  0.6 1.4 copy-start
  2.1 1.2 copy-start.8
  3.3 9.7 %copy-start.9 = (s32[8]{0:T(128)S(1)}, s32[8]{0:T(128)}, u32[]{:S(2)}) copy-start(s32[8]{0:T(128)} %param.17) | copy-start | bytes 100
  3.3 9.7 %copy-start.6 = (bf16[8,128,128]{2,1,0:T(8,128)(2,1)S(1)}, bf16[8,128,128]{2,1,0:T(8,128)(2,1)}, u32[]{:S(2)}) copy-start(bf16[8,128,128]{2,1,0:T(8,128)(2,1)} %param.16) | copy-start | bytes 786436
  4.5 42.7 %copy-start.7 = (bf16[2,128,128]{2,1,0:T(8,128)(2,1)S(1)}, bf16[2,128,128]{2,1,0:T(8,128)(2,1)}, u32[]{:S(2)}) copy-start(bf16[2,128,128]{2,1,0:T(8,128)(2,1)} %param.14) | copy-start | bytes 196612
  4.5 42.4 %collective-permute-start.1 = (bf16[1024,512]{1,0:T(8,128)(2,1)S(1)}, bf16[1024,512]{1,0:T(8,128)(2,1)S(1)}, u32[]{:S(2)}, u32[]{:S(2)}) collective-permute-start(bf16[1024,512]{1,0:T(8,128)(2,1)S(1)} %fusion.8), channel_id=1, source_target_pairs={{0,64},{64,0},{128,192},{192,128},{256,320},{320,256},{384,448},{4... | collective-permute-start | bytes 3145736 | tf_op jit(solution)/shard_map/ppermute | solution.py:12
  13.0 34.2 %collective-permute-start = (bf16[1,1040,128]{2,1,0:T(8,128)(2,1)S(1)}, bf16[1,1040,128]{2,1,0:T(8,128)(2,1)S(1)}, u32[]{:S(2)}, u32[]{:S(2)}) collective-permute-start(bf16[1,1040,128]{2,1,0:T(8,128)(2,1)S(1)} %fusion.25), channel_id=1, source_target_pairs={{0,128},{64,192},{128,0},{192,64},{256,384},{320,448},{384,256},{4... | collective-permute-start | bytes 798728 | tf_op jit(solution)/shard_map/ppermute | solution.py:12
  47.3 0.7 copy-start.5
  48.0 15.9 %collective-permute-start.3 = (bf16[1024,512]{1,0:T(8,128)(2,1)S(1)}, bf16[1024,512]{1,0:T(8,128)(2,1)}, u32[]{:S(2)}, u32[]{:S(2)}) collective-permute-start(bf16[1024,512]{1,0:T(8,128)(2,1)S(1)} %bitcast.78), channel_id=1, source_target_pairs={{0,128},{64,192},{128,0},{192,64},{256,384},{320,448},{384,256},{4... | collective-permute-start | bytes 3145736 | tf_op jit(solution)/shard_map/ppermute | solution.py:12
  53.3 12.5 %copy-start.1 = (bf16[1024,512]{1,0:T(8,128)(2,1)S(1)}, bf16[1024,512]{1,0:T(8,128)(2,1)}, u32[]{:S(2)}) copy-start(bf16[1024,512]{1,0:T(8,128)(2,1)} %param.15) | copy-start | bytes 3145732
  53.4 28.7 %collective-permute-start.2 = (bf16[1,1040,128]{2,1,0:T(8,128)(2,1)}, bf16[1,1040,128]{2,1,0:T(8,128)(2,1)}, u32[]{:S(2)}, u32[]{:S(2)}) collective-permute-start(bf16[1,1040,128]{2,1,0:T(8,128)(2,1)} %slice.63), channel_id=1, source_target_pairs={{0,64},{64,0},{128,192},{192,128},{256,320},{320,256},{384,448},{4... | collective-permute-start | bytes 798728 | tf_op jit(solution)/shard_map/ppermute | solution.py:12
  67.1 17.0 %collective-permute-start.4 = (f32[512,256]{0,1:T(8,128)}, f32[512,256]{0,1:T(8,128)}, u32[]{:S(2)}, u32[]{:S(2)}) collective-permute-start(f32[512,256]{0,1:T(8,128)} %convolution_bitcast_fusion), channel_id=1, source_target_pairs={{0,1},{1,0},{2,3},{3,2},{4,5},{5,4},{6,7},{7,6},{8,9},{9,8},{10,11... | collective-permute-start | bytes 1572872 | tf_op jit(solution)/shard_map/ppermute | solution.py:12
  82.0 2.1 %copy-start.2 = (bf16[1024,512]{1,0:T(8,128)(2,1)S(1)}, bf16[1024,512]{1,0:T(8,128)(2,1)}, u32[]{:S(2)}) copy-start(bf16[1024,512]{1,0:T(8,128)(2,1)} %param.15) | copy-start | bytes 3145732
  87.6 63.0 %all-to-all-start = ((bf16[64,96,128]{2,1,0:T(8,128)(2,1)}), bf16[64,96,128]{2,1,0:T(8,128)(2,1)S(1)}, u32[]{:S(2)}, u32[]{:S(2)}) async-start(bf16[64,96,128]{2,1,0:T(8,128)(2,1)} %pad_maximum_fusion), calls=%async_computation | async-start | bytes 3145728 | tf_op jit(solution)/shard_map/all_to_all | solution.py:84
  112.9 9.6 %collective-permute-start.5 = (bf16[1,1040,128]{2,1,0:T(8,128)(2,1)}, bf16[1,1040,128]{2,1,0:T(8,128)(2,1)S(1)}, u32[]{:S(2)}, u32[]{:S(2)}) collective-permute-start(bf16[1,1040,128]{2,1,0:T(8,128)(2,1)} %slice.68), channel_id=1, source_target_pairs={{0,128},{64,192},{128,0},{192,64},{256,384},{320,448},{384,256},{4... | collective-permute-start | bytes 798728 | tf_op jit(solution)/shard_map/ppermute | solution.py:12
  151.7 5.9 %collective-permute-start.6 = (bf16[64,64,128]{2,1,0:T(8,128)(2,1)}, bf16[64,64,128]{2,1,0:T(8,128)(2,1)}, u32[]{:S(2)}, u32[]{:S(2)}) collective-permute-start(bf16[64,64,128]{2,1,0:T(8,128)(2,1)} %slice.87), channel_id=1, source_target_pairs={{0,1},{1,0},{2,3},{3,2},{4,5},{5,4},{6,7},{7,6},{8,9},{9,8},{10,11... | collective-permute-start | bytes 3145736 | tf_op jit(solution)/shard_map/ppermute | solution.py:12
  156.9 2.6 %copy-start.3 = (bf16[4,1024,128]{2,1,0:T(8,128)(2,1)S(1)}, bf16[4,1024,128]{2,1,0:T(8,128)(2,1)}, u32[]{:S(2)}) copy-start(bf16[4,1024,128]{2,1,0:T(8,128)(2,1)} %slice.84) | copy-start | bytes 3145732
  159.5 1.8 %copy-start.4 = (bf16[32,64,128]{2,1,0:T(8,128)(2,1)S(1)}, bf16[32,64,128]{2,1,0:T(8,128)(2,1)}, u32[]{:S(2)}) copy-start(bf16[32,64,128]{2,1,0:T(8,128)(2,1)} %gather_fusion) | copy-start | bytes 1572868

commit v12 on v10

--- a/solution.py
+++ b/solution.py
@@ -75,7 +75,7 @@
     highs = [lax.reduce_precision(t, exponent_bits=8, mantissa_bits=7) for t in col_tiles]
     lows = [t - h for t, h in zip(col_tiles, highs)]
     split = jnp.concatenate([h.astype(jnp.bfloat16) for h in highs] + [l.astype(jnp.bfloat16) for l in lows], axis=1)
-    carried, head, split = lax.optimization_barrier((carried, head, split))
+    vals_all, rows_all, head, split = lax.optimization_barrier((vals_all, rows_all, head, split))
     outgoing = jnp.tile(head.reshape(2, half_rows, quarter), (n_sub // 2, 1, 1))
     outgoing = jnp.concatenate([outgoing, split.reshape(n_sub, -1, quarter)], axis=1)
     arrived = lax.all_to_all(outgoing, "sub", 0, 0, tiled=True)
@@ -85,9 +85,9 @@
     by_half = spread.reshape(n_sub // 2, 2, tiles, out_rows, lanes).sum(axis=0)
     projected = by_half.transpose(2, 0, 1, 3).reshape(out_rows, width)
 
-    theirs = from_partner(mine, "sub", 1)
-    picked_mine = jnp.take(mine, rows_all, axis=0)
-    picked_theirs = jnp.take(theirs, rows_all, axis=0)
+    theirs = from_partner(arrived, "sub", 1)
+    picked_mine = jnp.take(arrived, rows_all, axis=0)[:, :half_rows]
+    picked_theirs = jnp.take(theirs, rows_all, axis=0)[:, :half_rows]
     picked_low = jnp.where(core == 0, picked_mine, picked_theirs)
     picked_high = jnp.where(core == 0, picked_theirs, picked_mine)
     parent_sum = jnp.einsum(

time: 162 us -> 164 us (1.012)
  blocking collectives: 0 us -> 63.1 us
  waiting for transfers between devices: 73 us -> 35.7 us
  starting transfers between devices: 63.8 us -> 39.9 us
    all_to_all x0 -> x1, blocking collectives: none -> 63.1 us  [on_device(): arrived = lax.all_to_all(outgoing, 'sub', 0, 0, tiled=True)]
    all_to_all x1 -> x0, waiting for transfers between devices: 36.3 us -> none  [on_device(): arrived = lax.all_to_all(outgoing, 'sub', 0, 0, tiled=True)]
    all_to_all x1 -> x0, starting transfers between devices: 23.9 us -> none  [on_device(): arrived = lax.all_to_all(outgoing, 'sub', 0, 0, tiled=True)]
    optimization_barrier x0 -> x1, local copies, waits for them, and re-layouts: none -> 2.28 us  [on_device(): lax.optimization_barrier((vals_all, rows_all, head, split))]
  transfers between devices with their start and end apart: 7 -> 6, of which waited for: 4 -> 3; matrix products, arithmetic and copies ran while one was open for 6% -> 7% of each run, Pallas kernels for 0% -> 0%
where the time goes in v12:
time: 164 us; the launch traced here: 162 us
  blocking collectives  63.1 us (38%)
  starting transfers between devices  39.9 us (24%)
  waiting for transfers between devices  35.7 us (22%)
  local copies, waits for them, and re-layouts  9.36 us (6%)
  matrix products  8.26 us (5%)
  other arithmetic  4.93 us (3%)
    all_to_all x1, blocking collectives, on_device(): arrived = lax.all_to_all(outgoing, 'sub', 0, 0, tiled=True)  63.1 us
    ppermute x6, starting transfers between devices, from_partner(): return lax.ppermute(value, axis, pairs)  39.9 us
    ppermute x6, waiting for transfers between devices, from_partner(): return lax.ppermute(value, axis, pairs)  35.7 us
  transfers between devices with their start and end apart: 6, of which 3 were waited for; matrix products, arithmetic and copies ran while one was open for 7% of the time, Pallas kernels for 0%

profile of v12, /device:TPU:1, one launch (start us, length us, event | category | flops | bytes accessed | tf_op | source)
XLA Modules:
  0.0 162.2 jit_solution(15429248301067451876)
XLA Ops:
  0.6 0.8 eq.22
  1.5 0.6 copy-done
  2.1 1.0 fusion.5
  3.1 0.2 copy-done.6
  3.3 1.2 fusion.8
  4.5 8.4 %collective-permute-start.1 = (bf16[1024,512]{1,0:T(8,128)(2,1)S(1)}, bf16[1024,512]{1,0:T(8,128)(2,1)S(1)}, u32[]{:S(2)}, u32[]{:S(2)}) collective-permute-start(bf16[1024,512]{1,0:T(8,128)(2,1)S(1)} %fusion.8), channel_id=1, source_target_pairs={{0,64},{64,0},{128,192},{192,128},{256,320},{320,256},{384,448},{4... | collective-permute-start | bytes 3145736 | tf_op jit(solution)/shard_map/ppermute | solution.py:12
  13.0 3.1 %collective-permute-start = (bf16[1,1040,128]{2,1,0:T(8,128)(2,1)S(1)}, bf16[1,1040,128]{2,1,0:T(8,128)(2,1)S(1)}, u32[]{:S(2)}, u32[]{:S(2)}) collective-permute-start(bf16[1,1040,128]{2,1,0:T(8,128)(2,1)S(1)} %fusion.25), channel_id=1, source_target_pairs={{0,128},{64,192},{128,0},{192,64},{256,384},{320,448},{384,256},{4... | collective-permute-start | bytes 798728 | tf_op jit(solution)/shard_map/ppermute | solution.py:12
  16.1 30.8 %collective-permute-done.1 = bf16[1024,512]{1,0:T(8,128)(2,1)S(1)} collective-permute-done((bf16[1024,512]{1,0:T(8,128)(2,1)S(1)}, bf16[1024,512]{1,0:T(8,128)(2,1)S(1)}, u32[]{:S(2)}, u32[]{:S(2)}) %collective-permute-start.1) | collective-permute-done | bytes 1048608 | tf_op jit(solution)/shard_map/ppermute | solution.py:12
  46.9 0.3 add_convert_fusion.1
  47.3 0.4 convolution_convert_fusion.1
  47.7 3.6 %collective-permute-start.3 = (bf16[1024,512]{1,0:T(8,128)(2,1)S(1)}, bf16[1024,512]{1,0:T(8,128)(2,1)}, u32[]{:S(2)}, u32[]{:S(2)}) collective-permute-start(bf16[1024,512]{1,0:T(8,128)(2,1)S(1)} %bitcast.78), channel_id=1, source_target_pairs={{0,128},{64,192},{128,0},{192,64},{256,384},{320,448},{384,256},{4... | collective-permute-start | bytes 3145736 | tf_op jit(solution)/shard_map/ppermute | solution.py:12
  51.4 7.6 %collective-permute-start.2 = (bf16[2,1040,128]{2,1,0:T(8,128)(2,1)S(1)}, bf16[2,1040,128]{2,1,0:T(8,128)(2,1)S(1)}, u32[]{:S(2)}, u32[]{:S(2)}) collective-permute-start(bf16[2,1040,128]{2,1,0:T(8,128)(2,1)S(1)} %pad_maximum_fusion.1), channel_id=1, source_target_pairs={{0,64},{64,0},{128,192},{192,128},{256,320},{320,256},{384,448},{4... | collective-permute-start | bytes 1597448 | tf_op jit(solution)/shard_map/ppermute | solution.py:12
  59.0 4.6 %collective-permute-done.3 = bf16[1024,512]{1,0:T(8,128)(2,1)} collective-permute-done((bf16[1024,512]{1,0:T(8,128)(2,1)S(1)}, bf16[1024,512]{1,0:T(8,128)(2,1)}, u32[]{:S(2)}, u32[]{:S(2)}) %collective-permute-start.3) | collective-permute-done | bytes 1048608 | tf_op jit(solution)/shard_map/ppermute | solution.py:12
  63.6 1.5 add_convert_fusion
  65.1 0.4 convolution_convert_fusion
  65.6 0.5 convolution_bitcast_fusion
  66.1 14.9 %collective-permute-start.4 = (f32[512,256]{0,1:T(8,128)S(1)}, f32[512,256]{0,1:T(8,128)}, u32[]{:S(2)}, u32[]{:S(2)}) collective-permute-start(f32[512,256]{0,1:T(8,128)S(1)} %convolution_bitcast_fusion), channel_id=1, source_target_pairs={{0,1},{1,0},{2,3},{3,2},{4,5},{5,4},{6,7},{7,6},{8,9},{9,8},{10,11... | collective-permute-start | bytes 1572872 | tf_op jit(solution)/shard_map/ppermute | solution.py:12
  81.1 1.1 slice.77
  82.3 0.3 collective-permute-done.4
  82.6 1.8 %fusion.11 = f32[512,256]{0,1:T(8,128)S(1)} fusion(f32[512,256]{0,1:T(8,128)} %collective-permute-done.4, bf16[1024,512]{1,0:T(8,128)(2,1)} %param.15, bf16[1024,512]{1,0:T(8,128)(2,1)S(1)} %bitcast.77, s32[]{:T(128)S(6)} %select_n.42), kind=kOutput, calls=%fused_computation.16 | convolution fusion | flops 268566528 | bytes 2621444 | tf_op jit(solution)/shard_map/dot_general | solution.py:68
  84.5 0.1 copy.17
  84.6 0.1 copy.18
  84.9 0.2 tile.11
  85.3 63.1 %all_to_all.5 = bf16[64,96,128]{2,1,0:T(8,128)(2,1)S(1)} all-to-all(bf16[64,96,128]{2,1,0:T(8,128)(2,1)S(1)} %pad_maximum_fusion), channel_id=1, replica_groups=mesh['group'=8,'sub'=64] {'sub'}, dimensions={0} | all-to-all | bytes 3145728 | tf_op jit(solution)/shard_map/all_to_all | solution.py:81
  148.3 2.3 %collective-permute-start.5 = (bf16[64,96,128]{2,1,0:T(8,128)(2,1)S(1)}, bf16[64,96,128]{2,1,0:T(8,128)(2,1)}, u32[]{:S(2)}, u32[]{:S(2)}) collective-permute-start(bf16[64,96,128]{2,1,0:T(8,128)(2,1)S(1)} %all_to_all.5), channel_id=1, source_target_pairs={{0,1},{1,0},{2,3},{3,2},{4,5},{5,4},{6,7},{7,6},{8,9},{9,8},{10,11... | collective-permute-start | bytes 4718600 | tf_op jit(solution)/shard_map/ppermute | solution.py:12
  150.7 2.3 %copy.19 = bf16[32,128,128]{1,2,0:T(8,128)(2,1)} copy(bf16[32,128,128]{2,1,0:T(8,128)(2,1)} %bitcast.83) | data formatting | bytes 2097152 | tf_op jit(solution)/shard_map/optimization_barrier | solution.py:78
  153.1 0.9 slice_add_fusion
  154.0 1.7 %reduce_sum.9 = f32[2,2,8,128]{3,2,1,0:T(8,128)} reduce(f32[32,2,2,8,128]{4,3,2,1,0:T(8,128)} %bitcast.85, f32[]{:T(128)} %constant.79.clone.1), dimensions={0}, to_apply=%region_0.2 | reduce | flops 126976 | bytes 540676 | tf_op jit(solution)/shard_map/reduce_sum | solution.py:85
  155.7 1.5 gather_fusion
  157.2 2.1 %gather_fusion.1 = bf16[32,96,128]{2,1,0:T(8,128)(2,1)S(1)} fusion(bf16[64,96,128]{2,1,0:T(8,128)(2,1)} %collective-permute-done.5, s32[1024]{0:T(1024)S(1)} %pad_clamp_fusion), kind=kCustom, calls=%fused_computation.1.clone | custom fusion | bytes 1572992 | tf_op jit(solution)/shard_map/jit(_take)/gather | solution.py:90
  159.3 1.8 %convolution_bitcast_fusion.2 = f32[128,128]{1,0:T(8,128)S(1)} fusion(bf16[32,128,128]{1,2,0:T(8,128)(2,1)} %copy.19, pred[]{:T(512)S(6)} %eq.26, bf16[32,96,128]{2,1,0:T(8,128)(2,1)} %gather_fusion, pred[32]{0:T(512)(128)(4,1)S(1)} %compare_and_fusion, bf16[32,96,128]{2,1,0:T(8,128)(2,1)S(1)} %gather_fusion.1), kind=kOutput, calls=%fused_computation.17 | convolution fusion | flops 67895296 | bytes 1638913 | tf_op jit(solution)/shard_map/kab,kbm->am/dot_general | solution.py:95
  161.1 1.0 fusion.13
  (34 shorter events, 0.8 us)
Async XLA Ops:
  0.6 1.4 copy-start
  2.1 1.2 copy-start.6
  3.3 9.7 %copy-start.7 = (s32[8]{0:T(128)S(1)}, s32[8]{0:T(128)}, u32[]{:S(2)}) copy-start(s32[8]{0:T(128)} %param.17) | copy-start | bytes 100
  3.3 9.7 %copy-start.4 = (bf16[8,128,128]{2,1,0:T(8,128)(2,1)S(1)}, bf16[8,128,128]{2,1,0:T(8,128)(2,1)}, u32[]{:S(2)}) copy-start(bf16[8,128,128]{2,1,0:T(8,128)(2,1)} %param.16) | copy-start | bytes 786436
  4.5 42.7 %copy-start.5 = (bf16[2,128,128]{2,1,0:T(8,128)(2,1)S(1)}, bf16[2,128,128]{2,1,0:T(8,128)(2,1)}, u32[]{:S(2)}) copy-start(bf16[2,128,128]{2,1,0:T(8,128)(2,1)} %param.14) | copy-start | bytes 196612
  4.5 42.4 %collective-permute-start.1 = (bf16[1024,512]{1,0:T(8,128)(2,1)S(1)}, bf16[1024,512]{1,0:T(8,128)(2,1)S(1)}, u32[]{:S(2)}, u32[]{:S(2)}) collective-permute-start(bf16[1024,512]{1,0:T(8,128)(2,1)S(1)} %fusion.8), channel_id=1, source_target_pairs={{0,64},{64,0},{128,192},{192,128},{256,320},{320,256},{384,448},{4... | collective-permute-start | bytes 3145736 | tf_op jit(solution)/shard_map/ppermute | solution.py:12
  13.0 34.2 %collective-permute-start = (bf16[1,1040,128]{2,1,0:T(8,128)(2,1)S(1)}, bf16[1,1040,128]{2,1,0:T(8,128)(2,1)S(1)}, u32[]{:S(2)}, u32[]{:S(2)}) collective-permute-start(bf16[1,1040,128]{2,1,0:T(8,128)(2,1)S(1)} %fusion.25), channel_id=1, source_target_pairs={{0,128},{64,192},{128,0},{192,64},{256,384},{320,448},{384,256},{4... | collective-permute-start | bytes 798728 | tf_op jit(solution)/shard_map/ppermute | solution.py:12
  47.7 15.9 %collective-permute-start.3 = (bf16[1024,512]{1,0:T(8,128)(2,1)S(1)}, bf16[1024,512]{1,0:T(8,128)(2,1)}, u32[]{:S(2)}, u32[]{:S(2)}) collective-permute-start(bf16[1024,512]{1,0:T(8,128)(2,1)S(1)} %bitcast.78), channel_id=1, source_target_pairs={{0,128},{64,192},{128,0},{192,64},{256,384},{320,448},{384,256},{4... | collective-permute-start | bytes 3145736 | tf_op jit(solution)/shard_map/ppermute | solution.py:12
  51.4 14.1 %copy-start.1 = (bf16[1024,512]{1,0:T(8,128)(2,1)S(1)}, bf16[1024,512]{1,0:T(8,128)(2,1)}, u32[]{:S(2)}) copy-start(bf16[1024,512]{1,0:T(8,128)(2,1)} %param.15) | copy-start | bytes 3145732
  51.4 29.5 %collective-permute-start.2 = (bf16[2,1040,128]{2,1,0:T(8,128)(2,1)S(1)}, bf16[2,1040,128]{2,1,0:T(8,128)(2,1)S(1)}, u32[]{:S(2)}, u32[]{:S(2)}) collective-permute-start(bf16[2,1040,128]{2,1,0:T(8,128)(2,1)S(1)} %pad_maximum_fusion.1), channel_id=1, source_target_pairs={{0,64},{64,0},{128,192},{192,128},{256,320},{320,256},{384,448},{4... | collective-permute-start | bytes 1597448 | tf_op jit(solution)/shard_map/ppermute | solution.py:12
  66.1 16.5 %collective-permute-start.4 = (f32[512,256]{0,1:T(8,128)S(1)}, f32[512,256]{0,1:T(8,128)}, u32[]{:S(2)}, u32[]{:S(2)}) collective-permute-start(f32[512,256]{0,1:T(8,128)S(1)} %convolution_bitcast_fusion), channel_id=1, source_target_pairs={{0,1},{1,0},{2,3},{3,2},{4,5},{5,4},{6,7},{7,6},{8,9},{9,8},{10,11... | collective-permute-start | bytes 1572872 | tf_op jit(solution)/shard_map/ppermute | solution.py:12
  148.3 8.8 %collective-permute-start.5 = (bf16[64,96,128]{2,1,0:T(8,128)(2,1)S(1)}, bf16[64,96,128]{2,1,0:T(8,128)(2,1)}, u32[]{:S(2)}, u32[]{:S(2)}) collective-permute-start(bf16[64,96,128]{2,1,0:T(8,128)(2,1)S(1)} %all_to_all.5), channel_id=1, source_target_pairs={{0,1},{1,0},{2,3},{3,2},{4,5},{5,4},{6,7},{7,6},{8,9},{9,8},{10,11... | collective-permute-start | bytes 4718600 | tf_op jit(solution)/shard_map/ppermute | solution.py:12
  159.3 1.8 %copy-start.2 = (bf16[32,128,128]{1,2,0:T(8,128)(2,1)S(1)}, bf16[32,128,128]{1,2,0:T(8,128)(2,1)}, u32[]{:S(2)}) copy-start(bf16[32,128,128]{1,2,0:T(8,128)(2,1)} %copy.19) | copy-start | bytes 3145732
  159.3 1.8 %copy-start.3 = (bf16[32,96,128]{2,1,0:T(8,128)(2,1)S(1)}, bf16[32,96,128]{2,1,0:T(8,128)(2,1)}, u32[]{:S(2)}) copy-start(bf16[32,96,128]{2,1,0:T(8,128)(2,1)} %gather_fusion) | copy-start | bytes 2359300

commit v13 on v10

--- a/solution.py
+++ b/solution.py
@@ -39,7 +39,13 @@
     panel = jnp.dot(dense, modes, preferred_element_type=jnp.float32).astype(jnp.bfloat16)
     carried = packed[None]
     for level in range(levels):
-        sibling = from_partner(panel, "group", 2**level)
+        if level == 0:
+            sibling = from_partner(panel, "group", 2**level)
+        else:
+            rows_half = panel.shape[0] // 2
+            sibling = jnp.concatenate(
+                [from_partner(panel[:rows_half], "group", 2**level), from_partner(panel[rows_half:], "group", 2**level)]
+            )
         partner = levels - 1 - level
         carried, panel = lax.optimization_barrier((carried, panel))
         arrived = from_partner(carried, "group", 2**partner)

time: 162 us -> 166 us (1.025)
  starting transfers between devices: 63.8 us -> 67.8 us
  waiting for transfers between devices: 73 us -> 70 us
    ppermute x6 -> x7, waiting for transfers between devices: 36.7 us -> 33.7 us  [from_partner(): return lax.ppermute(value, axis, pairs)]
    ppermute x6 -> x7, starting transfers between devices: 40 us -> 42.2 us  [from_partner(): return lax.ppermute(value, axis, pairs)]
    all_to_all x1, starting transfers between devices: 23.9 us -> 25.7 us  [on_device(): arrived = lax.all_to_all(outgoing, 'sub', 0, 0, tiled=True)]
  transfers between devices with their start and end apart: 7 -> 8, of which waited for: 4 -> 4; matrix products, arithmetic and copies ran while one was open for 6% -> 6% of each run, Pallas kernels for 0% -> 0%
where the time goes in v13:
time: 166 us; the launch traced here: 163 us
  waiting for transfers between devices  70 us (42%)
  starting transfers between devices  67.8 us (41%)
  local copies, waits for them, and re-layouts  11.3 us (7%)
  matrix products  6.88 us (4%)
  other arithmetic  5.73 us (3%)
    ppermute x7, starting transfers between devices, from_partner(): return lax.ppermute(value, axis, pairs)  42.2 us
    all_to_all x1, waiting for transfers between devices, on_device(): arrived = lax.all_to_all(outgoing, 'sub', 0, 0, tiled=True)  36.3 us
    ppermute x7, waiting for transfers between devices, from_partner(): return lax.ppermute(value, axis, pairs)  33.7 us
    all_to_all x1, starting transfers between devices, on_device(): arrived = lax.all_to_all(outgoing, 'sub', 0, 0, tiled=True)  25.7 us
  transfers between devices with their start and end apart: 8, of which 4 were waited for; matrix products, arithmetic and copies ran while one was open for 6% of the time, Pallas kernels for 0%

profile of v13, /device:TPU:1, one launch (start us, length us, event | category | flops | bytes accessed | tf_op | source)
XLA Modules:
  0.0 162.9 jit_solution(16702997294515843417)
XLA Ops:
  0.6 0.8 eq.22
  1.5 0.6 copy-done
  2.1 1.0 fusion.5
  3.3 1.2 fusion.8
  4.5 8.4 %collective-permute-start.1 = (bf16[1024,512]{1,0:T(8,128)(2,1)S(1)}, bf16[1024,512]{1,0:T(8,128)(2,1)S(1)}, u32[]{:S(2)}, u32[]{:S(2)}) collective-permute-start(bf16[1024,512]{1,0:T(8,128)(2,1)S(1)} %fusion.8), channel_id=1, source_target_pairs={{0,64},{64,0},{128,192},{192,128},{256,320},{320,256},{384,448},{4... | collective-permute-start | bytes 3145736 | tf_op jit(solution)/shard_map/ppermute | solution.py:12
  13.0 3.1 %collective-permute-start = (bf16[1,1040,128]{2,1,0:T(8,128)(2,1)S(1)}, bf16[1,1040,128]{2,1,0:T(8,128)(2,1)S(1)}, u32[]{:S(2)}, u32[]{:S(2)}) collective-permute-start(bf16[1,1040,128]{2,1,0:T(8,128)(2,1)S(1)} %fusion.25), channel_id=1, source_target_pairs={{0,128},{64,192},{128,0},{192,64},{256,384},{320,448},{384,256},{4... | collective-permute-start | bytes 798728 | tf_op jit(solution)/shard_map/ppermute | solution.py:12
  16.1 30.8 %collective-permute-done.1 = bf16[1024,512]{1,0:T(8,128)(2,1)S(1)} collective-permute-done((bf16[1024,512]{1,0:T(8,128)(2,1)S(1)}, bf16[1024,512]{1,0:T(8,128)(2,1)S(1)}, u32[]{:S(2)}, u32[]{:S(2)}) %collective-permute-start.1) | collective-permute-done | bytes 1048608 | tf_op jit(solution)/shard_map/ppermute | solution.py:12
  47.3 0.4 convolution_convert_fusion.1
  47.7 1.0 fusion.40
  48.7 3.6 %collective-permute-start.4 = (bf16[512,512]{1,0:T(8,128)(2,1)}, bf16[512,512]{1,0:T(8,128)(2,1)S(1)}, u32[]{:S(2)}, u32[]{:S(2)}) collective-permute-start(bf16[512,512]{1,0:T(8,128)(2,1)} %bitcast.14), channel_id=1, source_target_pairs={{0,128},{64,192},{128,0},{192,64},{256,384},{320,448},{384,256},{4... | collective-permute-start | bytes 1572872 | tf_op jit(solution)/shard_map/ppermute | solution.py:12
  52.4 1.9 %collective-permute-start.3 = (bf16[512,512]{1,0:T(8,128)(2,1)}, bf16[512,512]{1,0:T(8,128)(2,1)}, u32[]{:S(2)}, u32[]{:S(2)}) collective-permute-start(bf16[512,512]{1,0:T(8,128)(2,1)} %bitcast.13), channel_id=1, source_target_pairs={{0,128},{64,192},{128,0},{192,64},{256,384},{320,448},{384,256},{4... | collective-permute-start | bytes 1572872 | tf_op jit(solution)/shard_map/ppermute | solution.py:12
  54.3 1.0 pad_maximum_fusion.1
  55.4 7.9 %collective-permute-start.2 = (bf16[2,1040,128]{2,1,0:T(8,128)(2,1)S(1)}, bf16[2,1040,128]{2,1,0:T(8,128)(2,1)S(1)}, u32[]{:S(2)}, u32[]{:S(2)}) collective-permute-start(bf16[2,1040,128]{2,1,0:T(8,128)(2,1)S(1)} %pad_maximum_fusion.1), channel_id=1, source_target_pairs={{0,64},{64,0},{128,192},{192,128},{256,320},{320,256},{384,448},{4... | collective-permute-start | bytes 1597448 | tf_op jit(solution)/shard_map/ppermute | solution.py:12
  63.3 1.6 collective-permute-done.3
  64.9 1.4 add_convert_fusion
  66.2 0.4 convolution_convert_fusion
  66.7 0.5 convolution_bitcast_fusion
  67.1 14.9 %collective-permute-start.5 = (f32[512,256]{0,1:T(8,128)S(1)}, f32[512,256]{0,1:T(8,128)S(1)}, u32[]{:S(2)}, u32[]{:S(2)}) collective-permute-start(f32[512,256]{0,1:T(8,128)S(1)} %convolution_bitcast_fusion), channel_id=1, source_target_pairs={{0,1},{1,0},{2,3},{3,2},{4,5},{5,4},{6,7},{7,6},{8,9},{9,8},{10,11... | collective-permute-start | bytes 1572872 | tf_op jit(solution)/shard_map/ppermute | solution.py:12
  82.2 1.3 collective-permute-done.5
  83.5 0.5 fusion.11
  84.8 1.3 pad_maximum_fusion
  86.1 25.7 %all-to-all-start = ((bf16[64,96,128]{2,1,0:T(8,128)(2,1)}), bf16[64,96,128]{2,1,0:T(8,128)(2,1)S(1)}, u32[]{:S(2)}, u32[]{:S(2)}) async-start(bf16[64,96,128]{2,1,0:T(8,128)(2,1)} %pad_maximum_fusion), calls=%async_computation | async-start | bytes 3145728 | tf_op jit(solution)/shard_map/all_to_all | solution.py:87
  111.8 2.3 %slice.89 = bf16[4,1024,128]{2,1,0:T(8,128)(2,1)} slice(bf16[4,1040,128]{2,1,0:T(8,128)(2,1)} %copy-done.2), slice={[0:4], [0:1024], [0:128]} | slice | bytes 2097152 | tf_op jit(solution)/shard_map/slice | solution.py:67
  114.0 0.7 fusion.35
  114.8 36.3 %all-to-all-done = bf16[64,96,128]{2,1,0:T(8,128)(2,1)S(1)} async-done(((bf16[64,96,128]{2,1,0:T(8,128)(2,1)}), bf16[64,96,128]{2,1,0:T(8,128)(2,1)S(1)}, u32[]{:S(2)}, u32[]{:S(2)}) %all-to-all-start) | async-done | bytes 1572896 | tf_op jit(solution)/shard_map/all_to_all | solution.py:87
  151.1 1.1 slice.97
  152.3 2.3 %collective-permute-start.6 = (bf16[64,64,128]{2,1,0:T(8,128)(2,1)}, bf16[64,64,128]{2,1,0:T(8,128)(2,1)}, u32[]{:S(2)}, u32[]{:S(2)}) collective-permute-start(bf16[64,64,128]{2,1,0:T(8,128)(2,1)} %slice.97), channel_id=1, source_target_pairs={{0,1},{1,0},{2,3},{3,2},{4,5},{5,4},{6,7},{7,6},{8,9},{9,8},{10,11... | collective-permute-start | bytes 3145736 | tf_op jit(solution)/shard_map/ppermute | solution.py:12
  154.7 2.7 %gather_fusion = bf16[32,64,128]{2,1,0:T(8,128)(2,1)} fusion(bf16[64,64,128]{2,1,0:T(8,128)(2,1)} %slice.97, s32[1024]{0:T(1024)S(1)} %pad_clamp_fusion), kind=kCustom, calls=%fused_computation.clone | custom fusion | bytes 1048704 | tf_op jit(solution)/shard_map/jit(_take)/gather | solution.py:95
  157.5 0.7 reduce_sum.9
  158.2 1.9 %gather_fusion.1 = bf16[32,64,128]{2,1,0:T(8,128)(2,1)S(1)} fusion(bf16[64,64,128]{2,1,0:T(8,128)(2,1)} %collective-permute-done.6, s32[1024]{0:T(1024)S(1)} %pad_clamp_fusion), kind=kCustom, calls=%fused_computation.1.clone | custom fusion | bytes 1048704 | tf_op jit(solution)/shard_map/jit(_take)/gather | solution.py:96
  160.1 1.8 %convolution_bitcast_fusion.2 = f32[128,128]{1,0:T(8,128)S(1)} fusion(bf16[32,128,128]{2,1,0:T(8,128)(2,1)S(1)} %bitcast.87, pred[]{:T(512)S(6)} %eq.26, bf16[32,64,128]{2,1,0:T(8,128)(2,1)} %gather_fusion, pred[32]{0:T(512)(128)(4,1)S(1)} %compare_and_fusion, bf16[32,64,128]{2,1,0:T(8,128)(2,1)S(1)} %gather_fusion.1), kind=kOutput, calls=%fused_computation.17 | convolution fusion | flops 67895296 | bytes 2162721 | tf_op jit(solution)/shard_map/kab,kbm->am/dot_general | solution.py:101
  161.9 1.0 fusion.13
  (42 shorter events, 1.7 us)
Async XLA Ops:
  0.6 1.4 copy-start
  2.1 1.2 copy-start.8
  3.3 9.7 %copy-start.9 = (s32[8]{0:T(128)S(1)}, s32[8]{0:T(128)}, u32[]{:S(2)}) copy-start(s32[8]{0:T(128)} %param.17) | copy-start | bytes 100
  3.3 9.7 %copy-start.6 = (bf16[8,128,128]{2,1,0:T(8,128)(2,1)S(1)}, bf16[8,128,128]{2,1,0:T(8,128)(2,1)}, u32[]{:S(2)}) copy-start(bf16[8,128,128]{2,1,0:T(8,128)(2,1)} %param.16) | copy-start | bytes 786436
  4.5 42.7 %copy-start.7 = (bf16[2,128,128]{2,1,0:T(8,128)(2,1)S(1)}, bf16[2,128,128]{2,1,0:T(8,128)(2,1)}, u32[]{:S(2)}) copy-start(bf16[2,128,128]{2,1,0:T(8,128)(2,1)} %param.14) | copy-start | bytes 196612
  4.5 42.4 %collective-permute-start.1 = (bf16[1024,512]{1,0:T(8,128)(2,1)S(1)}, bf16[1024,512]{1,0:T(8,128)(2,1)S(1)}, u32[]{:S(2)}, u32[]{:S(2)}) collective-permute-start(bf16[1024,512]{1,0:T(8,128)(2,1)S(1)} %fusion.8), channel_id=1, source_target_pairs={{0,64},{64,0},{128,192},{192,128},{256,320},{320,256},{384,448},{4... | collective-permute-start | bytes 3145736 | tf_op jit(solution)/shard_map/ppermute | solution.py:12
  13.0 34.2 %collective-permute-start = (bf16[1,1040,128]{2,1,0:T(8,128)(2,1)S(1)}, bf16[1,1040,128]{2,1,0:T(8,128)(2,1)S(1)}, u32[]{:S(2)}, u32[]{:S(2)}) collective-permute-start(bf16[1,1040,128]{2,1,0:T(8,128)(2,1)S(1)} %fusion.25), channel_id=1, source_target_pairs={{0,128},{64,192},{128,0},{192,64},{256,384},{320,448},{384,256},{4... | collective-permute-start | bytes 798728 | tf_op jit(solution)/shard_map/ppermute | solution.py:12
  47.3 1.5 copy-start.5
  48.7 14.5 %collective-permute-start.4 = (bf16[512,512]{1,0:T(8,128)(2,1)}, bf16[512,512]{1,0:T(8,128)(2,1)S(1)}, u32[]{:S(2)}, u32[]{:S(2)}) collective-permute-start(bf16[512,512]{1,0:T(8,128)(2,1)} %bitcast.14), channel_id=1, source_target_pairs={{0,128},{64,192},{128,0},{192,64},{256,384},{320,448},{384,256},{4... | collective-permute-start | bytes 1572872 | tf_op jit(solution)/shard_map/ppermute | solution.py:12
  52.4 12.5 %collective-permute-start.3 = (bf16[512,512]{1,0:T(8,128)(2,1)}, bf16[512,512]{1,0:T(8,128)(2,1)}, u32[]{:S(2)}, u32[]{:S(2)}) collective-permute-start(bf16[512,512]{1,0:T(8,128)(2,1)} %bitcast.13), channel_id=1, source_target_pairs={{0,128},{64,192},{128,0},{192,64},{256,384},{320,448},{384,256},{4... | collective-permute-start | bytes 1572872 | tf_op jit(solution)/shard_map/ppermute | solution.py:12
  55.3 11.3 %copy-start.1 = (bf16[1024,512]{1,0:T(8,128)(2,1)S(1)}, bf16[1024,512]{1,0:T(8,128)(2,1)}, u32[]{:S(2)}) copy-start(bf16[1024,512]{1,0:T(8,128)(2,1)} %param.15) | copy-start | bytes 3145732
  55.4 26.7 %collective-permute-start.2 = (bf16[2,1040,128]{2,1,0:T(8,128)(2,1)S(1)}, bf16[2,1040,128]{2,1,0:T(8,128)(2,1)S(1)}, u32[]{:S(2)}, u32[]{:S(2)}) collective-permute-start(bf16[2,1040,128]{2,1,0:T(8,128)(2,1)S(1)} %pad_maximum_fusion.1), channel_id=1, source_target_pairs={{0,64},{64,0},{128,192},{192,128},{256,320},{320,256},{384,448},{4... | collective-permute-start | bytes 1597448 | tf_op jit(solution)/shard_map/ppermute | solution.py:12
  67.1 16.4 %collective-permute-start.5 = (f32[512,256]{0,1:T(8,128)S(1)}, f32[512,256]{0,1:T(8,128)S(1)}, u32[]{:S(2)}, u32[]{:S(2)}) collective-permute-start(f32[512,256]{0,1:T(8,128)S(1)} %convolution_bitcast_fusion), channel_id=1, source_target_pairs={{0,1},{1,0},{2,3},{3,2},{4,5},{5,4},{6,7},{7,6},{8,9},{9,8},{10,11... | collective-permute-start | bytes 1572872 | tf_op jit(solution)/shard_map/ppermute | solution.py:12
  82.2 1.8 %copy-start.2 = (bf16[4,1040,128]{2,1,0:T(8,128)(2,1)}, bf16[4,1040,128]{2,1,0:T(8,128)(2,1)S(1)}, u32[]{:S(2)}) copy-start(bf16[4,1040,128]{2,1,0:T(8,128)(2,1)S(1)} %constant_dynamic-update-slice_fusion) | copy-start | bytes 3194884
  86.1 65.1 %all-to-all-start = ((bf16[64,96,128]{2,1,0:T(8,128)(2,1)}), bf16[64,96,128]{2,1,0:T(8,128)(2,1)S(1)}, u32[]{:S(2)}, u32[]{:S(2)}) async-start(bf16[64,96,128]{2,1,0:T(8,128)(2,1)} %pad_maximum_fusion), calls=%async_computation | async-start | bytes 3145728 | tf_op jit(solution)/shard_map/all_to_all | solution.py:87
  152.3 5.9 %collective-permute-start.6 = (bf16[64,64,128]{2,1,0:T(8,128)(2,1)}, bf16[64,64,128]{2,1,0:T(8,128)(2,1)}, u32[]{:S(2)}, u32[]{:S(2)}) collective-permute-start(bf16[64,64,128]{2,1,0:T(8,128)(2,1)} %slice.97), channel_id=1, source_target_pairs={{0,1},{1,0},{2,3},{3,2},{4,5},{5,4},{6,7},{7,6},{8,9},{9,8},{10,11... | collective-permute-start | bytes 3145736 | tf_op jit(solution)/shard_map/ppermute | solution.py:12
  157.4 2.6 %copy-start.3 = (bf16[4,1024,128]{2,1,0:T(8,128)(2,1)S(1)}, bf16[4,1024,128]{2,1,0:T(8,128)(2,1)}, u32[]{:S(2)}) copy-start(bf16[4,1024,128]{2,1,0:T(8,128)(2,1)} %slice.89) | copy-start | bytes 3145732
  160.0 1.8 %copy-start.4 = (bf16[32,64,128]{2,1,0:T(8,128)(2,1)S(1)}, bf16[32,64,128]{2,1,0:T(8,128)(2,1)}, u32[]{:S(2)}) copy-start(bf16[32,64,128]{2,1,0:T(8,128)(2,1)} %gather_fusion) | copy-start | bytes 1572868

commit v14 on v10

--- a/solution.py
+++ b/solution.py
@@ -90,9 +90,8 @@
     picked_theirs = jnp.take(theirs, rows_all, axis=0)
     picked_low = jnp.where(core == 0, picked_mine, picked_theirs)
     picked_high = jnp.where(core == 0, picked_theirs, picked_mine)
-    parent_sum = jnp.einsum(
-        "kab,kbm->am", vals_all[:, :, :half_rows], picked_low, preferred_element_type=jnp.float32
-    ) + jnp.einsum("kab,kbm->am", vals_all[:, :, half_rows:], picked_high, preferred_element_type=jnp.float32)
+    picked = jnp.concatenate([picked_low, picked_high], axis=1)
+    parent_sum = jnp.einsum("kab,kbm->am", vals_all, picked, preferred_element_type=jnp.float32)
     parent_out = parent_sum.astype(jnp.bfloat16)
     return (parent_out, projected)
 

time: 162 us -> 161 us (level)
  matrix products: 6.89 us -> 5.11 us
    dot_general x2 -> x1, matrix products: 2.82 us -> 1.04 us  [on_device(): jnp.einsum('kab,kbm->am', vals_all, picked, preferred_element_type=jnp.fl...]
where the time goes in v14:
time: 161 us; the launch traced here: 159 us
  waiting for transfers between devices  73 us (45%)
  starting transfers between devices  63.8 us (40%)
  local copies, waits for them, and re-layouts  11.3 us (7%)
  matrix products  5.11 us (3%)
  other arithmetic  5.09 us (3%)
    ppermute x6, starting transfers between devices, from_partner(): return lax.ppermute(value, axis, pairs)  40 us
    ppermute x6, waiting for transfers between devices, from_partner(): return lax.ppermute(value, axis, pairs)  36.7 us
    all_to_all x1, waiting for transfers between devices, on_device(): arrived = lax.all_to_all(outgoing, 'sub', 0, 0, tiled=True)  36.3 us
    all_to_all x1, starting transfers between devices, on_device(): arrived = lax.all_to_all(outgoing, 'sub', 0, 0, tiled=True)  23.9 us
  transfers between devices with their start and end apart: 7, of which 4 were waited for; matrix products, arithmetic and copies ran while one was open for 6% of the time, Pallas kernels for 0%

profile of v14, /device:TPU:1, one launch (start us, length us, event | category | flops | bytes accessed | tf_op | source)
XLA Modules:
  0.0 159.4 jit_solution(2581526553008557640)
XLA Ops:
  0.6 0.8 eq.22
  1.5 0.6 copy-done
  2.1 1.0 fusion.5
  3.1 0.2 copy-done.7
  3.3 1.2 fusion.8
  4.5 8.4 %collective-permute-start.1 = (bf16[1024,512]{1,0:T(8,128)(2,1)S(1)}, bf16[1024,512]{1,0:T(8,128)(2,1)S(1)}, u32[]{:S(2)}, u32[]{:S(2)}) collective-permute-start(bf16[1024,512]{1,0:T(8,128)(2,1)S(1)} %fusion.8), channel_id=1, source_target_pairs={{0,64},{64,0},{128,192},{192,128},{256,320},{320,256},{384,448},{4... | collective-permute-start | bytes 3145736 | tf_op jit(solution)/shard_map/ppermute | solution.py:12
  13.0 3.1 %collective-permute-start = (bf16[1,1040,128]{2,1,0:T(8,128)(2,1)S(1)}, bf16[1,1040,128]{2,1,0:T(8,128)(2,1)S(1)}, u32[]{:S(2)}, u32[]{:S(2)}) collective-permute-start(bf16[1,1040,128]{2,1,0:T(8,128)(2,1)S(1)} %fusion.21), channel_id=1, source_target_pairs={{0,128},{64,192},{128,0},{192,64},{256,384},{320,448},{384,256},{4... | collective-permute-start | bytes 798728 | tf_op jit(solution)/shard_map/ppermute | solution.py:12
  16.1 30.8 %collective-permute-done.1 = bf16[1024,512]{1,0:T(8,128)(2,1)S(1)} collective-permute-done((bf16[1024,512]{1,0:T(8,128)(2,1)S(1)}, bf16[1024,512]{1,0:T(8,128)(2,1)S(1)}, u32[]{:S(2)}, u32[]{:S(2)}) %collective-permute-start.1) | collective-permute-done | bytes 1048608 | tf_op jit(solution)/shard_map/ppermute | solution.py:12
  46.9 0.3 add_convert_fusion.1
  47.3 0.4 convolution_convert_fusion.1
  47.7 3.6 %collective-permute-start.3 = (bf16[1024,512]{1,0:T(8,128)(2,1)S(1)}, bf16[1024,512]{1,0:T(8,128)(2,1)}, u32[]{:S(2)}, u32[]{:S(2)}) collective-permute-start(bf16[1024,512]{1,0:T(8,128)(2,1)S(1)} %bitcast.75), channel_id=1, source_target_pairs={{0,128},{64,192},{128,0},{192,64},{256,384},{320,448},{384,256},{4... | collective-permute-start | bytes 3145736 | tf_op jit(solution)/shard_map/ppermute | solution.py:12
  51.4 7.6 %collective-permute-start.2 = (bf16[2,1040,128]{2,1,0:T(8,128)(2,1)S(1)}, bf16[2,1040,128]{2,1,0:T(8,128)(2,1)S(1)}, u32[]{:S(2)}, u32[]{:S(2)}) collective-permute-start(bf16[2,1040,128]{2,1,0:T(8,128)(2,1)S(1)} %pad_maximum_fusion.1), channel_id=1, source_target_pairs={{0,64},{64,0},{128,192},{192,128},{256,320},{320,256},{384,448},{4... | collective-permute-start | bytes 1597448 | tf_op jit(solution)/shard_map/ppermute | solution.py:12
  59.0 4.6 %collective-permute-done.3 = bf16[1024,512]{1,0:T(8,128)(2,1)} collective-permute-done((bf16[1024,512]{1,0:T(8,128)(2,1)S(1)}, bf16[1024,512]{1,0:T(8,128)(2,1)}, u32[]{:S(2)}, u32[]{:S(2)}) %collective-permute-start.3) | collective-permute-done | bytes 1048608 | tf_op jit(solution)/shard_map/ppermute | solution.py:12
  63.6 1.5 add_convert_fusion
  65.1 0.4 convolution_convert_fusion
  65.6 0.5 convolution_bitcast_fusion
  66.1 14.9 %collective-permute-start.4 = (f32[512,256]{0,1:T(8,128)S(1)}, f32[512,256]{0,1:T(8,128)S(1)}, u32[]{:S(2)}, u32[]{:S(2)}) collective-permute-start(f32[512,256]{0,1:T(8,128)S(1)} %convolution_bitcast_fusion), channel_id=1, source_target_pairs={{0,1},{1,0},{2,3},{3,2},{4,5},{5,4},{6,7},{7,6},{8,9},{9,8},{10,11... | collective-permute-start | bytes 1572872 | tf_op jit(solution)/shard_map/ppermute | solution.py:12
  81.1 1.3 collective-permute-done.4
  82.4 0.5 fusion.11
  83.4 0.2 tile.11
  83.7 1.3 pad_maximum_fusion
  85.0 23.9 %all-to-all-start = ((bf16[64,96,128]{2,1,0:T(8,128)(2,1)}), bf16[64,96,128]{2,1,0:T(8,128)(2,1)S(1)}, u32[]{:S(2)}, u32[]{:S(2)}) async-start(bf16[64,96,128]{2,1,0:T(8,128)(2,1)} %pad_maximum_fusion), calls=%async_computation | async-start | bytes 3145728 | tf_op jit(solution)/shard_map/all_to_all | solution.py:81
  108.9 2.3 %slice.65 = bf16[4,1024,128]{2,1,0:T(8,128)(2,1)} slice(bf16[4,1040,128]{2,1,0:T(8,128)(2,1)} %copy-done.2), slice={[0:4], [0:1024], [0:128]} | slice | bytes 2097152 | tf_op jit(solution)/shard_map/slice | solution.py:61
  111.1 0.7 fusion.31
  111.9 36.3 %all-to-all-done = bf16[64,96,128]{2,1,0:T(8,128)(2,1)S(1)} async-done(((bf16[64,96,128]{2,1,0:T(8,128)(2,1)}), bf16[64,96,128]{2,1,0:T(8,128)(2,1)S(1)}, u32[]{:S(2)}, u32[]{:S(2)}) %all-to-all-start) | async-done | bytes 1572896 | tf_op jit(solution)/shard_map/all_to_all | solution.py:81
  148.2 1.1 slice.70
  149.4 2.3 %collective-permute-start.5 = (bf16[64,64,128]{2,1,0:T(8,128)(2,1)}, bf16[64,64,128]{2,1,0:T(8,128)(2,1)}, u32[]{:S(2)}, u32[]{:S(2)}) collective-permute-start(bf16[64,64,128]{2,1,0:T(8,128)(2,1)} %slice.70), channel_id=1, source_target_pairs={{0,1},{1,0},{2,3},{3,2},{4,5},{5,4},{6,7},{7,6},{8,9},{9,8},{10,11... | collective-permute-start | bytes 3145736 | tf_op jit(solution)/shard_map/ppermute | solution.py:12
  151.7 2.6 %gather_fusion = bf16[32,64,128]{2,1,0:T(8,128)(2,1)} fusion(bf16[64,64,128]{2,1,0:T(8,128)(2,1)} %slice.70, s32[1024]{0:T(1024)S(1)} %pad_clamp_fusion), kind=kCustom, calls=%fused_computation.clone | custom fusion | bytes 1048704 | tf_op jit(solution)/shard_map/jit(_take)/gather | solution.py:89
  154.6 0.7 reduce_sum.9
  155.2 1.9 %gather_fusion.1 = bf16[32,64,128]{2,1,0:T(8,128)(2,1)S(1)} fusion(bf16[64,64,128]{2,1,0:T(8,128)(2,1)} %collective-permute-done.5, s32[1024]{0:T(1024)S(1)} %pad_clamp_fusion), kind=kCustom, calls=%fused_computation.1.clone | custom fusion | bytes 1048704 | tf_op jit(solution)/shard_map/jit(_take)/gather | solution.py:90
  157.3 1.0 copy-done.4
  158.4 1.0 fusion.12
  (37 shorter events, 1.2 us)
Async XLA Ops:
  0.6 1.4 copy-start
  2.1 1.2 copy-start.7
  3.3 9.7 %copy-start.8 = (s32[8]{0:T(128)S(1)}, s32[8]{0:T(128)}, u32[]{:S(2)}) copy-start(s32[8]{0:T(128)} %param.17) | copy-start | bytes 100
  3.3 9.7 %copy-start.5 = (bf16[8,128,128]{2,1,0:T(8,128)(2,1)S(1)}, bf16[8,128,128]{2,1,0:T(8,128)(2,1)}, u32[]{:S(2)}) copy-start(bf16[8,128,128]{2,1,0:T(8,128)(2,1)} %param.16) | copy-start | bytes 786436
  4.5 42.7 %copy-start.6 = (bf16[2,128,128]{2,1,0:T(8,128)(2,1)S(1)}, bf16[2,128,128]{2,1,0:T(8,128)(2,1)}, u32[]{:S(2)}) copy-start(bf16[2,128,128]{2,1,0:T(8,128)(2,1)} %param.14) | copy-start | bytes 196612
  4.5 42.4 %collective-permute-start.1 = (bf16[1024,512]{1,0:T(8,128)(2,1)S(1)}, bf16[1024,512]{1,0:T(8,128)(2,1)S(1)}, u32[]{:S(2)}, u32[]{:S(2)}) collective-permute-start(bf16[1024,512]{1,0:T(8,128)(2,1)S(1)} %fusion.8), channel_id=1, source_target_pairs={{0,64},{64,0},{128,192},{192,128},{256,320},{320,256},{384,448},{4... | collective-permute-start | bytes 3145736 | tf_op jit(solution)/shard_map/ppermute | solution.py:12
  13.0 34.2 %collective-permute-start = (bf16[1,1040,128]{2,1,0:T(8,128)(2,1)S(1)}, bf16[1,1040,128]{2,1,0:T(8,128)(2,1)S(1)}, u32[]{:S(2)}, u32[]{:S(2)}) collective-permute-start(bf16[1,1040,128]{2,1,0:T(8,128)(2,1)S(1)} %fusion.21), channel_id=1, source_target_pairs={{0,128},{64,192},{128,0},{192,64},{256,384},{320,448},{384,256},{4... | collective-permute-start | bytes 798728 | tf_op jit(solution)/shard_map/ppermute | solution.py:12
  47.7 15.9 %collective-permute-start.3 = (bf16[1024,512]{1,0:T(8,128)(2,1)S(1)}, bf16[1024,512]{1,0:T(8,128)(2,1)}, u32[]{:S(2)}, u32[]{:S(2)}) collective-permute-start(bf16[1024,512]{1,0:T(8,128)(2,1)S(1)} %bitcast.75), channel_id=1, source_target_pairs={{0,128},{64,192},{128,0},{192,64},{256,384},{320,448},{384,256},{4... | collective-permute-start | bytes 3145736 | tf_op jit(solution)/shard_map/ppermute | solution.py:12
  51.4 14.1 %copy-start.1 = (bf16[1024,512]{1,0:T(8,128)(2,1)S(1)}, bf16[1024,512]{1,0:T(8,128)(2,1)}, u32[]{:S(2)}) copy-start(bf16[1024,512]{1,0:T(8,128)(2,1)} %param.15) | copy-start | bytes 3145732
  51.4 29.5 %collective-permute-start.2 = (bf16[2,1040,128]{2,1,0:T(8,128)(2,1)S(1)}, bf16[2,1040,128]{2,1,0:T(8,128)(2,1)S(1)}, u32[]{:S(2)}, u32[]{:S(2)}) collective-permute-start(bf16[2,1040,128]{2,1,0:T(8,128)(2,1)S(1)} %pad_maximum_fusion.1), channel_id=1, source_target_pairs={{0,64},{64,0},{128,192},{192,128},{256,320},{320,256},{384,448},{4... | collective-permute-start | bytes 1597448 | tf_op jit(solution)/shard_map/ppermute | solution.py:12
  66.1 16.4 %collective-permute-start.4 = (f32[512,256]{0,1:T(8,128)S(1)}, f32[512,256]{0,1:T(8,128)S(1)}, u32[]{:S(2)}, u32[]{:S(2)}) collective-permute-start(f32[512,256]{0,1:T(8,128)S(1)} %convolution_bitcast_fusion), channel_id=1, source_target_pairs={{0,1},{1,0},{2,3},{3,2},{4,5},{5,4},{6,7},{7,6},{8,9},{9,8},{10,11... | collective-permute-start | bytes 1572872 | tf_op jit(solution)/shard_map/ppermute | solution.py:12
  81.1 1.9 %copy-start.2 = (bf16[4,1040,128]{2,1,0:T(8,128)(2,1)}, bf16[4,1040,128]{2,1,0:T(8,128)(2,1)S(1)}, u32[]{:S(2)}) copy-start(bf16[4,1040,128]{2,1,0:T(8,128)(2,1)S(1)} %constant_dynamic-update-slice_fusion) | copy-start | bytes 3194884
  85.0 63.3 %all-to-all-start = ((bf16[64,96,128]{2,1,0:T(8,128)(2,1)}), bf16[64,96,128]{2,1,0:T(8,128)(2,1)S(1)}, u32[]{:S(2)}, u32[]{:S(2)}) async-start(bf16[64,96,128]{2,1,0:T(8,128)(2,1)} %pad_maximum_fusion), calls=%async_computation | async-start | bytes 3145728 | tf_op jit(solution)/shard_map/all_to_all | solution.py:81
  149.4 5.9 %collective-permute-start.5 = (bf16[64,64,128]{2,1,0:T(8,128)(2,1)}, bf16[64,64,128]{2,1,0:T(8,128)(2,1)}, u32[]{:S(2)}, u32[]{:S(2)}) collective-permute-start(bf16[64,64,128]{2,1,0:T(8,128)(2,1)} %slice.70), channel_id=1, source_target_pairs={{0,1},{1,0},{2,3},{3,2},{4,5},{5,4},{6,7},{7,6},{8,9},{9,8},{10,11... | collective-permute-start | bytes 3145736 | tf_op jit(solution)/shard_map/ppermute | solution.py:12
  154.5 2.6 %copy-start.3 = (bf16[32,64,128]{2,1,0:T(8,128)(2,1)S(1)}, bf16[32,64,128]{2,1,0:T(8,128)(2,1)}, u32[]{:S(2)}) copy-start(bf16[32,64,128]{2,1,0:T(8,128)(2,1)} %gather_fusion) | copy-start | bytes 1572868
  157.1 1.2 copy-start.4

commit v15 on v14

--- a/solution.py
+++ b/solution.py
@@ -36,10 +36,18 @@
         .reshape(row_blocks * block_size, vertex_blocks * block_size)
         .astype(jnp.bfloat16)
     )
-    panel = jnp.dot(dense, modes, preferred_element_type=jnp.float32).astype(jnp.bfloat16)
+    rows_half = dense.shape[0] // 2
+    panel_parts = [
+        jnp.dot(dense[i * rows_half : (i + 1) * rows_half], modes, preferred_element_type=jnp.float32).astype(jnp.bfloat16)
+        for i in range(2)
+    ]
+    panel = jnp.concatenate(panel_parts, axis=0)
     carried = packed[None]
     for level in range(levels):
-        sibling = from_partner(panel, "group", 2**level)
+        if level == 0:
+            sibling = jnp.concatenate([from_partner(p, "group", 2**level) for p in panel_parts], axis=0)
+        else:
+            sibling = from_partner(panel, "group", 2**level)
         partner = levels - 1 - level
         carried, panel = lax.optimization_barrier((carried, panel))
         arrived = from_partner(carried, "group", 2**partner)

time: 161 us -> 161 us (level)
  waiting for transfers between devices: 73 us -> 70.2 us
  starting transfers between devices: 63.8 us -> 65.7 us
    ppermute x6 -> x7, waiting for transfers between devices: 36.7 us -> 33.9 us  [from_partner(): return lax.ppermute(value, axis, pairs)]
    ppermute x6 -> x7, starting transfers between devices: 40 us -> 41.8 us  [from_partner(): return lax.ppermute(value, axis, pairs)]
  transfers between devices with their start and end apart: 7 -> 8, of which waited for: 4 -> 5; matrix products, arithmetic and copies ran while one was open for 6% -> 6% of each run, Pallas kernels for 0% -> 0%
where the time goes in v15:
time: 161 us; the launch traced here: 160 us
  waiting for transfers between devices  70.2 us (44%)
  starting transfers between devices  65.7 us (41%)
  local copies, waits for them, and re-layouts  12.4 us (8%)
  matrix products  5.29 us (3%)
  other arithmetic  5.16 us (3%)
    ppermute x7, starting transfers between devices, from_partner(): return lax.ppermute(value, axis, pairs)  41.8 us
    all_to_all x1, waiting for transfers between devices, on_device(): arrived = lax.all_to_all(outgoing, 'sub', 0, 0, tiled=True)  36.3 us
    ppermute x7, waiting for transfers between devices, from_partner(): return lax.ppermute(value, axis, pairs)  33.9 us
    all_to_all x1, starting transfers between devices, on_device(): arrived = lax.all_to_all(outgoing, 'sub', 0, 0, tiled=True)  23.9 us
  transfers between devices with their start and end apart: 8, of which 5 were waited for; matrix products, arithmetic and copies ran while one was open for 6% of the time, Pallas kernels for 0%

profile of v15, /device:TPU:1, one launch (start us, length us, event | category | flops | bytes accessed | tf_op | source)
XLA Modules:
  0.0 159.8 jit_solution(6377340962757518359)
XLA Ops:
  0.6 0.8 eq.22
  1.5 0.6 copy-done
  2.1 1.0 convert_bitcast_fusion
  3.3 1.1 copy-done.7
  4.3 0.7 convolution_convert_fusion.2
  5.0 8.3 %collective-permute-start.2 = (bf16[512,512]{1,0:T(8,128)(2,1)S(1)}, bf16[512,512]{1,0:T(8,128)(2,1)S(1)}, u32[]{:S(2)}, u32[]{:S(2)}) collective-permute-start(bf16[512,512]{1,0:T(8,128)(2,1)S(1)} %convolution_convert_fusion.2), channel_id=1, source_target_pairs={{0,64},{64,0},{128,192},{192,128},{256,320},{320,256},{384,448},{4... | collective-permute-start | bytes 1572872 | tf_op jit(solution)/shard_map/ppermute | solution.py:12
  13.3 0.7 convolution_convert_fusion.3
  14.1 1.9 %collective-permute-start.1 = (bf16[512,512]{1,0:T(8,128)(2,1)S(1)}, bf16[512,512]{1,0:T(8,128)(2,1)S(1)}, u32[]{:S(2)}, u32[]{:S(2)}) collective-permute-start(bf16[512,512]{1,0:T(8,128)(2,1)S(1)} %convolution_convert_fusion.3), channel_id=1, source_target_pairs={{0,64},{64,0},{128,192},{192,128},{256,320},{320,256},{384,448},{4... | collective-permute-start | bytes 1572872 | tf_op jit(solution)/shard_map/ppermute | solution.py:12
  16.1 3.1 %collective-permute-start = (bf16[1,1040,128]{2,1,0:T(8,128)(2,1)S(1)}, bf16[1,1040,128]{2,1,0:T(8,128)(2,1)S(1)}, u32[]{:S(2)}, u32[]{:S(2)}) collective-permute-start(bf16[1,1040,128]{2,1,0:T(8,128)(2,1)S(1)} %fusion.18), channel_id=1, source_target_pairs={{0,128},{64,192},{128,0},{192,64},{256,384},{320,448},{384,256},{4... | collective-permute-start | bytes 798728 | tf_op jit(solution)/shard_map/ppermute | solution.py:12
  19.3 8.4 %collective-permute-done.2 = bf16[512,512]{1,0:T(8,128)(2,1)S(1)} collective-permute-done((bf16[512,512]{1,0:T(8,128)(2,1)S(1)}, bf16[512,512]{1,0:T(8,128)(2,1)S(1)}, u32[]{:S(2)}, u32[]{:S(2)}) %collective-permute-start.2) | collective-permute-done | bytes 524320 | tf_op jit(solution)/shard_map/ppermute | solution.py:12
  27.7 19.6 %collective-permute-done.1 = bf16[512,512]{1,0:T(8,128)(2,1)S(1)} collective-permute-done((bf16[512,512]{1,0:T(8,128)(2,1)S(1)}, bf16[512,512]{1,0:T(8,128)(2,1)S(1)}, u32[]{:S(2)}, u32[]{:S(2)}) %collective-permute-start.1) | collective-permute-done | bytes 524320 | tf_op jit(solution)/shard_map/ppermute | solution.py:12
  48.0 3.7 %collective-permute-start.4 = (bf16[1024,512]{1,0:T(8,128)(2,1)S(1)}, bf16[1024,512]{1,0:T(8,128)(2,1)}, u32[]{:S(2)}, u32[]{:S(2)}) collective-permute-start(bf16[1024,512]{1,0:T(8,128)(2,1)S(1)} %bitcast.80), channel_id=1, source_target_pairs={{0,128},{64,192},{128,0},{192,64},{256,384},{320,448},{384,256},{4... | collective-permute-start | bytes 3145736 | tf_op jit(solution)/shard_map/ppermute | solution.py:12
  51.8 7.6 %collective-permute-start.3 = (bf16[2,1040,128]{2,1,0:T(8,128)(2,1)S(1)}, bf16[2,1040,128]{2,1,0:T(8,128)(2,1)S(1)}, u32[]{:S(2)}, u32[]{:S(2)}) collective-permute-start(bf16[2,1040,128]{2,1,0:T(8,128)(2,1)S(1)} %pad_maximum_fusion.2), channel_id=1, source_target_pairs={{0,64},{64,0},{128,192},{192,128},{256,320},{320,256},{384,448},{4... | collective-permute-start | bytes 1597448 | tf_op jit(solution)/shard_map/ppermute | solution.py:12
  59.4 4.6 %collective-permute-done.4 = bf16[1024,512]{1,0:T(8,128)(2,1)} collective-permute-done((bf16[1024,512]{1,0:T(8,128)(2,1)S(1)}, bf16[1024,512]{1,0:T(8,128)(2,1)}, u32[]{:S(2)}, u32[]{:S(2)}) %collective-permute-start.4) | collective-permute-done | bytes 1048608 | tf_op jit(solution)/shard_map/ppermute | solution.py:12
  64.0 1.5 add_convert_fusion
  65.5 0.4 convolution_convert_fusion
  66.0 0.5 convolution_bitcast_fusion
  66.4 14.8 %collective-permute-start.5 = (f32[512,256]{0,1:T(8,128)S(1)}, f32[512,256]{0,1:T(8,128)S(1)}, u32[]{:S(2)}, u32[]{:S(2)}) collective-permute-start(f32[512,256]{0,1:T(8,128)S(1)} %convolution_bitcast_fusion), channel_id=1, source_target_pairs={{0,1},{1,0},{2,3},{3,2},{4,5},{5,4},{6,7},{7,6},{8,9},{9,8},{10,11... | collective-permute-start | bytes 1572872 | tf_op jit(solution)/shard_map/ppermute | solution.py:12
  81.5 1.3 collective-permute-done.5
  82.8 0.5 fusion.4
  84.0 1.3 pad_maximum_fusion
  85.3 23.9 %all-to-all-start = ((bf16[64,96,128]{2,1,0:T(8,128)(2,1)}), bf16[64,96,128]{2,1,0:T(8,128)(2,1)S(1)}, u32[]{:S(2)}, u32[]{:S(2)}) async-start(bf16[64,96,128]{2,1,0:T(8,128)(2,1)} %pad_maximum_fusion), calls=%async_computation | async-start | bytes 3145728 | tf_op jit(solution)/shard_map/all_to_all | solution.py:89
  109.2 2.3 %slice.83 = bf16[4,1024,128]{2,1,0:T(8,128)(2,1)} slice(bf16[4,1040,128]{2,1,0:T(8,128)(2,1)} %copy-done.2), slice={[0:4], [0:1024], [0:128]} | slice | bytes 2097152 | tf_op jit(solution)/shard_map/slice | solution.py:69
  111.5 0.7 fusion.28
  112.3 36.3 %all-to-all-done = bf16[64,96,128]{2,1,0:T(8,128)(2,1)S(1)} async-done(((bf16[64,96,128]{2,1,0:T(8,128)(2,1)}), bf16[64,96,128]{2,1,0:T(8,128)(2,1)S(1)}, u32[]{:S(2)}, u32[]{:S(2)}) %all-to-all-start) | async-done | bytes 1572896 | tf_op jit(solution)/shard_map/all_to_all | solution.py:89
  148.6 1.1 slice.88
  149.7 2.3 %collective-permute-start.6 = (bf16[64,64,128]{2,1,0:T(8,128)(2,1)}, bf16[64,64,128]{2,1,0:T(8,128)(2,1)}, u32[]{:S(2)}, u32[]{:S(2)}) collective-permute-start(bf16[64,64,128]{2,1,0:T(8,128)(2,1)} %slice.88), channel_id=1, source_target_pairs={{0,1},{1,0},{2,3},{3,2},{4,5},{5,4},{6,7},{7,6},{8,9},{9,8},{10,11... | collective-permute-start | bytes 3145736 | tf_op jit(solution)/shard_map/ppermute | solution.py:12
  152.1 2.7 %gather_fusion = bf16[32,64,128]{2,1,0:T(8,128)(2,1)} fusion(bf16[64,64,128]{2,1,0:T(8,128)(2,1)} %slice.88, s32[1024]{0:T(1024)S(1)} %pad_clamp_fusion), kind=kCustom, calls=%fused_computation.clone | custom fusion | bytes 1048704 | tf_op jit(solution)/shard_map/jit(_take)/gather | solution.py:97
  155.0 0.7 reduce_sum.9
  155.6 1.9 %gather_fusion.1 = bf16[32,64,128]{2,1,0:T(8,128)(2,1)S(1)} fusion(bf16[64,64,128]{2,1,0:T(8,128)(2,1)} %collective-permute-done.6, s32[1024]{0:T(1024)S(1)} %pad_clamp_fusion), kind=kCustom, calls=%fused_computation.1.clone | custom fusion | bytes 1048704 | tf_op jit(solution)/shard_map/jit(_take)/gather | solution.py:98
  157.7 1.0 copy-done.4
  158.7 1.0 fusion.5
  (42 shorter events, 2.4 us)
Async XLA Ops:
  0.6 1.4 copy-start
  3.1 1.2 copy-start.7
  5.0 22.6 %collective-permute-start.2 = (bf16[512,512]{1,0:T(8,128)(2,1)S(1)}, bf16[512,512]{1,0:T(8,128)(2,1)S(1)}, u32[]{:S(2)}, u32[]{:S(2)}) collective-permute-start(bf16[512,512]{1,0:T(8,128)(2,1)S(1)} %convolution_convert_fusion.2), channel_id=1, source_target_pairs={{0,64},{64,0},{128,192},{192,128},{256,320},{320,256},{384,448},{4... | collective-permute-start | bytes 1572872 | tf_op jit(solution)/shard_map/ppermute | solution.py:12
  13.3 2.7 %copy-start.8 = (s32[8]{0:T(128)S(1)}, s32[8]{0:T(128)}, u32[]{:S(2)}) copy-start(s32[8]{0:T(128)} %param.17) | copy-start | bytes 100
  13.3 2.8 %copy-start.5 = (bf16[8,128,128]{2,1,0:T(8,128)(2,1)S(1)}, bf16[8,128,128]{2,1,0:T(8,128)(2,1)}, u32[]{:S(2)}) copy-start(bf16[8,128,128]{2,1,0:T(8,128)(2,1)} %param.16) | copy-start | bytes 786436
  14.1 33.2 %collective-permute-start.1 = (bf16[512,512]{1,0:T(8,128)(2,1)S(1)}, bf16[512,512]{1,0:T(8,128)(2,1)S(1)}, u32[]{:S(2)}, u32[]{:S(2)}) collective-permute-start(bf16[512,512]{1,0:T(8,128)(2,1)S(1)} %convolution_convert_fusion.3), channel_id=1, source_target_pairs={{0,64},{64,0},{128,192},{192,128},{256,320},{320,256},{384,448},{4... | collective-permute-start | bytes 1572872 | tf_op jit(solution)/shard_map/ppermute | solution.py:12
  16.1 31.5 %copy-start.6 = (bf16[2,128,128]{2,1,0:T(8,128)(2,1)S(1)}, bf16[2,128,128]{2,1,0:T(8,128)(2,1)}, u32[]{:S(2)}) copy-start(bf16[2,128,128]{2,1,0:T(8,128)(2,1)} %param.14) | copy-start | bytes 196612
  16.1 31.4 %collective-permute-start = (bf16[1,1040,128]{2,1,0:T(8,128)(2,1)S(1)}, bf16[1,1040,128]{2,1,0:T(8,128)(2,1)S(1)}, u32[]{:S(2)}, u32[]{:S(2)}) collective-permute-start(bf16[1,1040,128]{2,1,0:T(8,128)(2,1)S(1)} %fusion.18), channel_id=1, source_target_pairs={{0,128},{64,192},{128,0},{192,64},{256,384},{320,448},{384,256},{4... | collective-permute-start | bytes 798728 | tf_op jit(solution)/shard_map/ppermute | solution.py:12
  48.0 16.0 %collective-permute-start.4 = (bf16[1024,512]{1,0:T(8,128)(2,1)S(1)}, bf16[1024,512]{1,0:T(8,128)(2,1)}, u32[]{:S(2)}, u32[]{:S(2)}) collective-permute-start(bf16[1024,512]{1,0:T(8,128)(2,1)S(1)} %bitcast.80), channel_id=1, source_target_pairs={{0,128},{64,192},{128,0},{192,64},{256,384},{320,448},{384,256},{4... | collective-permute-start | bytes 3145736 | tf_op jit(solution)/shard_map/ppermute | solution.py:12
  51.8 14.1 %copy-start.1 = (bf16[1024,512]{1,0:T(8,128)(2,1)S(1)}, bf16[1024,512]{1,0:T(8,128)(2,1)}, u32[]{:S(2)}) copy-start(bf16[1024,512]{1,0:T(8,128)(2,1)} %param.15) | copy-start | bytes 3145732
  51.8 29.5 %collective-permute-start.3 = (bf16[2,1040,128]{2,1,0:T(8,128)(2,1)S(1)}, bf16[2,1040,128]{2,1,0:T(8,128)(2,1)S(1)}, u32[]{:S(2)}, u32[]{:S(2)}) collective-permute-start(bf16[2,1040,128]{2,1,0:T(8,128)(2,1)S(1)} %pad_maximum_fusion.2), channel_id=1, source_target_pairs={{0,64},{64,0},{128,192},{192,128},{256,320},{320,256},{384,448},{4... | collective-permute-start | bytes 1597448 | tf_op jit(solution)/shard_map/ppermute | solution.py:12
  66.4 16.3 %collective-permute-start.5 = (f32[512,256]{0,1:T(8,128)S(1)}, f32[512,256]{0,1:T(8,128)S(1)}, u32[]{:S(2)}, u32[]{:S(2)}) collective-permute-start(f32[512,256]{0,1:T(8,128)S(1)} %convolution_bitcast_fusion), channel_id=1, source_target_pairs={{0,1},{1,0},{2,3},{3,2},{4,5},{5,4},{6,7},{7,6},{8,9},{9,8},{10,11... | collective-permute-start | bytes 1572872 | tf_op jit(solution)/shard_map/ppermute | solution.py:12
  81.4 1.9 %copy-start.2 = (bf16[4,1040,128]{2,1,0:T(8,128)(2,1)}, bf16[4,1040,128]{2,1,0:T(8,128)(2,1)S(1)}, u32[]{:S(2)}) copy-start(bf16[4,1040,128]{2,1,0:T(8,128)(2,1)S(1)} %constant_dynamic-update-slice_fusion) | copy-start | bytes 3194884
  85.3 63.3 %all-to-all-start = ((bf16[64,96,128]{2,1,0:T(8,128)(2,1)}), bf16[64,96,128]{2,1,0:T(8,128)(2,1)S(1)}, u32[]{:S(2)}, u32[]{:S(2)}) async-start(bf16[64,96,128]{2,1,0:T(8,128)(2,1)} %pad_maximum_fusion), calls=%async_computation | async-start | bytes 3145728 | tf_op jit(solution)/shard_map/all_to_all | solution.py:89
  149.7 5.9 %collective-permute-start.6 = (bf16[64,64,128]{2,1,0:T(8,128)(2,1)}, bf16[64,64,128]{2,1,0:T(8,128)(2,1)}, u32[]{:S(2)}, u32[]{:S(2)}) collective-permute-start(bf16[64,64,128]{2,1,0:T(8,128)(2,1)} %slice.88), channel_id=1, source_target_pairs={{0,1},{1,0},{2,3},{3,2},{4,5},{5,4},{6,7},{7,6},{8,9},{9,8},{10,11... | collective-permute-start | bytes 3145736 | tf_op jit(solution)/shard_map/ppermute | solution.py:12
  154.9 2.6 %copy-start.3 = (bf16[32,64,128]{2,1,0:T(8,128)(2,1)S(1)}, bf16[32,64,128]{2,1,0:T(8,128)(2,1)}, u32[]{:S(2)}) copy-start(bf16[32,64,128]{2,1,0:T(8,128)(2,1)} %gather_fusion) | copy-start | bytes 1572868
  157.5 1.2 copy-start.4

commit v16 on v14

--- a/solution.py
+++ b/solution.py
@@ -40,13 +40,12 @@
     carried = packed[None]
     for level in range(levels):
         sibling = from_partner(panel, "group", 2**level)
-        partner = levels - 1 - level
-        carried, panel = lax.optimization_barrier((carried, panel))
-        arrived = from_partner(carried, "group", 2**partner)
         total = (panel.astype(jnp.float32) + sibling.astype(jnp.float32)).astype(jnp.bfloat16)
-        if level < levels - 1:
+        if level == 0:
+            carried, panel = lax.optimization_barrier((carried, panel))
+            arrived = from_partner(carried, "group", 2**level)
             arrived, total = lax.optimization_barrier((arrived, total))
-        carried = jnp.concatenate([carried, arrived], axis=0)
+            carried = jnp.concatenate([carried, arrived], axis=0)
         mapped = jnp.einsum(
             "ab,rbm->ram",
             level_maps[level],
@@ -58,8 +57,6 @@
     half_rows = block_size // 2
     column = (group_index % merged) * quarter
     head = lax.dynamic_slice_in_dim(panel[:block_size], column, quarter, 1)
-    vals_all = carried[:, : n_parent * block_size].reshape(-1, block_size, block_size)
-    rows_all = carried[:, n_parent * block_size, :n_parent].reshape(-1).astype(jnp.int32)
 
     half = width // 2
     keep_cols = lax.dynamic_slice_in_dim(panel, core * half, half, 1)
@@ -76,6 +73,9 @@
     lows = [t - h for t, h in zip(col_tiles, highs)]
     split = jnp.concatenate([h.astype(jnp.bfloat16) for h in highs] + [l.astype(jnp.bfloat16) for l in lows], axis=1)
     carried, head, split = lax.optimization_barrier((carried, head, split))
+    carried = jnp.concatenate([carried, from_partner(carried, "group", 2 ** (levels - 1))], axis=0)
+    vals_all = carried[:, : n_parent * block_size].reshape(-1, block_size, block_size)
+    rows_all = carried[:, n_parent * block_size, :n_parent].reshape(-1).astype(jnp.int32)
     outgoing = jnp.tile(head.reshape(2, half_rows, quarter), (n_sub // 2, 1, 1))
     outgoing = jnp.concatenate([outgoing, split.reshape(n_sub, -1, quarter)], axis=1)
     arrived = lax.all_to_all(outgoing, "sub", 0, 0, tiled=True)

time: 161 us -> 174 us (1.081)
  waiting for transfers between devices: 73 us -> 87.2 us
  starting transfers between devices: 63.8 us -> 59 us
    ppermute x6, waiting for transfers between devices: 36.7 us -> 65.6 us  [from_partner(): return lax.ppermute(value, axis, pairs)]
    all_to_all x1, waiting for transfers between devices: 36.3 us -> 21.7 us  [on_device(): arrived = lax.all_to_all(outgoing, 'sub', 0, 0, tiled=True)]
    ppermute x6, starting transfers between devices: 40 us -> 35.3 us  [from_partner(): return lax.ppermute(value, axis, pairs)]
    concatenate x1, other arithmetic: 0.05 us -> 1.8 us  [on_device(): carried = jnp.concatenate([carried, arrived], axis=0)]
  transfers between devices with their start and end apart: 7 -> 7, of which waited for: 4 -> 5; matrix products, arithmetic and copies ran while one was open for 6% -> 5% of each run, Pallas kernels for 0% -> 0%
where the time goes in v16:
time: 174 us; the launch traced here: 172 us
  waiting for transfers between devices  87.2 us (50%)
  starting transfers between devices  59 us (34%)
  local copies, waits for them, and re-layouts  12.5 us (7%)
  matrix products  6.44 us (4%)
  other arithmetic  6.15 us (4%)
    ppermute x6, waiting for transfers between devices, from_partner(): return lax.ppermute(value, axis, pairs)  65.6 us
    ppermute x6, starting transfers between devices, from_partner(): return lax.ppermute(value, axis, pairs)  35.3 us
    all_to_all x1, starting transfers between devices, on_device(): arrived = lax.all_to_all(outgoing, 'sub', 0, 0, tiled=True)  23.6 us
    all_to_all x1, waiting for transfers between devices, on_device(): arrived = lax.all_to_all(outgoing, 'sub', 0, 0, tiled=True)  21.7 us
  transfers between devices with their start and end apart: 7, of which 5 were waited for; matrix products, arithmetic and copies ran while one was open for 5% of the time, Pallas kernels for 0%

profile of v16, /device:TPU:1, one launch (start us, length us, event | category | flops | bytes accessed | tf_op | source)
XLA Modules:
  0.0 172.3 jit_solution(4817503971302046616)
XLA Ops:
  0.6 0.8 eq.22
  1.5 0.6 copy-done
  2.1 1.0 fusion.5
  3.3 1.2 fusion.8
  4.5 8.4 %collective-permute-start.1 = (bf16[1024,512]{1,0:T(8,128)(2,1)S(1)}, bf16[1024,512]{1,0:T(8,128)(2,1)S(1)}, u32[]{:S(2)}, u32[]{:S(2)}) collective-permute-start(bf16[1024,512]{1,0:T(8,128)(2,1)S(1)} %fusion.8), channel_id=1, source_target_pairs={{0,64},{64,0},{128,192},{192,128},{256,320},{320,256},{384,448},{4... | collective-permute-start | bytes 3145736 | tf_op jit(solution)/shard_map/ppermute | solution.py:12
  13.0 1.9 %collective-permute-start = (bf16[1,1040,128]{2,1,0:T(8,128)(2,1)S(1)}, bf16[1,1040,128]{2,1,0:T(8,128)(2,1)S(1)}, u32[]{:S(2)}, u32[]{:S(2)}) collective-permute-start(bf16[1,1040,128]{2,1,0:T(8,128)(2,1)S(1)} %fusion.21), channel_id=1, source_target_pairs={{0,64},{64,0},{128,192},{192,128},{256,320},{320,256},{384,448},{4... | collective-permute-start | bytes 798728 | tf_op jit(solution)/shard_map/ppermute | solution.py:12
  15.0 32.0 %collective-permute-done.1 = bf16[1024,512]{1,0:T(8,128)(2,1)S(1)} collective-permute-done((bf16[1024,512]{1,0:T(8,128)(2,1)S(1)}, bf16[1024,512]{1,0:T(8,128)(2,1)S(1)}, u32[]{:S(2)}, u32[]{:S(2)}) %collective-permute-start.1) | collective-permute-done | bytes 1048608 | tf_op jit(solution)/shard_map/ppermute | solution.py:12
  47.2 10.1 %collective-permute-done = bf16[1,1040,128]{2,1,0:T(8,128)(2,1)S(1)} collective-permute-done((bf16[1,1040,128]{2,1,0:T(8,128)(2,1)S(1)}, bf16[1,1040,128]{2,1,0:T(8,128)(2,1)S(1)}, u32[]{:S(2)}, u32[]{:S(2)}) %collective-permute-start) | collective-permute-done | bytes 266272 | tf_op jit(solution)/shard_map/ppermute | solution.py:12
  57.4 0.4 convolution_convert_fusion.1
  58.1 3.5 %collective-permute-start.2 = (bf16[1024,512]{1,0:T(8,128)(2,1)S(1)}, bf16[1024,512]{1,0:T(8,128)(2,1)}, u32[]{:S(2)}, u32[]{:S(2)}) collective-permute-start(bf16[1024,512]{1,0:T(8,128)(2,1)S(1)} %bitcast.76), channel_id=1, source_target_pairs={{0,128},{64,192},{128,0},{192,64},{256,384},{320,448},{384,256},{4... | collective-permute-start | bytes 3145736 | tf_op jit(solution)/shard_map/ppermute | solution.py:12
  61.7 12.2 %collective-permute-done.2 = bf16[1024,512]{1,0:T(8,128)(2,1)} collective-permute-done((bf16[1024,512]{1,0:T(8,128)(2,1)S(1)}, bf16[1024,512]{1,0:T(8,128)(2,1)}, u32[]{:S(2)}, u32[]{:S(2)}) %collective-permute-start.2) | collective-permute-done | bytes 1048608 | tf_op jit(solution)/shard_map/ppermute | solution.py:12
  73.9 1.5 add_convert_fusion
  75.4 0.4 convolution_convert_fusion
  75.9 0.5 convolution_bitcast_fusion
  76.3 16.0 %collective-permute-start.3 = (f32[512,256]{0,1:T(8,128)S(1)}, f32[512,256]{0,1:T(8,128)}, u32[]{:S(2)}, u32[]{:S(2)}) collective-permute-start(f32[512,256]{0,1:T(8,128)S(1)} %convolution_bitcast_fusion), channel_id=1, source_target_pairs={{0,1},{1,0},{2,3},{3,2},{4,5},{5,4},{6,7},{7,6},{8,9},{9,8},{10,11... | collective-permute-start | bytes 1572872 | tf_op jit(solution)/shard_map/ppermute | solution.py:12
  92.4 1.8 %pad_maximum_fusion.1 = bf16[2,1040,128]{2,1,0:T(8,128)(2,1)} fusion(bf16[1,1040,128]{2,1,0:T(8,128)(2,1)} %copy-done.4, bf16[1,1040,128]{2,1,0:T(8,128)(2,1)S(1)} %fusion.21), kind=kLoop, calls=%fused_computation.23 | loop fusion | flops 266240 | bytes 1064960 | tf_op jit(solution)/shard_map/concatenate | solution.py:48
  94.3 1.8 %fusion.11 = f32[512,256]{0,1:T(8,128)S(1)} fusion(f32[512,256]{0,1:T(8,128)} %collective-permute-done.3, bf16[1024,512]{1,0:T(8,128)(2,1)} %param.15, bf16[1024,512]{1,0:T(8,128)(2,1)S(1)} %bitcast.75, s32[]{:T(128)S(6)} %select_n.42), kind=kOutput, calls=%fused_computation.16 | convolution fusion | flops 268566528 | bytes 2621444 | tf_op jit(solution)/shard_map/dot_general | solution.py:65
  96.8 1.3 pad_maximum_fusion
  98.1 23.6 %all-to-all-start = ((bf16[64,96,128]{2,1,0:T(8,128)(2,1)}), bf16[64,96,128]{2,1,0:T(8,128)(2,1)S(1)}, u32[]{:S(2)}, u32[]{:S(2)}) async-start(bf16[64,96,128]{2,1,0:T(8,128)(2,1)} %pad_maximum_fusion), calls=%async_computation | async-start | bytes 3145728 | tf_op jit(solution)/shard_map/all_to_all | solution.py:81
  121.7 3.1 %collective-permute-start.4 = (bf16[2,1040,128]{2,1,0:T(8,128)(2,1)}, bf16[2,1040,128]{2,1,0:T(8,128)(2,1)}, u32[]{:S(2)}, u32[]{:S(2)}) collective-permute-start(bf16[2,1040,128]{2,1,0:T(8,128)(2,1)} %pad_maximum_fusion.1), channel_id=1, source_target_pairs={{0,128},{64,192},{128,0},{192,64},{256,384},{320,448},{384,256},{4... | collective-permute-start | bytes 1597448 | tf_op jit(solution)/shard_map/ppermute | solution.py:12
  124.9 1.1 constant_dynamic-update-slice_fusion.1
  126.0 11.2 %collective-permute-done.4 = bf16[2,1040,128]{2,1,0:T(8,128)(2,1)} collective-permute-done((bf16[2,1040,128]{2,1,0:T(8,128)(2,1)}, bf16[2,1040,128]{2,1,0:T(8,128)(2,1)}, u32[]{:S(2)}, u32[]{:S(2)}) %collective-permute-start.4) | collective-permute-done | bytes 532512 | tf_op jit(solution)/shard_map/ppermute | solution.py:12
  137.2 1.1 constant_dynamic-update-slice_fusion
  138.3 1.0 slice.68
  139.4 21.7 %all-to-all-done = bf16[64,96,128]{2,1,0:T(8,128)(2,1)S(1)} async-done(((bf16[64,96,128]{2,1,0:T(8,128)(2,1)}), bf16[64,96,128]{2,1,0:T(8,128)(2,1)S(1)}, u32[]{:S(2)}, u32[]{:S(2)}) %all-to-all-start) | async-done | bytes 1572896 | tf_op jit(solution)/shard_map/all_to_all | solution.py:81
  161.1 1.1 slice.70
  162.2 2.3 %collective-permute-start.5 = (bf16[64,64,128]{2,1,0:T(8,128)(2,1)}, bf16[64,64,128]{2,1,0:T(8,128)(2,1)}, u32[]{:S(2)}, u32[]{:S(2)}) collective-permute-start(bf16[64,64,128]{2,1,0:T(8,128)(2,1)} %slice.70), channel_id=1, source_target_pairs={{0,1},{1,0},{2,3},{3,2},{4,5},{5,4},{6,7},{7,6},{8,9},{9,8},{10,11... | collective-permute-start | bytes 3145736 | tf_op jit(solution)/shard_map/ppermute | solution.py:12
  164.6 2.7 %gather_fusion = bf16[32,64,128]{2,1,0:T(8,128)(2,1)} fusion(bf16[64,64,128]{2,1,0:T(8,128)(2,1)} %slice.70, s32[1024]{0:T(1024)S(1)} %pad_clamp_fusion), kind=kCustom, calls=%fused_computation.clone | custom fusion | bytes 1048704 | tf_op jit(solution)/shard_map/jit(_take)/gather | solution.py:89
  167.5 0.7 reduce_sum.9
  168.2 1.9 %gather_fusion.1 = bf16[32,64,128]{2,1,0:T(8,128)(2,1)S(1)} fusion(bf16[64,64,128]{2,1,0:T(8,128)(2,1)} %collective-permute-done.5, s32[1024]{0:T(1024)S(1)} %pad_clamp_fusion), kind=kCustom, calls=%fused_computation.1.clone | custom fusion | bytes 1048704 | tf_op jit(solution)/shard_map/jit(_take)/gather | solution.py:90
  170.2 1.0 copy-done.3
  171.3 1.0 fusion.12
  (37 shorter events, 2.1 us)
Async XLA Ops:
  0.6 1.4 copy-start
  2.1 1.2 copy-start.7
  3.3 9.7 %copy-start.8 = (s32[8]{0:T(128)S(1)}, s32[8]{0:T(128)}, u32[]{:S(2)}) copy-start(s32[8]{0:T(128)} %param.17) | copy-start | bytes 100
  3.3 9.7 %copy-start.5 = (bf16[8,128,128]{2,1,0:T(8,128)(2,1)S(1)}, bf16[8,128,128]{2,1,0:T(8,128)(2,1)}, u32[]{:S(2)}) copy-start(bf16[8,128,128]{2,1,0:T(8,128)(2,1)} %param.16) | copy-start | bytes 786436
  4.5 52.9 %copy-start.6 = (bf16[2,128,128]{2,1,0:T(8,128)(2,1)S(1)}, bf16[2,128,128]{2,1,0:T(8,128)(2,1)}, u32[]{:S(2)}) copy-start(bf16[2,128,128]{2,1,0:T(8,128)(2,1)} %param.14) | copy-start | bytes 196612
  4.5 42.4 %collective-permute-start.1 = (bf16[1024,512]{1,0:T(8,128)(2,1)S(1)}, bf16[1024,512]{1,0:T(8,128)(2,1)S(1)}, u32[]{:S(2)}, u32[]{:S(2)}) collective-permute-start(bf16[1024,512]{1,0:T(8,128)(2,1)S(1)} %fusion.8), channel_id=1, source_target_pairs={{0,64},{64,0},{128,192},{192,128},{256,320},{320,256},{384,448},{4... | collective-permute-start | bytes 3145736 | tf_op jit(solution)/shard_map/ppermute | solution.py:12
  13.0 44.4 %collective-permute-start = (bf16[1,1040,128]{2,1,0:T(8,128)(2,1)S(1)}, bf16[1,1040,128]{2,1,0:T(8,128)(2,1)S(1)}, u32[]{:S(2)}, u32[]{:S(2)}) collective-permute-start(bf16[1,1040,128]{2,1,0:T(8,128)(2,1)S(1)} %fusion.21), channel_id=1, source_target_pairs={{0,64},{64,0},{128,192},{192,128},{256,320},{320,256},{384,448},{4... | collective-permute-start | bytes 798728 | tf_op jit(solution)/shard_map/ppermute | solution.py:12
  57.4 0.7 copy-start.4
  58.1 15.8 %collective-permute-start.2 = (bf16[1024,512]{1,0:T(8,128)(2,1)S(1)}, bf16[1024,512]{1,0:T(8,128)(2,1)}, u32[]{:S(2)}, u32[]{:S(2)}) collective-permute-start(bf16[1024,512]{1,0:T(8,128)(2,1)S(1)} %bitcast.76), channel_id=1, source_target_pairs={{0,128},{64,192},{128,0},{192,64},{256,384},{320,448},{384,256},{4... | collective-permute-start | bytes 3145736 | tf_op jit(solution)/shard_map/ppermute | solution.py:12
  61.6 14.2 %copy-start.1 = (bf16[1024,512]{1,0:T(8,128)(2,1)S(1)}, bf16[1024,512]{1,0:T(8,128)(2,1)}, u32[]{:S(2)}) copy-start(bf16[1024,512]{1,0:T(8,128)(2,1)} %param.15) | copy-start | bytes 3145732
  76.3 17.9 %collective-permute-start.3 = (f32[512,256]{0,1:T(8,128)S(1)}, f32[512,256]{0,1:T(8,128)}, u32[]{:S(2)}, u32[]{:S(2)}) collective-permute-start(f32[512,256]{0,1:T(8,128)S(1)} %convolution_bitcast_fusion), channel_id=1, source_target_pairs={{0,1},{1,0},{2,3},{3,2},{4,5},{5,4},{6,7},{7,6},{8,9},{9,8},{10,11... | collective-permute-start | bytes 1572872 | tf_op jit(solution)/shard_map/ppermute | solution.py:12
  98.1 63.0 %all-to-all-start = ((bf16[64,96,128]{2,1,0:T(8,128)(2,1)}), bf16[64,96,128]{2,1,0:T(8,128)(2,1)S(1)}, u32[]{:S(2)}, u32[]{:S(2)}) async-start(bf16[64,96,128]{2,1,0:T(8,128)(2,1)} %pad_maximum_fusion), calls=%async_computation | async-start | bytes 3145728 | tf_op jit(solution)/shard_map/all_to_all | solution.py:81
  121.7 15.4 %collective-permute-start.4 = (bf16[2,1040,128]{2,1,0:T(8,128)(2,1)}, bf16[2,1040,128]{2,1,0:T(8,128)(2,1)}, u32[]{:S(2)}, u32[]{:S(2)}) collective-permute-start(bf16[2,1040,128]{2,1,0:T(8,128)(2,1)} %pad_maximum_fusion.1), channel_id=1, source_target_pairs={{0,128},{64,192},{128,0},{192,64},{256,384},{320,448},{384,256},{4... | collective-permute-start | bytes 1597448 | tf_op jit(solution)/shard_map/ppermute | solution.py:12
  162.2 5.9 %collective-permute-start.5 = (bf16[64,64,128]{2,1,0:T(8,128)(2,1)}, bf16[64,64,128]{2,1,0:T(8,128)(2,1)}, u32[]{:S(2)}, u32[]{:S(2)}) collective-permute-start(bf16[64,64,128]{2,1,0:T(8,128)(2,1)} %slice.70), channel_id=1, source_target_pairs={{0,1},{1,0},{2,3},{3,2},{4,5},{5,4},{6,7},{7,6},{8,9},{9,8},{10,11... | collective-permute-start | bytes 3145736 | tf_op jit(solution)/shard_map/ppermute | solution.py:12
  167.4 2.6 %copy-start.2 = (bf16[32,64,128]{2,1,0:T(8,128)(2,1)S(1)}, bf16[32,64,128]{2,1,0:T(8,128)(2,1)}, u32[]{:S(2)}) copy-start(bf16[32,64,128]{2,1,0:T(8,128)(2,1)} %gather_fusion) | copy-start | bytes 1572868
  170.1 1.2 copy-start.3
